TPU v7x, 128 devices: a whole 4x4x4 slice. The times are simulated.
128 devices in a mesh: gz: 64 (over x, y_lo, z, core), xy: 2 (over y_hi).
Axes of the slice: x: 4, y: 4 (y_hi: 2, y_lo: 2; y = y_hi * 2 + y_lo), z: 4, core: 2. Of those that a mesh axis runs over, the one named last changes fastest.
Arguments:
- moments: bfloat16 [361, 512, 256], P(None, 'gz', 'xy'), may hold values from -4 to 4
- counts: int32 [512, 256], P('gz', 'xy'), may hold values from 0 to 7
- m2x: bfloat16 [1296, 361], replicated, may hold values from -0.3125 to 0.3125
- x2l: bfloat16 [361, 1296], replicated, may hold values from -0.0625 to 0.0625
- decay_rate: float32 [648], replicated, may hold values from 0.00048828125 to 0.05
- wave_x: float32 [648], replicated, may hold values from -3.140625 to 3.140625
- wave_y: float32 [648], replicated, may hold values from -3.140625 to 3.140625
- offsets: int32 [6, 2], replicated, may hold values from -2 to 2, as said below
Outputs:
- local_out: bfloat16 [361, 512, 256], P(None, 'gz', 'xy')
Inputs may be any that keep to these rules, and one draw needn't show every extreme that they name: `offsets`: some row is (2, -2) and some row is (-2, 2).
All inputs are finite; a program needn't handle non-finite values.
Results may differ from a plain program's by a relative error of at most 0.0064.
Values may be sent and summed in bfloat16 or wider, within the bound.
No kernel may reach another device: no remote copies, remote signals or barrier semaphores. Data moves between devices by JAX's collectives and lax.ppermute only.
A program may use at most 192 MiB of HBM per device.

v0:
```python
import jax
import jax.numpy as jnp
from jax import lax
from jax.sharding import PartitionSpec as P

BY = 8
R = 2
NOFF = 6


def from_behind(value, axis, steps):
    count = lax.axis_size(axis)
    pairs = [(source, (source + steps) % count) for source in range(count)]
    return lax.ppermute(value, axis, pairs)


def with_halo(block, axis, dim, width):
    low = from_behind(lax.slice_in_dim(block, block.shape[dim] - width, None, axis=dim), axis, 1)
    high = from_behind(lax.slice_in_dim(block, 0, width, axis=dim), axis, -1)
    return jnp.concatenate([low, block, high], axis=dim)


def entering_sums(outgoing, rate_rows, layers):
    rows, boxes = outgoing.shape
    count = lax.axis_size("gz")
    me = lax.axis_index("gz")
    band = -(-rows // count)
    padded = band * count
    held = jnp.pad(outgoing, ((0, padded - rows), (0, 0)))
    held = lax.all_to_all(held, "gz", 0, 0, tiled=True).reshape(count, band, boxes)
    rates = jnp.pad(rate_rows, (0, padded - rows), constant_values=1.0)
    my_rates = lax.dynamic_slice_in_dim(rates, me * band, band)
    slab = jnp.arange(count, dtype=jnp.int32)
    gap = (slab[:, None] - 1 - slab[None, :]) % count
    weights = jnp.exp(-my_rates[:, None, None] * (layers * gap.astype(jnp.float32))[None])
    weights = weights / (1.0 - jnp.exp(-my_rates * (layers * count)))[:, None, None]
    sums = jnp.einsum("rst,trb->srb", weights, held, precision=lax.Precision.HIGHEST)
    sums = lax.all_to_all(sums.reshape(padded, boxes), "gz", 0, 0, tiled=True)
    return sums[:rows]


def body(moments, counts, m2x, x2l, decay_rate, wave_x, wave_y, offsets):
    coeffs, layers, plane_size = moments.shape
    exp_rows = m2x.shape[0]
    half_rows = exp_rows // 2
    columns = plane_size // BY
    ext_columns = columns + 2 * R
    ext_boxes = ext_columns * BY
    rate = decay_rate[None, None, :]
    factor = jnp.exp(-rate)
    weight = jnp.sqrt(1.0 - factor * factor)
    multipole = (moments.astype(jnp.float32) * counts.astype(jnp.float32)[None]).astype(
        jnp.bfloat16
    )
    multipole = with_halo(multipole, "xy", 2, R * BY)
    by_box = jnp.transpose(multipole, (0, 2, 1)).reshape(coeffs, ext_boxes * layers)
    expansion = jnp.einsum(
        "pkc,cn->pnk",
        m2x.reshape(2, half_rows, coeffs),
        by_box,
        preferred_element_type=jnp.float32,
    )
    box_terms = (weight * expansion).reshape(2, ext_boxes, layers, half_rows)

    outgoing = box_terms[:, :, layers - 1, :]
    for j in range(layers - 1):
        outgoing = outgoing + jnp.exp(-rate * float(layers - 1 - j)) * box_terms[:, :, j, :]
    before_term = from_behind(box_terms[:, :, layers - 1, :], "gz", 1)

    rows_out = jnp.transpose(outgoing, (0, 2, 1)).reshape(exp_rows, ext_boxes)
    entering = entering_sums(rows_out, jnp.concatenate([decay_rate, decay_rate]), float(layers))
    entering = jnp.transpose(entering.reshape(2, half_rows, ext_boxes), (0, 2, 1))

    layer_pos = jnp.arange(layers, dtype=jnp.float32)[None, None, :, None]
    upward = jnp.exp(-rate[:, :, None, :] * (layer_pos + 1.0)) * entering[:, :, None, :]
    for j in range(layers - 2):
        gap = layer_pos - float(j)
        coeff = jnp.where(gap >= 2.0, jnp.exp(-rate[:, :, None, :] * jnp.maximum(gap, 0.0)), 0.0)
        upward = upward + coeff * box_terms[:, :, j : j + 1, :]
    first = layer_pos == 0.0
    upward = upward - jnp.where(first, factor[:, :, None, :] * before_term[:, :, None, :], 0.0)

    field = upward.astype(jnp.bfloat16).reshape(2, ext_columns, BY, layers, half_rows)
    field = jnp.concatenate([field[:, :, BY - R :], field, field[:, :, :R]], axis=2)
    acc_real = jnp.zeros((columns, BY, layers, half_rows), jnp.float32)
    acc_imag = jnp.zeros((columns, BY, layers, half_rows), jnp.float32)
    for list_entry in range(NOFF):
        step_x = offsets[list_entry, 0]
        step_y = offsets[list_entry, 1]
        moved = lax.dynamic_slice(
            field, (0, R - step_x, R - step_y, 0, 0), (2, columns, BY, layers, half_rows)
        )
        phase_angle = wave_x * step_x.astype(jnp.float32) + wave_y * step_y.astype(jnp.float32)
        cosine = jnp.cos(phase_angle)
        sine_part = jnp.sin(phase_angle)
        part_real = moved[0].astype(jnp.float32)
        part_imag = moved[1].astype(jnp.float32)
        acc_real = acc_real + part_real * cosine - part_imag * sine_part
        acc_imag = acc_imag + part_real * sine_part + part_imag * cosine
    shifted = jnp.stack([acc_real, acc_imag]).astype(jnp.bfloat16)
    shifted = shifted.reshape(2, columns * BY * layers, half_rows)
    local_out = jnp.einsum(
        "cpk,pnk->cn",
        x2l.reshape(coeffs, 2, half_rows),
        shifted,
        preferred_element_type=jnp.float32,
    ).astype(jnp.bfloat16)
    local_out = local_out.reshape(coeffs, plane_size, layers)
    return jnp.transpose(local_out, (0, 2, 1))


def solution(mesh):
    in_specs = (P(None, "gz", "xy"), P("gz", "xy"), P(), P(), P(), P(), P(), P())
    out_specs = P(None, "gz", "xy")
    return jax.shard_map(body, mesh=mesh, in_specs=in_specs, out_specs=out_specs, check_vma=False)
```

profile of v0, /device:TPU:0, one launch (start us, length us, event | category | flops | bytes accessed | tf_op | source)
XLA Modules:
  0.0 186.1 jit_solution(3253721310293365453)
XLA Ops:
  0.0 1.7 copy.52
  1.7 0.7 convert_element_type.163
  2.4 0.2 multiply_convert_fusion
  2.6 3.4 %collective-permute-start = (bf16[361,8,16]{0,2,1:T(8,128)(2,1)S(1)}, bf16[361,8,16]{0,2,1:T(8,128)(2,1)S(1)}, u32[]{:S(2)}, u32[]{:S(2)}) collective-permute-start(bf16[361,8,16]{0,2,1:T(8,128)(2,1)S(1)} %get-tuple-element.17), channel_id=1, source_target_pairs={{0,1},{1,0},{2,3},{3,2},{4,5},{5,4},{6,7},{7,6},{8,9},{9,8},{10,11... | collective-permute-start | bytes 277256 | tf_op jit(solution)/shard_map/ppermute | solution.py:14
  6.0 0.3 collective-permute-start.1
  6.3 2.8 %collective-permute-done = bf16[361,8,16]{0,2,1:T(8,128)(2,1)S(1)} collective-permute-done((bf16[361,8,16]{0,2,1:T(8,128)(2,1)S(1)}, bf16[361,8,16]{0,2,1:T(8,128)(2,1)S(1)}, u32[]{:S(2)}, u32[]{:S(2)}) %collective-permute-start) | collective-permute-done | bytes 92448 | tf_op jit(solution)/shard_map/ppermute | solution.py:14
  9.1 3.0 %collective-permute-done.1 = bf16[361,8,16]{0,2,1:T(8,128)(2,1)S(1)} collective-permute-done((bf16[361,8,16]{0,2,1:T(8,128)(2,1)S(1)}, bf16[361,8,16]{0,2,1:T(8,128)(2,1)S(1)}, u32[]{:S(2)}, u32[]{:S(2)}) %collective-permute-start.1) | collective-permute-done | bytes 92448 | tf_op jit(solution)/shard_map/ppermute | solution.py:14
  12.2 4.8 %multiply_bitcast_fusion = f32[2,1280,648]{1,2,0:T(8,128)} fusion(bf16[2,648,361]{2,1,0:T(8,128)(2,1)S(1)} %bitcast.133, f32[648]{0:T(1024)S(1)} %get-tuple-element.47, bf16[361,160,8]{0,1,2:T(8,128)(2,1)S(1)} %maximum_bitcast_fusion), kind=kOutput, calls=%fused_computation.1 | convolution fusion | flops 1199370240 | bytes 8497984 | tf_op jit(solution)/shard_map/pkc,cn->pnk/dot_general | solution.py:57
  17.0 8.6 %copy.55 = f32[2,1280,648]{2,1,0:T(8,128)} copy(f32[2,1280,648]{1,2,0:T(8,128)} %multiply_bitcast_fusion) | data formatting | bytes 13271040 | tf_op jit(solution)/shard_map/mul | solution.py:63
  25.6 23.9 %fusion.82 = (f32[2,160,1,648]{3,2,1,0:T(1,128)}, f32[2,160,1,648]{3,2,1,0:T(1,128)}, f32[2,160,1,648]{3,2,1,0:T(1,128)}, f32[2,160,1,648]{3,2,1,0:T(1,128)}, f3...) fusion(f32[2,160,8,648]{3,2,1,0:T(8,128)} %bitcast.134), kind=kLoop, calls=%fused_computation.162 | loop fusion | bytes 13271040 | tf_op jit(solution)/shard_map/slice | solution.py:67
  49.5 1.0 copy.107
  50.5 0.7 fusion.85
  73.7 0.5 iota_add_fusion.5
  74.3 0.6 fusion.69
  74.9 0.6 fusion.70
  75.5 0.6 fusion.73
  76.1 0.6 fusion.74
  76.7 4.6 %fusion.35 = (f32[2,648,160]{1,2,0:T(8,128)}, f32[2,20,8,648]{3,2,1,0:T(8,128)}) fusion(f32[2,160,1,648]{3,2,1,0:T(1,128)} %get-tuple-element.7, f32[2,160,1,648]{3,2,1,0:T(1,128)} %get-tuple-element.14, f32[2,160,1,648]{3,2,1,0:T(1,128)} %get-tuple-element.8, f32[2,160,1,648]{3,2,1,0:T(1,128)} %get-tuple-element.9, ...), kind=kLoop, calls=%fused_computation.64 | loop fusion | flops 3110400 | bytes 9141984 | tf_op jit(solution)/shard_map/transpose | solution.py:70
  81.3 2.8 %copy.83 = f32[2,648,160]{2,1,0:T(8,128)} copy(f32[2,648,160]{1,2,0:T(8,128)} %get-tuple-element.38) | data formatting | bytes 1658880
  84.0 1.4 pad.8.clone
  85.5 1.4 all_to_all.12
  86.8 10.1 %all-to-all-start = ((f32[64,21,160]{2,1,0:T(8,128)}), f32[64,21,160]{2,1,0:T(8,128)S(1)}, u32[]{:S(2)}, u32[]{:S(2)}) async-start(f32[64,21,160]{2,1,0:T(8,128)} %all_to_all.12), calls=%async_computation | async-start | bytes 3145728 | tf_op jit(solution)/shard_map/all_to_all | solution.py:30
  96.9 0.5 iota_compare_fusion
  97.5 0.7 exponential_subtract_fusion
  98.1 1.3 fusion.52
  99.5 1.5 multiply_exponential_fusion
  100.9 19.2 %all-to-all-done = f32[64,21,160]{2,1,0:T(8,128)S(1)} async-done(((f32[64,21,160]{2,1,0:T(8,128)}), f32[64,21,160]{2,1,0:T(8,128)S(1)}, u32[]{:S(2)}, u32[]{:S(2)}) %all-to-all-start) | async-done | bytes 860192 | tf_op jit(solution)/shard_map/all_to_all | solution.py:30
  120.2 2.6 %convolution_bitcast_fusion = f32[64,21,160]{2,0,1:T(8,128)S(1)} fusion(f32[64,21,160]{2,1,0:T(8,128)S(1)} %all-to-all-done, f32[21]{0:T(128)} %get-tuple-element.5, f32[64,64]{1,0:T(8,128)} %fusion.52, f32[21]{0:T(128)} %get-tuple-element.6), kind=kOutput, calls=%fused_computation.57 | convolution fusion | flops 165322752 | bytes 1736872 | tf_op jit(solution)/shard_map/rst,trb->srb/dot_general | solution.py:37
  122.8 2.0 %copy.65 = f32[64,21,160]{2,1,0:T(8,128)} copy(f32[64,21,160]{2,0,1:T(8,128)S(1)} %convolution_bitcast_fusion) | data formatting | bytes 1720320 | tf_op jit(solution)/shard_map/rst,trb->srb/transpose | solution.py:37
  124.7 5.8 %all-to-all-start.1 = ((f32[64,21,160]{2,1,0:T(8,128)}), f32[64,21,160]{2,1,0:T(8,128)}, u32[]{:S(2)}, u32[]{:S(2)}) async-start(f32[64,21,160]{2,1,0:T(8,128)} %copy.65), calls=%async_computation.1 | async-start | bytes 3145728 | tf_op jit(solution)/shard_map/all_to_all | solution.py:38
  130.6 0.7 fusion.57
  131.3 1.0 copy.108
  132.3 1.1 copy.109
  133.4 1.4 copy_bitcast_fusion.3
  134.8 1.5 copy_bitcast_fusion.1
  136.3 17.3 %all-to-all-done.1 = f32[64,21,160]{2,1,0:T(8,128)} async-done(((f32[64,21,160]{2,1,0:T(8,128)}), f32[64,21,160]{2,1,0:T(8,128)}, u32[]{:S(2)}, u32[]{:S(2)}) %all-to-all-start.1) | async-done | bytes 860192 | tf_op jit(solution)/shard_map/all_to_all | solution.py:38
  153.7 1.5 all_to_all.15
  155.3 1.2 slice.165
  156.5 1.8 copy.66
  158.3 7.2 %subtract_convert_fusion = bf16[2,20,8,8,648]{4,3,2,1,0:T(8,128)(2,1)S(1)} fusion(f32[2,20,8,648]{3,2,1,0:T(8,128)S(1)} %copy-done.6, f32[2,20,8,648]{3,2,1,0:T(8,128)} %bitcast.141, f32[8,648]{1,0:T(8,128)S(1)} %copy-done.12, f32[2,20,8,648]{3,2,1,0:T(8,128)} %get-tuple-element.61, f32[8,648]{1,0:T(8,128)S(1)} %copy-done.11, ...), kind=kLoop, calls=%fused_computation | loop fusion | flops 26542080 | bytes 10098440 | tf_op jit(solution)/shard_map/convert_element_type | solution.py:83
  165.7 1.4 pad_maximum_fusion
  167.1 5.3 %fusion.11 = bf16[1,16,8,8,648]{4,3,2,1,0:T(8,128)(2,1)} fusion(f32[648]{0:T(1024)S(1)} %get-tuple-element.20, f32[648]{0:T(1024)S(1)} %copy-done.14, f32[648]{0:T(1024)S(1)} %get-tuple-element.21, f32[648]{0:T(1024)S(1)} %copy-done.15, f32[648]{0:T(1024)S(1)} %get-tuple-element.22, f32[648]{0:T(1024)S(1)} %get-tuple-element.26, ...), kind=kLoop, calls=%fused_computation.38 | loop fusion | flops 23887872 | bytes 17283508 | tf_op jit(solution)/shard_map/convert.3
  172.4 4.2 %fusion.23 = bf16[1,16,8,8,648]{4,3,2,1,0:T(8,128)(2,1)S(1)} fusion(f32[648]{0:T(1024)S(1)} %get-tuple-element.20, f32[648]{0:T(1024)S(1)} %copy-done.14, f32[648]{0:T(1024)S(1)} %get-tuple-element.21, f32[648]{0:T(1024)S(1)} %copy-done.15, f32[648]{0:T(1024)S(1)} %get-tuple-element.22, f32[648]{0:T(1024)S(1)} %get-tuple-element.26, ...), kind=kLoop, calls=%fused_computation.50 | loop fusion | flops 23887872 | bytes 17283508 | tf_op jit(solution)/shard_map/convert.2
  176.7 2.5 %copy.67 = bf16[1,1024,648]{1,2,0:T(8,128)(2,1)} copy(bf16[1,1024,648]{2,1,0:T(8,128)(2,1)} %bitcast.136) | data formatting | bytes 2654208 | tf_op jit(solution)/shard_map/stack | solution.py:100
  179.2 1.5 copy.68
  180.8 3.5 %fusion.31 = bf16[361,1024]{1,0:T(8,128)(2,1)S(1)} fusion(bf16[361,2,648]{0,2,1:T(8,128)(2,1)} %bitcast.143, bf16[1,1024,648]{1,2,0:T(8,128)(2,1)} %copy.68, bf16[1,1024,648]{1,2,0:T(8,128)(2,1)} %copy.67), kind=kOutput, calls=%fused_computation.59 | convolution fusion | flops 959865856 | bytes 4329248 | tf_op jit(solution)/shard_map/cpk,pnk->cn/dot_general | solution.py:102
  184.2 0.4 copy.69
  184.6 1.5 copy.70
  (51 shorter events, 0.4 us)
Async XLA Ops:
  0.0 12.2 %copy-start = (bf16[1296,361]{1,0:T(8,128)(2,1)S(1)}, bf16[1296,361]{1,0:T(8,128)(2,1)}, u32[]{:S(2)}) copy-start(bf16[1296,361]{1,0:T(8,128)(2,1)} %param.10) | copy-start | bytes 2807140
  0.0 6.2 %copy-start.17 = (f32[648]{0:T(1024)S(1)}, f32[648]{0:T(1024)}, u32[]{:S(2)}) copy-start(f32[648]{0:T(1024)} %param.12) | copy-start | bytes 7780
  2.6 6.5 %collective-permute-start = (bf16[361,8,16]{0,2,1:T(8,128)(2,1)S(1)}, bf16[361,8,16]{0,2,1:T(8,128)(2,1)S(1)}, u32[]{:S(2)}, u32[]{:S(2)}) collective-permute-start(bf16[361,8,16]{0,2,1:T(8,128)(2,1)S(1)} %get-tuple-element.17), channel_id=1, source_target_pairs={{0,1},{1,0},{2,3},{3,2},{4,5},{5,4},{6,7},{7,6},{8,9},{9,8},{10,11... | collective-permute-start | bytes 277256 | tf_op jit(solution)/shard_map/ppermute | solution.py:14
  6.0 6.1 %collective-permute-start.1 = (bf16[361,8,16]{0,2,1:T(8,128)(2,1)S(1)}, bf16[361,8,16]{0,2,1:T(8,128)(2,1)S(1)}, u32[]{:S(2)}, u32[]{:S(2)}) collective-permute-start(bf16[361,8,16]{0,2,1:T(8,128)(2,1)S(1)} %get-tuple-element.18), channel_id=1, source_target_pairs={{0,1},{1,0},{2,3},{3,2},{4,5},{5,4},{6,7},{7,6},{8,9},{9,8},{10,11... | collective-permute-start | bytes 277256 | tf_op jit(solution)/shard_map/ppermute | solution.py:14
  25.6 24.9 %copy-start.16 = (s32[6,2]{0,1:T(2,128)S(1)}, s32[6,2]{0,1:T(2,128)}, u32[]{:S(2)}) copy-start(s32[6,2]{0,1:T(2,128)} %param.15) | copy-start | bytes 148
  50.5 26.1 %collective-permute-start.2 = (f32[2,160,648]{2,1,0:T(8,128)}, f32[2,160,648]{2,1,0:T(8,128)}, u32[]{:S(2)}, u32[]{:S(2)}) collective-permute-start(f32[2,160,648]{2,1,0:T(8,128)} %bitcast.130), channel_id=1, source_target_pairs={{0,2},{2,4},{4,6},{6,8},{8,10},{10,12},{12,14},{14,16},{16,18},{18... | collective-permute-start | bytes 2488328 | tf_op jit(solution)/shard_map/ppermute | solution.py:14
  85.5 12.0 %copy-start.18 = (f32[648]{0:T(1024)S(1)}, f32[648]{0:T(1024)}, u32[]{:S(2)}) copy-start(f32[648]{0:T(1024)} %param.12) | copy-start | bytes 7780
  86.8 33.3 %all-to-all-start = ((f32[64,21,160]{2,1,0:T(8,128)}), f32[64,21,160]{2,1,0:T(8,128)S(1)}, u32[]{:S(2)}, u32[]{:S(2)}) async-start(f32[64,21,160]{2,1,0:T(8,128)} %all_to_all.12), calls=%async_computation | async-start | bytes 3145728 | tf_op jit(solution)/shard_map/all_to_all | solution.py:30
  122.7 7.8 %copy-start.19 = (f32[648]{0:T(1024)S(1)}, f32[648]{0:T(1024)}, u32[]{:S(2)}) copy-start(f32[648]{0:T(1024)} %param.14) | copy-start | bytes 7780
  122.8 7.8 %copy-start.20 = (f32[648]{0:T(1024)S(1)}, f32[648]{0:T(1024)}, u32[]{:S(2)}) copy-start(f32[648]{0:T(1024)} %param.13) | copy-start | bytes 7780
  124.7 8.7 %copy-start.4 = (f32[2,160,1,648]{3,2,1,0:T(1,128)S(1)}, f32[2,160,1,648]{3,2,1,0:T(1,128)}, u32[]{:S(2)}) copy-start(f32[2,160,1,648]{3,2,1,0:T(1,128)} %get-tuple-element.9) | copy-start | bytes 2488324
  124.7 28.9 %all-to-all-start.1 = ((f32[64,21,160]{2,1,0:T(8,128)}), f32[64,21,160]{2,1,0:T(8,128)}, u32[]{:S(2)}, u32[]{:S(2)}) async-start(f32[64,21,160]{2,1,0:T(8,128)} %copy.65), calls=%async_computation.1 | async-start | bytes 3145728 | tf_op jit(solution)/shard_map/all_to_all | solution.py:38
  130.6 2.8 %copy-start.5 = (f32[2,160,1,648]{3,2,1,0:T(1,128)S(1)}, f32[2,160,1,648]{3,2,1,0:T(1,128)}, u32[]{:S(2)}) copy-start(f32[2,160,1,648]{3,2,1,0:T(1,128)} %get-tuple-element.10) | copy-start | bytes 2488324
  132.3 2.5 %copy-start.2 = (f32[2,160,1,648]{3,2,1,0:T(1,128)S(1)}, f32[2,160,1,648]{3,2,1,0:T(1,128)}, u32[]{:S(2)}) copy-start(f32[2,160,1,648]{3,2,1,0:T(1,128)} %get-tuple-element.8) | copy-start | bytes 2488324
  132.3 2.5 %copy-start.3 = (f32[2,160,1,648]{3,2,1,0:T(1,128)S(1)}, f32[2,160,1,648]{3,2,1,0:T(1,128)}, u32[]{:S(2)}) copy-start(f32[2,160,1,648]{3,2,1,0:T(1,128)} %get-tuple-element.14) | copy-start | bytes 2488324
  155.2 3.0 %copy-start.6 = (f32[2,20,8,648]{3,2,1,0:T(8,128)S(1)}, f32[2,20,8,648]{3,2,1,0:T(8,128)}, u32[]{:S(2)}) copy-start(f32[2,20,8,648]{3,2,1,0:T(8,128)} %get-tuple-element.39) | copy-start | bytes 2488324
  155.2 3.0 %copy-start.7 = (f32[8,648]{1,0:T(8,128)S(1)}, f32[8,648]{1,0:T(8,128)}, u32[]{:S(2)}) copy-start(f32[8,648]{1,0:T(8,128)} %get-tuple-element.31) | copy-start | bytes 62212
  155.2 3.0 %copy-start.8 = (f32[8,648]{1,0:T(8,128)S(1)}, f32[8,648]{1,0:T(8,128)}, u32[]{:S(2)}) copy-start(f32[8,648]{1,0:T(8,128)} %get-tuple-element.32) | copy-start | bytes 62212
  155.2 3.0 %copy-start.9 = (f32[8,648]{1,0:T(8,128)S(1)}, f32[8,648]{1,0:T(8,128)}, u32[]{:S(2)}) copy-start(f32[8,648]{1,0:T(8,128)} %get-tuple-element.33) | copy-start | bytes 62212
  155.2 3.0 %copy-start.10 = (f32[8,648]{1,0:T(8,128)S(1)}, f32[8,648]{1,0:T(8,128)}, u32[]{:S(2)}) copy-start(f32[8,648]{1,0:T(8,128)} %get-tuple-element.34) | copy-start | bytes 62212
  155.2 3.0 %copy-start.11 = (f32[8,648]{1,0:T(8,128)S(1)}, f32[8,648]{1,0:T(8,128)}, u32[]{:S(2)}) copy-start(f32[8,648]{1,0:T(8,128)} %get-tuple-element.35) | copy-start | bytes 62212
  155.2 3.0 %copy-start.12 = (f32[8,648]{1,0:T(8,128)S(1)}, f32[8,648]{1,0:T(8,128)}, u32[]{:S(2)}) copy-start(f32[8,648]{1,0:T(8,128)} %get-tuple-element.36) | copy-start | bytes 62212
  155.3 3.0 %copy-start.13 = (f32[8,648]{1,0:T(8,128)S(1)}, f32[8,648]{1,0:T(8,128)}, u32[]{:S(2)}) copy-start(f32[8,648]{1,0:T(8,128)} %get-tuple-element.37) | copy-start | bytes 62212
  165.7 1.4 copy-start.14
  165.7 1.4 copy-start.15
  180.7 5.4 %copy-start.1 = (bf16[1296,361]{1,0:T(8,128)(2,1)S(1)}, bf16[1296,361]{1,0:T(8,128)(2,1)}, u32[]{:S(2)}) copy-start(bf16[1296,361]{1,0:T(8,128)(2,1)} %param.10) | copy-start | bytes 2807140
where the time goes:
time: 188 us; the launch traced here: 186 us
  local copies, waits for them, and re-layouts  59.2 us (31%)
  waiting for transfers between devices  42.4 us (23%)
  other arithmetic  31.4 us (17%)
  between operations  22.8 us (12%)
  starting transfers between devices  19.5 us (10%)
  matrix products  10.8 us (6%)
    slice x1, local copies, waits for them, and re-layouts, body(): box_terms[:, :, j, :]  23.9 us
    all_to_all x1, waiting for transfers between devices, entering_sums(): lax.all_to_all(held, 'gz', 0, 0, tiled=True).reshape(count, band, boxes)  19.2 us
    all_to_all x1, waiting for transfers between devices, entering_sums(): sums = lax.all_to_all(sums.reshape(padded, boxes), 'gz', 0, 0, tiled=True)  17.3 us
    all_to_all x1, starting transfers between devices, entering_sums(): lax.all_to_all(held, 'gz', 0, 0, tiled=True).reshape(count, band, boxes)  10.1 us
    another operation x2, other arithmetic  9.57 us
    mul x1, local copies, waits for them, and re-layouts, body(): box_terms = (weight * expansion).reshape(2, ext_boxes, layers, half_rows)  8.6 us
    unnamed x47, local copies, waits for them, and re-layouts  7.65 us
    convert_element_type x1, other arithmetic, body(): upward.astype(jnp.bfloat16).reshape(2, ext_columns, BY, layers, half_rows)  7.18 us
  transfers between devices with their start and end apart: 5, of which 4 were waited for; matrix products, arithmetic and copies ran while one was open for 7% of the time, Pallas kernels for 0%

commit v1 on v0

v1 whole, which is shorter than its diff:
```python
import jax
import jax.numpy as jnp
from jax import lax
from jax.sharding import PartitionSpec as P

BY = 8
R = 2
NOFF = 6
TILE_ROWS = 16
TILE = TILE_ROWS * 256


def from_behind(value, axis, steps):
    count = lax.axis_size(axis)
    pairs = [(source, (source + steps) % count) for source in range(count)]
    return lax.ppermute(value, axis, pairs)


def with_halo(block, axis, dim, width):
    low = from_behind(lax.slice_in_dim(block, block.shape[dim] - width, None, axis=dim), axis, 1)
    high = from_behind(lax.slice_in_dim(block, 0, width, axis=dim), axis, -1)
    return jnp.concatenate([low, block, high], axis=dim)


def cyclic_decayed_sum(held, gain_of):
    count = held.shape[0]
    result, offset, span, block, left = None, 0, 1, held, count
    while left:
        if left & 1:
            term = jnp.roll(block, offset, axis=0)
            if offset:
                term = gain_of(offset) * term
            result = term if result is None else result + term
            offset += span
        left >>= 1
        if left:
            block = block + gain_of(span) * jnp.roll(block, span, axis=0)
            span *= 2
    return result


def entering_sums(outgoing, rate_full, layers):
    shape = outgoing.shape
    size = outgoing.size
    count = lax.axis_size("gz")
    me = lax.axis_index("gz")
    chunk = -(-size // (count * TILE)) * TILE
    padded = chunk * count

    def spread(values, fill):
        flat = jnp.pad(values.reshape(-1), (0, padded - size), constant_values=fill)
        return flat.reshape(count, TILE_ROWS, chunk // TILE_ROWS)

    held = lax.all_to_all(spread(outgoing.astype(jnp.bfloat16), 0), "gz", 0, 0, tiled=True)
    held = held.reshape(count, chunk).astype(jnp.float32)
    my_rates = lax.dynamic_index_in_dim(spread(rate_full, 1.0).reshape(count, chunk), me, 0, False)
    sums = cyclic_decayed_sum(held, lambda steps: jnp.exp(-my_rates * (layers * steps)))
    sums = jnp.roll(sums, 1, axis=0) / (1.0 - jnp.exp(-my_rates * (layers * count)))
    sums = sums.astype(jnp.bfloat16).reshape(count, TILE_ROWS, chunk // TILE_ROWS)
    back = lax.all_to_all(sums, "gz", 0, 0, tiled=True)
    return back.reshape(-1)[:size].reshape(shape).astype(jnp.float32)


def body(moments, counts, m2x, x2l, decay_rate, wave_x, wave_y, offsets):
    coeffs, layers, plane_size = moments.shape
    exp_rows = m2x.shape[0]
    half_rows = exp_rows // 2
    columns = plane_size // BY
    ext_columns = columns + 2 * R
    ext_boxes = ext_columns * BY
    rate = decay_rate[None, None, None, :]
    factor = jnp.exp(-rate)
    weight = jnp.sqrt(1.0 - factor * factor)
    multipole = (moments.astype(jnp.float32) * counts.astype(jnp.float32)[None]).astype(
        jnp.bfloat16
    )
    multipole = with_halo(multipole, "xy", 2, R * BY).reshape(coeffs, layers * ext_boxes)
    halves = []
    for part in range(2):
        rows = m2x[part * half_rows : (part + 1) * half_rows]
        expansion = lax.dot_general(
            multipole, rows, (((0,), (1,)), ((), ())), preferred_element_type=jnp.float32
        )
        halves.append(expansion.reshape(layers, ext_boxes, half_rows))
    box_terms = weight * jnp.stack(halves)

    outgoing = box_terms[:, layers - 1]
    for j in range(layers - 1):
        outgoing = outgoing + jnp.exp(-rate[0] * float(layers - 1 - j)) * box_terms[:, j]
    outgoing, box_terms = lax.optimization_barrier((outgoing, box_terms))
    before_term = from_behind(box_terms[:, layers - 1].astype(jnp.bfloat16), "gz", 1)

    rate_full = jnp.broadcast_to(decay_rate, outgoing.shape)
    entering = entering_sums(outgoing, rate_full, float(layers))

    layer_pos = jnp.arange(layers, dtype=jnp.float32)[None, :, None, None]
    upward = jnp.exp(-rate * (layer_pos + 1.0)) * entering[:, None]
    for j in range(layers - 2):
        gap = layer_pos - float(j)
        coeff = jnp.where(gap >= 2.0, jnp.exp(-rate * jnp.maximum(gap, 0.0)), 0.0)
        upward = upward + coeff * box_terms[:, j : j + 1]
    first = layer_pos == 0.0
    upward = upward - jnp.where(first, factor * before_term[:, None].astype(jnp.float32), 0.0)

    field = upward.astype(jnp.bfloat16).reshape(2, layers, ext_columns, BY, half_rows)
    field = jnp.transpose(field, (0, 2, 3, 1, 4))
    field = jnp.concatenate([field[:, :, BY - R :], field, field[:, :, :R]], axis=2)
    acc_real = jnp.zeros((columns, BY, layers, half_rows), jnp.float32)
    acc_imag = jnp.zeros((columns, BY, layers, half_rows), jnp.float32)
    for list_entry in range(NOFF):
        step_x = offsets[list_entry, 0]
        step_y = offsets[list_entry, 1]
        moved = lax.dynamic_slice(
            field, (0, R - step_x, R - step_y, 0, 0), (2, columns, BY, layers, half_rows)
        )
        phase_angle = wave_x * step_x.astype(jnp.float32) + wave_y * step_y.astype(jnp.float32)
        cosine = jnp.cos(phase_angle)
        sine_part = jnp.sin(phase_angle)
        part_real = moved[0].astype(jnp.float32)
        part_imag = moved[1].astype(jnp.float32)
        acc_real = acc_real + part_real * cosine - part_imag * sine_part
        acc_imag = acc_imag + part_real * sine_part + part_imag * cosine
    local_out = None
    for part, acc in enumerate((acc_real, acc_imag)):
        shifted = acc.astype(jnp.bfloat16).reshape(columns * BY * layers, half_rows)
        product = lax.dot_general(
            x2l[:, part * half_rows : (part + 1) * half_rows],
            shifted,
            (((1,), (1,)), ((), ())),
            preferred_element_type=jnp.float32,
        )
        local_out = product if local_out is None else local_out + product
    local_out = local_out.astype(jnp.bfloat16).reshape(coeffs, columns, BY, layers)
    return jnp.transpose(local_out, (0, 3, 1, 2)).reshape(coeffs, layers, plane_size)


def solution(mesh):
    in_specs = (P(None, "gz", "xy"), P("gz", "xy"), P(), P(), P(), P(), P(), P())
    out_specs = P(None, "gz", "xy")
    return jax.shard_map(body, mesh=mesh, in_specs=in_specs, out_specs=out_specs, check_vma=False)
```

time: 188 us -> 115 us (0.61)
  waiting for transfers between devices: 42.4 us -> 6.53 us
  local copies, waits for them, and re-layouts: 59.2 us -> 26.1 us
  matrix products: 10.8 us -> 5.04 us
  starting transfers between devices: 19.5 us -> 23.2 us
  other arithmetic: 31.4 us -> 29.1 us
    all_to_all x2, waiting for transfers between devices: 36.6 us -> 6.52 us  [the longest x1 6.52 us: entering_sums(): back = lax.all_to_all(sums, 'gz', 0, 0, tiled=True)]
    slice x3 -> x11, local copies, waits for them, and re-layouts: 25.8 us -> 4.73 us  [the longest x1 3.6 us: body(): part_real = moved[0].astype(jnp.float32)]
    convert_element_type x1 -> x6, other arithmetic: 7.18 us -> 20.8 us  [the longest x2 11.7 us: body(): shifted = acc.astype(jnp.bfloat16).reshape(columns * BY * layers, half_rows)]
    another operation x2 -> x0, other arithmetic: 9.57 us -> none
    mul x3 -> x1, local copies, waits for them, and re-layouts: 11.5 us -> 4.83 us  [body(): upward = upward + coeff * box_terms[:, j:j + 1]]
    ppermute x3, waiting for transfers between devices: 5.85 us -> 0.01 us  [from_behind(): return lax.ppermute(value, axis, pairs)]
    dot_general x3 -> x4, matrix products: 10.8 us -> 5.04 us  [the longest x2 3.43 us: body(): lax.dot_general(multipole, rows, (((0,), (1,)), ((), ())), preferred_elem...]
    transpose x2 -> x0, other arithmetic: 4.74 us -> none  [the longest x1 4.64 us: body(): rows_out = jnp.transpose(outgoing, (0, 2, 1)).reshape(exp_rows, ext_boxes)]
  transfers between devices with their start and end apart: 5 -> 5, of which waited for: 4 -> 1; matrix products, arithmetic and copies ran while one was open for 7% -> 15% of each run, Pallas kernels for 0% -> 0%
where the time goes in v1:
time: 115 us; the launch traced here: 113 us
  other arithmetic  29.1 us (25%)
  local copies, waits for them, and re-layouts  26.1 us (23%)
  starting transfers between devices  23.2 us (20%)
  between operations  23 us (20%)
  waiting for transfers between devices  6.53 us (6%)
  matrix products  5.04 us (4%)
    convert_element_type x2, other arithmetic, body(): shifted = acc.astype(jnp.bfloat16).reshape(columns * BY * layers, half_rows)  11.7 us
    all_to_all x1, starting transfers between devices, entering_sums(): lax.all_to_all(spread(outgoing.astype(jnp.bfloat16), 0), 'gz', 0, 0, tile...  9.88 us
    all_to_all x1, starting transfers between devices, entering_sums(): back = lax.all_to_all(sums, 'gz', 0, 0, tiled=True)  9.69 us
    convert_element_type x1, other arithmetic, body(): upward.astype(jnp.bfloat16).reshape(2, layers, ext_columns, BY, half_rows)  7.12 us
    unnamed x66, local copies, waits for them, and re-layouts  6.82 us
    all_to_all x1, waiting for transfers between devices, entering_sums(): back = lax.all_to_all(sums, 'gz', 0, 0, tiled=True)  6.52 us
    mul x1, local copies, waits for them, and re-layouts, body(): upward = upward + coeff * box_terms[:, j:j + 1]  4.83 us
    ppermute x3, starting transfers between devices, from_behind(): return lax.ppermute(value, axis, pairs)  3.66 us
  transfers between devices with their start and end apart: 5, of which 1 were waited for; matrix products, arithmetic and copies ran while one was open for 15% of the time, Pallas kernels for 0%

profile of v1, /device:TPU:0, one launch (start us, length us, event | category | flops | bytes accessed | tf_op | source)
XLA Modules:
  0.0 113.0 jit_solution(16150923253596194031)
XLA Ops:
  0.0 1.6 %copy.31 = bf16[361,8,128]{0,2,1:T(8,128)(2,1)S(1)} copy(bf16[361,8,128]{2,1,0:T(8,128)(2,1)} %param.8) | data formatting | bytes 1478656 | tf_op args[0]
  1.6 0.7 convert_element_type.230
  2.3 0.2 multiply_convert_fusion
  2.5 3.4 %collective-permute-start = (bf16[361,8,16]{0,2,1:T(8,128)(2,1)S(1)}, bf16[361,8,16]{0,2,1:T(8,128)(2,1)S(1)}, u32[]{:S(2)}, u32[]{:S(2)}) collective-permute-start(bf16[361,8,16]{0,2,1:T(8,128)(2,1)S(1)} %get-tuple-element.38), channel_id=1, source_target_pairs={{0,1},{1,0},{2,3},{3,2},{4,5},{5,4},{6,7},{7,6},{8,9},{9,8},{10,11... | collective-permute-start | bytes 277256 | tf_op jit(solution)/shard_map/ppermute | solution.py:16
  5.9 0.3 collective-permute-start.1
  6.4 0.9 reshape.609
  7.4 0.2 reshape_reshape.3
  7.6 0.7 fusion.82
  15.6 0.8 subtract_reduce_fusion
  16.4 0.7 fusion.55
  17.1 2.2 %convolution_bitcast_fusion.1 = f32[1,8,160,648]{3,2,1,0:T(8,128)S(1)} fusion(bf16[1296,361]{1,0:T(8,128)(2,1)} %param.10, bf16[361,8,16]{0,2,1:T(8,128)(2,1)S(1)} %collective-permute-done.1, bf16[361,8,128]{0,2,1:T(8,128)(2,1)S(1)} %multiply_convert_fusion, bf16[361,8,16]{0,2,1:T(8,128)(2,1)S(1)} %collective-permute-done), kind=kOutput, calls=%fused_computation.52 | convolution fusion | flops 601628160 | bytes 4739584 | tf_op jit(solution)/shard_map/dot_general | solution.py:81
  19.4 1.2 %convolution_bitcast_fusion = f32[1,8,160,648]{3,2,1,0:T(8,128)S(1)} fusion(bf16[1296,361]{1,0:T(8,128)(2,1)S(1)} %copy-done.7, bf16[361,8,16]{0,2,1:T(8,128)(2,1)S(1)} %collective-permute-done.1, bf16[361,8,128]{0,2,1:T(8,128)(2,1)S(1)} %multiply_convert_fusion, bf16[361,8,16]{0,2,1:T(8,128)(2,1)S(1)} %collective-permute-done), kind=kOutput, calls=%fused_computation.51 | convolution fusion | flops 601628160 | bytes 4798464 | tf_op jit(solution)/shard_map/dot_general | solution.py:81
  20.6 0.8 maximum_multiply_fusion
  21.4 3.0 %copy-done = f32[2,8,160,648]{3,2,1,0:T(8,128)} copy-done((f32[2,8,160,648]{3,2,1,0:T(8,128)}, f32[2,8,160,648]{3,2,1,0:T(8,128)S(1)}, u32[]{:S(2)}) %copy-start) | copy-done | bytes 6635544
  24.4 0.5 fusion.33
  25.0 1.0 reshape.607
  26.1 1.0 reshape.608
  27.0 9.9 %all-to-all-start = ((bf16[64,16,256]{2,1,0:T(8,128)(2,1)}), bf16[64,16,256]{2,1,0:T(8,128)(2,1)S(1)}, u32[]{:S(2)}, u32[]{:S(2)}) async-start(bf16[64,16,256]{2,1,0:T(8,128)(2,1)} %reshape.608), calls=%async_computation | async-start | bytes 1048576 | tf_op jit(solution)/shard_map/all_to_all | solution.py:54
  36.9 0.6 iota_compare_fusion
  52.3 0.7 multiply_exponential_fusion
  53.1 2.1 %fusion.53 = bf16[2,160,648]{2,1,0:T(8,128)(2,1)} fusion(f32[2,8,160,648]{3,2,1,0:T(8,128)} %copy-done), kind=kLoop, calls=%fused_computation.108 | loop fusion | bytes 829440 | tf_op jit(solution)/shard_map/convert_element_type | solution.py:91
  55.2 0.1 convert_element_type.233
  55.3 0.6 copy.53
  56.0 0.1 slice.280
  56.2 0.6 copy.55
  56.8 0.2 fusion.25
  57.0 0.2 fusion.26
  57.2 0.2 fusion.27
  57.5 0.1 fusion.28
  58.1 0.3 copy.56
  58.5 0.9 fusion.31
  59.4 9.7 %all-to-all-start.1 = ((bf16[64,16,256]{2,1,0:T(8,128)(2,1)}), bf16[64,16,256]{2,1,0:T(8,128)(2,1)S(1)}, u32[]{:S(2)}, u32[]{:S(2)}) async-start(bf16[64,16,256]{2,1,0:T(8,128)(2,1)} %fusion.31), calls=%async_computation.1 | async-start | bytes 1048576 | tf_op jit(solution)/shard_map/all_to_all | solution.py:60
  69.1 4.8 %slice_bitcast_fusion.13 = (f32[2,20,8,648]{3,2,1,0:T(8,128)S(1)}, f32[2,20,8,648]{3,2,1,0:T(8,128)S(1)}, f32[2,20,8,648]{3,2,1,0:T(8,128)}, f32[2,20,8,648]{3,2...) fusion(f32[2,8,160,648]{3,2,1,0:T(8,128)} %copy-done), kind=kLoop, calls=%fused_computation.100 | loop fusion | bytes 9953280 | tf_op jit(solution)/shard_map/mul | solution.py:101
  74.0 1.0 multiply_bitcast_fusion
  75.0 6.5 %all-to-all-done.1 = bf16[64,16,256]{2,1,0:T(8,128)(2,1)S(1)} async-done(((bf16[64,16,256]{2,1,0:T(8,128)(2,1)}), bf16[64,16,256]{2,1,0:T(8,128)(2,1)S(1)}, u32[]{:S(2)}, u32[]{:S(2)}) %all-to-all-start.1) | async-done | bytes 524320 | tf_op jit(solution)/shard_map/all_to_all | solution.py:60
  81.5 0.4 copy.57
  81.9 0.9 slice_convert_fusion.1
  82.9 2.2 %reshape.613 = f32[2,20,8,648]{3,2,1,0:T(8,128)S(1)} reshape(f32[207360]{0:T(1024)} %slice_convert_fusion.1) | data formatting | bytes 1658880 | tf_op jit(solution)/shard_map/convert_element_type | solution.py:61
  85.1 7.1 %subtract_convert_fusion = bf16[2,20,8,8,648]{4,3,2,1,0:T(8,128)(2,1)S(1)} fusion(f32[2,20,8,648]{3,2,1,0:T(8,128)} %multiply_bitcast_fusion, f32[2,20,8,648]{3,2,1,0:T(8,128)S(1)} %get-tuple-element.10, f32[8,648]{1,0:T(8,128)} %get-tuple-element.57, f32[2,20,8,648]{3,2,1,0:T(8,128)} %get-tuple-element.11, f32[8,648]{1,0:T(8,128)} %get-tuple-element.56, ...), kind=kLoop, calls=%fused_computation.1 | loop fusion | flops 26542080 | bytes 10098440 | tf_op jit(solution)/shard_map/convert_element_type | solution.py:105
  92.2 0.2 fusion.78
  92.4 1.4 %pad_maximum_fusion = bf16[2,20,12,8,648]{4,3,2,1,0:T(8,128)(2,1)S(1)} fusion(bf16[2,20,2,8,648]{4,3,2,1,0:T(8,128)(2,1)S(1)} %get-tuple-element.28, bf16[2,20,8,8,648]{4,3,2,1,0:T(8,128)(2,1)S(1)} %subtract_convert_fusion, bf16[2,20,2,8,648]{4,3,2,1,0:T(8,128)(2,1)S(1)} %get-tuple-element.27), kind=kLoop, calls=%fused_computation.2 | loop fusion | flops 4976640 | bytes 9953280 | tf_op jit(solution)/shard_map/concatenate | solution.py:107
  93.9 3.6 %constant_dynamic-slice_fusion.5 = (bf16[1,16,8,8,648]{4,3,2,1,0:T(8,128)(2,1)S(1)}, bf16[1,16,8,8,648]{4,3,2,1,0:T(8,128)(2,1)S(1)}, bf16[1,16,8,8,648]{4,3,2,1...) fusion(bf16[2,20,12,8,648]{4,3,2,1,0:T(8,128)(2,1)S(1)} %pad_ma, ...), kind=kLoop, calls=%fused_computation.145 | loop fusion | bytes 31850548 | tf_op jit(solution)/shard_map/slice | solution.py:119
  97.7 6.1 %fusion.23 = bf16[1024,648]{1,0:T(8,128)(2,1)S(1)} fusion(bf16[1,16,8,8,648]{4,3,2,1,0:T(8,128)(2,1)S(1)} %get-tuple-element.21, bf16[1,16,8,8,648]{4,3,2,1,0:T(8,128)(2,1)S(1)} %get-tuple-element.16, bf16[1,16,8,8,648]{4,3,2,1,0:T(8,128)(2,1)} %get-tuple-element.22, bf16[1,16,8,8,648]{4,3,2,1,0:T(8,128)(2,1)S(1)} %get-tuple-element.17, ...), kind=kLoop, calls=%fused_computation.50 | loop fusion | flops 23887872 | bytes 17283456 | tf_op jit(solution)/shard_map/convert_element_type | solution.py:125
  103.8 5.6 %fusion.11 = bf16[1024,648]{1,0:T(8,128)(2,1)S(1)} fusion(bf16[1,16,8,8,648]{4,3,2,1,0:T(8,128)(2,1)S(1)} %get-tuple-element.21, bf16[1,16,8,8,648]{4,3,2,1,0:T(8,128)(2,1)S(1)} %get-tuple-element.16, bf16[1,16,8,8,648]{4,3,2,1,0:T(8,128)(2,1)S(1)} %copy-done.1, bf16[1,16,8,8,648]{4,3,2,1,0:T(8,128)(2,1)S(1)} %get-tuple-element.17, ...), kind=kLoop, calls=%fused_computation.38 | loop fusion | flops 23887872 | bytes 17283456 | tf_op jit(solution)/shard_map/convert_element_type | solution.py:125
  109.5 0.8 fusion.49
  110.3 0.8 fusion.24
  111.1 0.4 copy.40
  111.5 1.5 %copy.42 = bf16[361,8,128]{2,1,0:T(8,128)(2,1)} copy(bf16[361,8,128]{0,1,2:T(8,128)(2,1)S(1)} %bitcast.231) | data formatting | bytes 1478656 | tf_op jit(solution)/shard_map/reshape | solution.py:134
  (90 shorter events, 1.2 us)
Async XLA Ops:
  0.0 6.2 %copy-start.25 = (f32[648]{0:T(1024)S(1)}, f32[648]{0:T(1024)}, u32[]{:S(2)}) copy-start(f32[648]{0:T(1024)} %param.12) | copy-start | bytes 7780
  2.5 14.6 %collective-permute-start = (bf16[361,8,16]{0,2,1:T(8,128)(2,1)S(1)}, bf16[361,8,16]{0,2,1:T(8,128)(2,1)S(1)}, u32[]{:S(2)}, u32[]{:S(2)}) collective-permute-start(bf16[361,8,16]{0,2,1:T(8,128)(2,1)S(1)} %get-tuple-element.38), channel_id=1, source_target_pairs={{0,1},{1,0},{2,3},{3,2},{4,5},{5,4},{6,7},{7,6},{8,9},{9,8},{10,11... | collective-permute-start | bytes 277256 | tf_op jit(solution)/shard_map/ppermute | solution.py:16
  5.9 11.2 %collective-permute-start.1 = (bf16[361,8,16]{0,2,1:T(8,128)(2,1)S(1)}, bf16[361,8,16]{0,2,1:T(8,128)(2,1)S(1)}, u32[]{:S(2)}, u32[]{:S(2)}) collective-permute-start(bf16[361,8,16]{0,2,1:T(8,128)(2,1)S(1)} %get-tuple-element.39), channel_id=1, source_target_pairs={{0,1},{1,0},{2,3},{3,2},{4,5},{5,4},{6,7},{7,6},{8,9},{9,8},{10,11... | collective-permute-start | bytes 277256 | tf_op jit(solution)/shard_map/ppermute | solution.py:16
  6.3 15.1 %copy-start.22 = (f32[648]{0:T(1024)}, f32[648]{0:T(1024)S(1)}, u32[]{:S(2)}) copy-start(f32[648]{0:T(1024)S(1)} %get-tuple-element.60) | copy-start | bytes 7780
  6.3 1.3 %copy-start.24 = (s32[6,2]{0,1:T(2,128)S(1)}, s32[6,2]{0,1:T(2,128)}, u32[]{:S(2)}) copy-start(s32[6,2]{0,1:T(2,128)} %param.15) | copy-start | bytes 148
  6.4 10.0 %copy-start.26 = (f32[648]{0:T(1024)S(1)}, f32[648]{0:T(1024)}, u32[]{:S(2)}) copy-start(f32[648]{0:T(1024)} %param.14) | copy-start | bytes 7780
  6.4 10.0 %copy-start.27 = (f32[648]{0:T(1024)S(1)}, f32[648]{0:T(1024)}, u32[]{:S(2)}) copy-start(f32[648]{0:T(1024)} %param.13) | copy-start | bytes 7780
  7.6 11.8 %copy-start.7 = (bf16[1296,361]{1,0:T(8,128)(2,1)S(1)}, bf16[1296,361]{1,0:T(8,128)(2,1)}, u32[]{:S(2)}) copy-start(bf16[1296,361]{1,0:T(8,128)(2,1)} %param.10) | copy-start | bytes 2807140
  21.4 3.1 %copy-start = (f32[2,8,160,648]{3,2,1,0:T(8,128)}, f32[2,8,160,648]{3,2,1,0:T(8,128)S(1)}, u32[]{:S(2)}) copy-start(f32[2,8,160,648]{3,2,1,0:T(8,128)S(1)} %maximum_multiply_fusion) | copy-start | bytes 19906564
  27.0 28.1 %all-to-all-start = ((bf16[64,16,256]{2,1,0:T(8,128)(2,1)}), bf16[64,16,256]{2,1,0:T(8,128)(2,1)S(1)}, u32[]{:S(2)}, u32[]{:S(2)}) async-start(bf16[64,16,256]{2,1,0:T(8,128)(2,1)} %reshape.608), calls=%async_computation | async-start | bytes 1048576 | tf_op jit(solution)/shard_map/all_to_all | solution.py:54
  55.1 18.8 %collective-permute-start.2 = (bf16[2,160,648]{2,1,0:T(8,128)(2,1)}, bf16[2,160,648]{2,1,0:T(8,128)(2,1)S(1)}, u32[]{:S(2)}, u32[]{:S(2)}) collective-permute-start(bf16[2,160,648]{2,1,0:T(8,128)(2,1)} %fusion.53), channel_id=1, source_target_pairs={{0,2},{2,4},{4,6},{6,8},{8,10},{10,12},{12,14},{14,16},{16,18},{18... | collective-permute-start | bytes 1244168 | tf_op jit(solution)/shard_map/ppermute | solution.py:16
  55.9 0.9 copy-start.9
  56.2 0.8 copy-start.8
  59.4 22.1 %all-to-all-start.1 = ((bf16[64,16,256]{2,1,0:T(8,128)(2,1)}), bf16[64,16,256]{2,1,0:T(8,128)(2,1)S(1)}, u32[]{:S(2)}, u32[]{:S(2)}) async-start(bf16[64,16,256]{2,1,0:T(8,128)(2,1)} %fusion.31), calls=%async_computation.1 | async-start | bytes 1048576 | tf_op jit(solution)/shard_map/all_to_all | solution.py:60
  69.1 4.8 %copy-start.23 = (f32[648]{0:T(1024)S(1)}, f32[648]{0:T(1024)}, u32[]{:S(2)}) copy-start(f32[648]{0:T(1024)} %copy-done.22) | copy-start | bytes 7780
  73.9 11.2 %copy-start.28 = (pred[8]{0:T(512)(128)(4,1)S(1)}, pred[8]{0:T(512)(128)(4,1)}, u32[]{:S(2)}) copy-start(pred[8]{0:T(512)(128)(4,1)} %iota_compare_fusion) | copy-start | bytes 28
  93.8 3.7 %copy-start.10 = (f32[648]{0:T(1024)S(1)}, f32[648]{0:T(1024)}, u32[]{:S(2)}) copy-start(f32[648]{0:T(1024)} %get-tuple-element.40) | copy-start | bytes 7780
  93.8 3.7 %copy-start.11 = (f32[648]{0:T(1024)S(1)}, f32[648]{0:T(1024)}, u32[]{:S(2)}) copy-start(f32[648]{0:T(1024)} %get-tuple-element.41) | copy-start | bytes 7780
  93.8 3.7 %copy-start.12 = (f32[648]{0:T(1024)S(1)}, f32[648]{0:T(1024)}, u32[]{:S(2)}) copy-start(f32[648]{0:T(1024)} %get-tuple-element.42) | copy-start | bytes 7780
  93.8 3.7 %copy-start.13 = (f32[648]{0:T(1024)S(1)}, f32[648]{0:T(1024)}, u32[]{:S(2)}) copy-start(f32[648]{0:T(1024)} %get-tuple-element.43) | copy-start | bytes 7780
  93.9 3.7 %copy-start.14 = (f32[648]{0:T(1024)S(1)}, f32[648]{0:T(1024)}, u32[]{:S(2)}) copy-start(f32[648]{0:T(1024)} %get-tuple-element.44) | copy-start | bytes 7780
  93.9 3.7 %copy-start.15 = (f32[648]{0:T(1024)S(1)}, f32[648]{0:T(1024)}, u32[]{:S(2)}) copy-start(f32[648]{0:T(1024)} %get-tuple-element.45) | copy-start | bytes 7780
  93.9 3.7 %copy-start.16 = (f32[648]{0:T(1024)S(1)}, f32[648]{0:T(1024)}, u32[]{:S(2)}) copy-start(f32[648]{0:T(1024)} %get-tuple-element.46) | copy-start | bytes 7780
  93.9 3.7 %copy-start.17 = (f32[648]{0:T(1024)S(1)}, f32[648]{0:T(1024)}, u32[]{:S(2)}) copy-start(f32[648]{0:T(1024)} %get-tuple-element.47) | copy-start | bytes 7780
  93.9 3.7 %copy-start.18 = (f32[648]{0:T(1024)S(1)}, f32[648]{0:T(1024)}, u32[]{:S(2)}) copy-start(f32[648]{0:T(1024)} %get-tuple-element.48) | copy-start | bytes 7780
  93.9 3.7 %copy-start.19 = (f32[648]{0:T(1024)S(1)}, f32[648]{0:T(1024)}, u32[]{:S(2)}) copy-start(f32[648]{0:T(1024)} %get-tuple-element.49) | copy-start | bytes 7780
  93.9 3.7 %copy-start.20 = (f32[648]{0:T(1024)S(1)}, f32[648]{0:T(1024)}, u32[]{:S(2)}) copy-start(f32[648]{0:T(1024)} %get-tuple-element.50) | copy-start | bytes 7780
  93.9 3.7 %copy-start.21 = (f32[648]{0:T(1024)S(1)}, f32[648]{0:T(1024)}, u32[]{:S(2)}) copy-start(f32[648]{0:T(1024)} %get-tuple-element.51) | copy-start | bytes 7780
  97.6 6.1 %copy-start.1 = (bf16[1,16,8,8,648]{4,3,2,1,0:T(8,128)(2,1)S(1)}, bf16[1,16,8,8,648]{4,3,2,1,0:T(8,128)(2,1)}, u32[]{:S(2)}) copy-start(bf16[1,16,8,8,648]{4,3,2,1,0:T(8,128)(2,1)} %get-tuple-element.22) | copy-start | bytes 3981316
  97.7 6.1 %copy-start.2 = (bf16[1,16,8,8,648]{4,3,2,1,0:T(8,128)(2,1)S(1)}, bf16[1,16,8,8,648]{4,3,2,1,0:T(8,128)(2,1)}, u32[]{:S(2)}) copy-start(bf16[1,16,8,8,648]{4,3,2,1,0:T(8,128)(2,1)} %get-tuple-element.23) | copy-start | bytes 3981316
  97.7 6.1 %copy-start.3 = (bf16[1,16,8,8,648]{4,3,2,1,0:T(8,128)(2,1)S(1)}, bf16[1,16,8,8,648]{4,3,2,1,0:T(8,128)(2,1)}, u32[]{:S(2)}) copy-start(bf16[1,16,8,8,648]{4,3,2,1,0:T(8,128)(2,1)} %get-tuple-element.24) | copy-start | bytes 3981316
  97.7 6.1 %copy-start.4 = (bf16[1,16,8,8,648]{4,3,2,1,0:T(8,128)(2,1)S(1)}, bf16[1,16,8,8,648]{4,3,2,1,0:T(8,128)(2,1)}, u32[]{:S(2)}) copy-start(bf16[1,16,8,8,648]{4,3,2,1,0:T(8,128)(2,1)} %get-tuple-element.25) | copy-start | bytes 3981316
  97.7 6.1 %copy-start.5 = (bf16[1,16,8,8,648]{4,3,2,1,0:T(8,128)(2,1)S(1)}, bf16[1,16,8,8,648]{4,3,2,1,0:T(8,128)(2,1)}, u32[]{:S(2)}) copy-start(bf16[1,16,8,8,648]{4,3,2,1,0:T(8,128)(2,1)} %get-tuple-element.26) | copy-start | bytes 3981316
  103.8 5.7 %copy-start.6 = (bf16[361,1296]{0,1:T(8,128)(2,1)S(1)}, bf16[361,1296]{0,1:T(8,128)(2,1)}, u32[]{:S(2)}) copy-start(bf16[361,1296]{0,1:T(8,128)(2,1)} %param.11) | copy-start | bytes 2807140

commit v2 on v1

--- a/solution.py
+++ b/solution.py
@@ -6,20 +6,14 @@
 BY = 8
 R = 2
 NOFF = 6
-TILE_ROWS = 16
-TILE = TILE_ROWS * 256
+TILE_ROWS = 8
+TILE = TILE_ROWS * 128
 
 
 def from_behind(value, axis, steps):
     count = lax.axis_size(axis)
     pairs = [(source, (source + steps) % count) for source in range(count)]
     return lax.ppermute(value, axis, pairs)
-
-
-def with_halo(block, axis, dim, width):
-    low = from_behind(lax.slice_in_dim(block, block.shape[dim] - width, None, axis=dim), axis, 1)
-    high = from_behind(lax.slice_in_dim(block, 0, width, axis=dim), axis, -1)
-    return jnp.concatenate([low, block, high], axis=dim)
 
 
 def cyclic_decayed_sum(held, gain_of):
@@ -51,14 +45,40 @@
         flat = jnp.pad(values.reshape(-1), (0, padded - size), constant_values=fill)
         return flat.reshape(count, TILE_ROWS, chunk // TILE_ROWS)
 
-    held = lax.all_to_all(spread(outgoing.astype(jnp.bfloat16), 0), "gz", 0, 0, tiled=True)
-    held = held.reshape(count, chunk).astype(jnp.float32)
+    held = lax.all_to_all(spread(outgoing, 0.0), "gz", 0, 0, tiled=True)
+    held = held.reshape(count, chunk)
     my_rates = lax.dynamic_index_in_dim(spread(rate_full, 1.0).reshape(count, chunk), me, 0, False)
     sums = cyclic_decayed_sum(held, lambda steps: jnp.exp(-my_rates * (layers * steps)))
     sums = jnp.roll(sums, 1, axis=0) / (1.0 - jnp.exp(-my_rates * (layers * count)))
-    sums = sums.astype(jnp.bfloat16).reshape(count, TILE_ROWS, chunk // TILE_ROWS)
+    sums = sums.reshape(count, TILE_ROWS, chunk // TILE_ROWS)
     back = lax.all_to_all(sums, "gz", 0, 0, tiled=True)
-    return back.reshape(-1)[:size].reshape(shape).astype(jnp.float32)
+    return back.reshape(-1)[:size].reshape(shape)
+
+
+def decayed_upward(box_terms, entering, before_term, rate, factor):
+    layers = box_terms.shape[1]
+    layer_pos = jnp.arange(layers, dtype=jnp.float32)[None, :, None, None]
+    upward = jnp.exp(-rate * (layer_pos + 1.0)) * entering[:, None]
+    for j in range(layers - 2):
+        gap = layer_pos - float(j)
+        coeff = jnp.where(gap >= 2.0, jnp.exp(-rate * jnp.maximum(gap, 0.0)), 0.0)
+        upward = upward + coeff * box_terms[:, j : j + 1]
+    first = layer_pos == 0.0
+    return upward - jnp.where(first, factor * before_term[:, None].astype(jnp.float32), 0.0)
+
+
+def expand(multipole, m2x, weight):
+    coeffs, layers, boxes = multipole.shape
+    half_rows = m2x.shape[0] // 2
+    flat = multipole.reshape(coeffs, layers * boxes)
+    halves = []
+    for part in range(2):
+        rows = m2x[part * half_rows : (part + 1) * half_rows]
+        expansion = lax.dot_general(
+            flat, rows, (((0,), (1,)), ((), ())), preferred_element_type=jnp.float32
+        )
+        halves.append(expansion.reshape(layers, boxes, half_rows))
+    return weight * jnp.stack(halves)
 
 
 def body(moments, counts, m2x, x2l, decay_rate, wave_x, wave_y, offsets):
@@ -67,40 +87,36 @@
     half_rows = exp_rows // 2
     columns = plane_size // BY
     ext_columns = columns + 2 * R
-    ext_boxes = ext_columns * BY
+    width = R * BY
     rate = decay_rate[None, None, None, :]
     factor = jnp.exp(-rate)
     weight = jnp.sqrt(1.0 - factor * factor)
     multipole = (moments.astype(jnp.float32) * counts.astype(jnp.float32)[None]).astype(
         jnp.bfloat16
     )
-    multipole = with_halo(multipole, "xy", 2, R * BY).reshape(coeffs, layers * ext_boxes)
-    halves = []
-    for part in range(2):
-        rows = m2x[part * half_rows : (part + 1) * half_rows]
-        expansion = lax.dot_general(
-            multipole, rows, (((0,), (1,)), ((), ())), preferred_element_type=jnp.float32
-        )
-        halves.append(expansion.reshape(layers, ext_boxes, half_rows))
-    box_terms = weight * jnp.stack(halves)
+    halo_low = from_behind(multipole[:, :, plane_size - width :], "xy", 1)
+    halo_high = from_behind(multipole[:, :, :width], "xy", -1)
+    box_terms = expand(multipole, m2x, weight)
+    halo_terms = expand(jnp.concatenate([halo_low, halo_high], axis=2), m2x, weight)
 
     outgoing = box_terms[:, layers - 1]
     for j in range(layers - 1):
         outgoing = outgoing + jnp.exp(-rate[0] * float(layers - 1 - j)) * box_terms[:, j]
     outgoing, box_terms = lax.optimization_barrier((outgoing, box_terms))
     before_term = from_behind(box_terms[:, layers - 1].astype(jnp.bfloat16), "gz", 1)
+    halo_before = from_behind(halo_terms[:, layers - 1].astype(jnp.bfloat16), "gz", 1)
 
     rate_full = jnp.broadcast_to(decay_rate, outgoing.shape)
     entering = entering_sums(outgoing, rate_full, float(layers))
+    entering_low = from_behind(entering[:, plane_size - width :], "xy", 1)
+    entering_high = from_behind(entering[:, :width], "xy", -1)
+    halo_entering = jnp.concatenate([entering_low, entering_high], axis=1)
 
-    layer_pos = jnp.arange(layers, dtype=jnp.float32)[None, :, None, None]
-    upward = jnp.exp(-rate * (layer_pos + 1.0)) * entering[:, None]
-    for j in range(layers - 2):
-        gap = layer_pos - float(j)
-        coeff = jnp.where(gap >= 2.0, jnp.exp(-rate * jnp.maximum(gap, 0.0)), 0.0)
-        upward = upward + coeff * box_terms[:, j : j + 1]
-    first = layer_pos == 0.0
-    upward = upward - jnp.where(first, factor * before_term[:, None].astype(jnp.float32), 0.0)
+    upward = decayed_upward(box_terms, entering, before_term, rate, factor)
+    halo_upward = decayed_upward(halo_terms, halo_entering, halo_before, rate, factor)
+    upward = jnp.concatenate(
+        [halo_upward[:, :, :width], upward, halo_upward[:, :, width:]], axis=2
+    )
 
     field = upward.astype(jnp.bfloat16).reshape(2, layers, ext_columns, BY, half_rows)
     field = jnp.transpose(field, (0, 2, 3, 1, 4))

time: 115 us -> 149 us (1.30)
  local copies, waits for them, and re-layouts: 26.1 us -> 41.3 us
  waiting for transfers between devices: 6.53 us -> 15.4 us
  other arithmetic: 29.1 us -> 36.7 us
  starting transfers between devices: 23.2 us -> 26.3 us
    ppermute x3 -> x6, waiting for transfers between devices: 0.01 us -> 15.4 us  [from_behind(): return lax.ppermute(value, axis, pairs)]
    mul x1 -> x9, local copies, waits for them, and re-layouts: 4.83 us -> 19 us  [the longest x8 16.7 us: decayed_upward(): upward = upward + coeff * box_terms[:, j:j + 1]]
    convert_element_type x4 -> x0, other arithmetic: 9.11 us -> none  [the longest x1 7.12 us: body(): upward.astype(jnp.bfloat16).reshape(2, layers, ext_columns, BY, half_rows)]
    another operation x0 -> x2, other arithmetic: none -> 6.95 us
    all_to_all x1, waiting for transfers between devices: 6.52 us -> 0.01 us  [entering_sums(): back = lax.all_to_all(sums, 'gz', 0, 0, tiled=True)]
    ppermute x3 -> x6, starting transfers between devices: 3.66 us -> 7.32 us  [from_behind(): return lax.ppermute(value, axis, pairs)]
    mul x1 -> x4, other arithmetic: 0.78 us -> 3.88 us  [the longest x2 2.67 us: decayed_upward(): factor * before_term[:, None].astype(jnp.float32)]
    reshape x0 -> x2, local copies, waits for them, and re-layouts: none -> 2.27 us  [the longest x1 1.99 us: entering_sums(): return back.reshape(-1)[:size].reshape(shape)]
  transfers between devices with their start and end apart: 5 -> 8, of which waited for: 1 -> 1; matrix products, arithmetic and copies ran while one was open for 15% -> 30% of each run, Pallas kernels for 0% -> 0%
where the time goes in v2:
time: 149 us; the launch traced here: 147 us
  local copies, waits for them, and re-layouts  41.3 us (28%)
  other arithmetic  36.7 us (25%)
  starting transfers between devices  26.3 us (18%)
  between operations  23.7 us (16%)
  waiting for transfers between devices  15.4 us (10%)
  matrix products  4.11 us (3%)
    mul x8, local copies, waits for them, and re-layouts, decayed_upward(): upward = upward + coeff * box_terms[:, j:j + 1]  16.7 us
    ppermute x6, waiting for transfers between devices, from_behind(): return lax.ppermute(value, axis, pairs)  15.4 us
    convert_element_type x2, other arithmetic, body(): shifted = acc.astype(jnp.bfloat16).reshape(columns * BY * layers, half_rows)  11.7 us
    all_to_all x1, starting transfers between devices, entering_sums(): held = lax.all_to_all(spread(outgoing, 0.0), 'gz', 0, 0, tiled=True)  9.88 us
    all_to_all x1, starting transfers between devices, entering_sums(): back = lax.all_to_all(sums, 'gz', 0, 0, tiled=True)  9.13 us
    ppermute x6, starting transfers between devices, from_behind(): return lax.ppermute(value, axis, pairs)  7.32 us
    another operation x2, other arithmetic  6.95 us
    unnamed x102, local copies, waits for them, and re-layouts  6.01 us
  transfers between devices with their start and end apart: 8, of which 1 were waited for; matrix products, arithmetic and copies ran while one was open for 30% of the time, Pallas kernels for 0%

profile of v2, /device:TPU:0, one launch (start us, length us, event | category | flops | bytes accessed | tf_op | source)
XLA Modules:
  0.0 147.5 jit_solution(17420266762786284294)
XLA Ops:
  0.0 1.6 %copy.48 = bf16[361,8,128]{0,2,1:T(8,128)(2,1)S(1)} copy(bf16[361,8,128]{2,1,0:T(8,128)(2,1)} %param.8) | data formatting | bytes 1478656 | tf_op args[0]
  1.6 0.8 convert_element_type.213
  3.1 0.9 convolution_bitcast_fusion
  4.0 0.9 convolution_bitcast_fusion.1
  4.9 0.6 multiply_exponential_fusion.12
  6.1 2.4 %copy-done = f32[2,8,128,648]{2,3,1,0:T(8,128)} copy-done((f32[2,8,128,648]{2,3,1,0:T(8,128)}, f32[2,8,128,648]{2,3,1,0:T(8,128)S(1)}, u32[]{:S(2)}) %copy-start) | copy-done | bytes 5308440
  8.5 0.8 fusion.34
  9.6 0.7 reshape.611
  10.4 1.1 reshape.612
  11.4 9.9 %all-to-all-start = ((f32[64,8,384]{2,1,0:T(8,128)}), f32[64,8,384]{2,1,0:T(8,128)S(1)}, u32[]{:S(2)}, u32[]{:S(2)}) async-start(f32[64,8,384]{2,1,0:T(8,128)} %reshape.612), calls=%async_computation | async-start | bytes 1572864 | tf_op jit(solution)/shard_map/all_to_all | solution.py:48
  21.3 1.9 %fusion.58 = bf16[2,128,648]{1,2,0:T(8,128)(2,1)} fusion(f32[2,8,128,648]{2,3,1,0:T(8,128)} %copy-done), kind=kLoop, calls=%fused_computation.118 | loop fusion | bytes 663552 | tf_op jit(solution)/shard_map/convert_element_type | solution.py:106
  23.3 0.7 fusion.88
  23.9 2.9 %collective-permute-start.2 = (bf16[361,8,16]{0,2,1:T(8,128)(2,1)}, bf16[361,8,16]{0,2,1:T(8,128)(2,1)S(1)}, u32[]{:S(2)}, u32[]{:S(2)}) collective-permute-start(bf16[361,8,16]{0,2,1:T(8,128)(2,1)} %get-tuple-element.48), channel_id=1, source_target_pairs={{0,1},{1,0},{2,3},{3,2},{4,5},{5,4},{6,7},{7,6},{8,9},{9,8},{10,11... | collective-permute-start | bytes 277256 | tf_op jit(solution)/shard_map/ppermute | solution.py:16
  26.8 0.6 collective-permute-start.3
  27.5 4.1 %slice_bitcast_fusion.14 = (f32[2,128,648]{1,2,0:T(8,128)}, f32[2,128,648]{1,2,0:T(8,128)}, f32[2,128,648]{1,2,0:T(8,128)}, f32[2,128,648]{1,2,0:T(8,128)}, f32[2,128,648]{1,2,0:T(8,128)}, /*index=5*/f32[2,128,648]{1,2,0:T(8,128)}) fusion(f32[2,8,128,648]{2,3,1,0:T(8,128)} %copy-done), kind=kLoop, calls=%fused_computation.106 | loop fusion | bytes 7962624 | tf_op jit(solution)/shard_map/mul | solution.py:65
  35.6 0.7 fusion.89
  58.9 0.7 reshape.614
  59.9 1.5 %multiply_exponential_fusion = (f32[8,648]{1,0:T(8,128)}, f32[8,648]{1,0:T(8,128)}, f32[8,648]{1,0:T(8,128)}, f32[8,648]{1,0:T(8,128)}, f32[8,648]{1,0:T(8,128)}, /*index=5*/f32[8,648]{1,0:T(8,128)}, f32[8,648]{1,0:T(8,128)}) fusion(f32[8]{0:T(128)} %iota_add_fusion.5, f32[648]{0:T(1024)} %get-tuple-element.77, f32[8]{0:T(128)} %get-tuple-element.98, ...), kind=kLoop, calls=%fused_computation.136 | loop fusion | flops 67392 | bytes 148016 | tf_op jit(solution)/shard_map/exp | solution.py:61
  61.4 1.4 fusion.61
  62.8 0.7 subtract_reduce_fusion
  63.6 0.6 div.11
  64.2 1.4 copy.61
  65.5 2.3 %copy.62 = f32[2,128,648]{2,1,0:T(8,128)} copy(f32[2,128,648]{1,2,0:T(8,128)} %get-tuple-element.26) | data formatting | bytes 1327104 | tf_op jit(solution)/shard_map/mul | solution.py:65
  67.8 2.3 %copy.63 = f32[2,128,648]{2,1,0:T(8,128)} copy(f32[2,128,648]{1,2,0:T(8,128)} %get-tuple-element.25) | data formatting | bytes 1327104 | tf_op jit(solution)/shard_map/mul | solution.py:65
  70.1 2.3 %copy.64 = f32[2,128,648]{2,1,0:T(8,128)} copy(f32[2,128,648]{1,2,0:T(8,128)} %get-tuple-element.24) | data formatting | bytes 1327104 | tf_op jit(solution)/shard_map/mul | solution.py:65
  72.4 2.3 %copy.65 = f32[2,128,648]{2,1,0:T(8,128)} copy(f32[2,128,648]{1,2,0:T(8,128)} %get-tuple-element.23) | data formatting | bytes 1327104 | tf_op jit(solution)/shard_map/mul | solution.py:65
  74.7 1.1 copy.66
  77.2 0.8 maximum_multiply_fusion.1
  80.7 0.9 maximum_divide_fusion
  81.7 9.1 %all-to-all-start.1 = ((f32[64,8,384]{2,1,0:T(8,128)}), f32[64,8,384]{2,1,0:T(8,128)S(1)}, u32[]{:S(2)}, u32[]{:S(2)}) async-start(f32[64,8,384]{2,1,0:T(8,128)} %maximum_divide_fusion), calls=%async_computation.1 | async-start | bytes 1572864 | tf_op jit(solution)/shard_map/all_to_all | solution.py:54
  91.0 0.9 slice_bitcast_fusion.20
  91.9 15.3 %collective-permute-done.4 = bf16[2,32,648]{2,1,0:T(8,128)(2,1)S(1)} collective-permute-done((bf16[2,32,648]{2,1,0:T(8,128)(2,1)S(1)}, bf16[2,32,648]{2,1,0:T(8,128)(2,1)S(1)}, u32[]{:S(2)}, u32[]{:S(2)}) %collective-permute-start.4) | collective-permute-done | bytes 82976 | tf_op jit(solution)/shard_map/ppermute | solution.py:16
  107.2 0.7 convert_multiply_fusion.25
  107.9 2.0 %convert_multiply_fusion.24 = f32[2,128,648]{1,2,0:T(8,128)} fusion(bf16[2,128,648]{1,2,0:T(8,128)(2,1)} %collective-permute-done.5, f32[648]{0:T(1024)S(1)} %get-tuple-element.70), kind=kLoop, calls=%fused_computation.100 | loop fusion | flops 331776 | bytes 997920 | tf_op jit(solution)/shard_map/mul | solution.py:67
  109.9 2.3 %copy.67 = f32[2,128,648]{2,1,0:T(8,128)} copy(f32[2,128,648]{1,2,0:T(8,128)} %convert_multiply_fusion.24) | data formatting | bytes 1327104 | tf_op jit(solution)/shard_map/mul | solution.py:67
  112.2 0.9 slice.341
  113.1 2.0 %reshape.615 = f32[2,128,648]{2,1,0:T(8,128)S(1)} reshape(f32[54,8,384]{2,1,0:T(8,128)} %slice.341) | data formatting | bytes 1327104 | tf_op jit(solution)/shard_map/reshape | solution.py:55
  115.1 3.0 %collective-permute-start = (f32[2,16,648]{2,1,0:T(8,128)S(1)}, f32[2,16,648]{2,1,0:T(8,128)S(1)}, u32[]{:S(2)}, u32[]{:S(2)}) collective-permute-start(f32[2,16,648]{2,1,0:T(8,128)S(1)} %get-tuple-element.37), channel_id=1, source_target_pairs={{0,1},{1,0},{2,3},{3,2},{4,5},{5,4},{6,7},{7,6},{8,9},{9,8},{10,11... | collective-permute-start | bytes 248840 | tf_op jit(solution)/shard_map/ppermute | solution.py:16
  118.1 0.6 collective-permute-start.1
  118.8 6.0 %subtract_convert_fusion = bf16[2,8,128,648]{3,1,2,0:T(8,128)(2,1)S(1)} fusion(f32[2,128,648]{2,1,0:T(8,128)} %copy.67, f32[2,128,648]{2,1,0:T(8,128)} %copy.66, f32[8,648]{1,0:T(8,128)} %get-tuple-element.67, f32[2,128,648]{2,1,0:T(8,128)} %copy.65, f32[8,648]{1,0:T(8,128)} %get-tuple-element.66, f32[2,128,648]{2,1,0:T(8,128)} %copy.64, ...), kind=kLoop, calls=%fused_computation | loop fusion | flops 21233664 | bytes 8107784 | tf_op jit(solution)/shard_map/convert.13
  125.0 0.9 subtract_convert_fusion.1
  126.8 1.4 pad_maximum_fusion
  128.3 3.7 %constant_dynamic-slice_fusion.5 = (bf16[1,16,8,8,648]{4,3,2,1,0:T(8,128)(2,1)S(1)}, bf16[1,16,8,8,648]{4,3,2,1,0:T(8,128)(2,1)S(1)}, bf16[1,16,8,8,648]{4,3,2,1...) fusion(bf16[2,20,12,8,648]{4,3,2,1,0:T(8,128)(2,1)S(1)} %pad_ma, ...), kind=kLoop, calls=%fused_computation.165 | loop fusion | bytes 31850548 | tf_op jit(solution)/shard_map/slice | solution.py:135
  132.1 6.1 %fusion.23 = bf16[1024,648]{1,0:T(8,128)(2,1)S(1)} fusion(bf16[1,16,8,8,648]{4,3,2,1,0:T(8,128)(2,1)S(1)} %get-tuple-element.15, bf16[1,16,8,8,648]{4,3,2,1,0:T(8,128)(2,1)S(1)} %get-tuple-element.10, bf16[1,16,8,8,648]{4,3,2,1,0:T(8,128)(2,1)} %get-tuple-element.16, bf16[1,16,8,8,648]{4,3,2,1,0:T(8,128)(2,1)S(1)} %get-tuple-element.11, ...), kind=kLoop, calls=%fused_computation.51 | loop fusion | flops 23887872 | bytes 17283456 | tf_op jit(solution)/shard_map/convert_element_type | solution.py:141
  138.3 5.6 %fusion.11 = bf16[1024,648]{1,0:T(8,128)(2,1)S(1)} fusion(bf16[1,16,8,8,648]{4,3,2,1,0:T(8,128)(2,1)S(1)} %get-tuple-element.15, bf16[1,16,8,8,648]{4,3,2,1,0:T(8,128)(2,1)S(1)} %get-tuple-element.10, bf16[1,16,8,8,648]{4,3,2,1,0:T(8,128)(2,1)S(1)} %copy-done.1, bf16[1,16,8,8,648]{4,3,2,1,0:T(8,128)(2,1)S(1)} %get-tuple-element.11, ...), kind=kLoop, calls=%fused_computation.39 | loop fusion | flops 23887872 | bytes 17283456 | tf_op jit(solution)/shard_map/convert_element_type | solution.py:141
  143.9 0.8 fusion.52
  144.7 0.8 fusion.24
  145.9 1.5 %copy.70 = bf16[361,8,128]{2,1,0:T(8,128)(2,1)} copy(bf16[361,8,128]{0,1,2:T(8,128)(2,1)S(1)} %bitcast.260) | data formatting | bytes 1478656 | tf_op jit(solution)/shard_map/reshape | solution.py:150
  (152 shorter events, 11.2 us)
Async XLA Ops:
  1.6 1.5 %copy-start.6 = (bf16[1296,361]{1,0:T(8,128)(2,1)S(1)}, bf16[1296,361]{1,0:T(8,128)(2,1)}, u32[]{:S(2)}) copy-start(bf16[1296,361]{1,0:T(8,128)(2,1)} %param.10) | copy-start | bytes 2807140
  3.1 1.7 %copy-start.44 = (f32[648]{0:T(1024)S(1)}, f32[648]{0:T(1024)}, u32[]{:S(2)}) copy-start(f32[648]{0:T(1024)} %param.12) | copy-start | bytes 7780
  6.1 2.4 %copy-start = (f32[2,8,128,648]{2,3,1,0:T(8,128)}, f32[2,8,128,648]{2,3,1,0:T(8,128)S(1)}, u32[]{:S(2)}) copy-start(f32[2,8,128,648]{2,3,1,0:T(8,128)S(1)} %maximum_multiply_fusion) | copy-start | bytes 15925252
  11.4 66.6 %all-to-all-start = ((f32[64,8,384]{2,1,0:T(8,128)}), f32[64,8,384]{2,1,0:T(8,128)S(1)}, u32[]{:S(2)}, u32[]{:S(2)}) async-start(f32[64,8,384]{2,1,0:T(8,128)} %reshape.612), calls=%async_computation | async-start | bytes 1572864 | tf_op jit(solution)/shard_map/all_to_all | solution.py:48
  23.2 84.7 %collective-permute-start.5 = (bf16[2,128,648]{1,2,0:T(8,128)(2,1)}, bf16[2,128,648]{1,2,0:T(8,128)(2,1)}, u32[]{:S(2)}, u32[]{:S(2)}) collective-permute-start(bf16[2,128,648]{1,2,0:T(8,128)(2,1)} %fusion.58), channel_id=1, source_target_pairs={{0,2},{2,4},{4,6},{6,8},{8,10},{10,12},{12,14},{14,16},{16,18},{18... | collective-permute-start | bytes 995336 | tf_op jit(solution)/shard_map/ppermute | solution.py:16
  23.9 52.5 %collective-permute-start.2 = (bf16[361,8,16]{0,2,1:T(8,128)(2,1)}, bf16[361,8,16]{0,2,1:T(8,128)(2,1)S(1)}, u32[]{:S(2)}, u32[]{:S(2)}) collective-permute-start(bf16[361,8,16]{0,2,1:T(8,128)(2,1)} %get-tuple-element.48), channel_id=1, source_target_pairs={{0,1},{1,0},{2,3},{3,2},{4,5},{5,4},{6,7},{7,6},{8,9},{9,8},{10,11... | collective-permute-start | bytes 277256 | tf_op jit(solution)/shard_map/ppermute | solution.py:16
  26.8 49.6 %collective-permute-start.3 = (bf16[361,8,16]{0,2,1:T(8,128)(2,1)}, bf16[361,8,16]{0,2,1:T(8,128)(2,1)S(1)}, u32[]{:S(2)}, u32[]{:S(2)}) collective-permute-start(bf16[361,8,16]{0,2,1:T(8,128)(2,1)} %get-tuple-element.49), channel_id=1, source_target_pairs={{0,1},{1,0},{2,3},{3,2},{4,5},{5,4},{6,7},{7,6},{8,9},{9,8},{10,11... | collective-permute-start | bytes 277256 | tf_op jit(solution)/shard_map/ppermute | solution.py:16
  27.5 8.1 %copy-start.43 = (s32[6,2]{0,1:T(2,128)S(1)}, s32[6,2]{0,1:T(2,128)}, u32[]{:S(2)}) copy-start(s32[6,2]{0,1:T(2,128)} %param.15) | copy-start | bytes 148
  65.5 9.2 %copy-start.9 = (f32[2,128,648]{1,2,0:T(8,128)S(1)}, f32[2,128,648]{1,2,0:T(8,128)}, u32[]{:S(2)}) copy-start(f32[2,128,648]{1,2,0:T(8,128)} %get-tuple-element.22) | copy-start | bytes 1990660
  78.3 0.7 copy-start.26
  81.7 30.5 %all-to-all-start.1 = ((f32[64,8,384]{2,1,0:T(8,128)}), f32[64,8,384]{2,1,0:T(8,128)S(1)}, u32[]{:S(2)}, u32[]{:S(2)}) async-start(f32[64,8,384]{2,1,0:T(8,128)} %maximum_divide_fusion), calls=%async_computation.1 | async-start | bytes 1572864 | tf_op jit(solution)/shard_map/all_to_all | solution.py:54
  90.8 16.4 %collective-permute-start.4 = (bf16[2,32,648]{2,1,0:T(8,128)(2,1)S(1)}, bf16[2,32,648]{2,1,0:T(8,128)(2,1)S(1)}, u32[]{:S(2)}, u32[]{:S(2)}) collective-permute-start(bf16[2,32,648]{2,1,0:T(8,128)(2,1)S(1)} %fusion.59), channel_id=1, source_target_pairs={{0,2},{2,4},{4,6},{6,8},{8,10},{10,12},{12,14},{14,16},{16,18},{18... | collective-permute-start | bytes 248840 | tf_op jit(solution)/shard_map/ppermute | solution.py:16
  91.9 26.8 %copy-start.7 = (f32[2,128,648]{2,1,0:T(8,128)S(1)}, f32[2,128,648]{2,1,0:T(8,128)}, u32[]{:S(2)}) copy-start(f32[2,128,648]{2,1,0:T(8,128)} %copy.62) | copy-start | bytes 1990660
  91.9 26.8 %copy-start.8 = (f32[2,128,648]{2,1,0:T(8,128)S(1)}, f32[2,128,648]{2,1,0:T(8,128)}, u32[]{:S(2)}) copy-start(f32[2,128,648]{2,1,0:T(8,128)} %copy.63) | copy-start | bytes 1990660
  91.9 26.8 %copy-start.45 = (pred[8]{0:T(512)(128)(4,1)S(1)}, pred[8]{0:T(512)(128)(4,1)}, u32[]{:S(2)}) copy-start(pred[8]{0:T(512)(128)(4,1)} %iota_compare_fusion) | copy-start | bytes 28
  115.1 9.8 %collective-permute-start = (f32[2,16,648]{2,1,0:T(8,128)S(1)}, f32[2,16,648]{2,1,0:T(8,128)S(1)}, u32[]{:S(2)}, u32[]{:S(2)}) collective-permute-start(f32[2,16,648]{2,1,0:T(8,128)S(1)} %get-tuple-element.37), channel_id=1, source_target_pairs={{0,1},{1,0},{2,3},{3,2},{4,5},{5,4},{6,7},{7,6},{8,9},{9,8},{10,11... | collective-permute-start | bytes 248840 | tf_op jit(solution)/shard_map/ppermute | solution.py:16
  118.1 6.8 %collective-permute-start.1 = (f32[2,16,648]{2,1,0:T(8,128)S(1)}, f32[2,16,648]{2,1,0:T(8,128)S(1)}, u32[]{:S(2)}, u32[]{:S(2)}) collective-permute-start(f32[2,16,648]{2,1,0:T(8,128)S(1)} %get-tuple-element.38), channel_id=1, source_target_pairs={{0,1},{1,0},{2,3},{3,2},{4,5},{5,4},{6,7},{7,6},{8,9},{9,8},{10,11... | collective-permute-start | bytes 248840 | tf_op jit(solution)/shard_map/ppermute | solution.py:16
  118.7 6.2 %copy-start.11 = (f32[2,32,648]{2,1,0:T(8,128)S(1)}, f32[2,32,648]{2,1,0:T(8,128)}, u32[]{:S(2)}) copy-start(f32[2,32,648]{2,1,0:T(8,128)} %get-tuple-element.31) | copy-start | bytes 497668
  118.7 6.2 %copy-start.12 = (f32[2,32,648]{2,1,0:T(8,128)S(1)}, f32[2,32,648]{2,1,0:T(8,128)}, u32[]{:S(2)}) copy-start(f32[2,32,648]{2,1,0:T(8,128)} %get-tuple-element.32) | copy-start | bytes 497668
  118.7 6.2 %copy-start.13 = (f32[2,32,648]{2,1,0:T(8,128)S(1)}, f32[2,32,648]{2,1,0:T(8,128)}, u32[]{:S(2)}) copy-start(f32[2,32,648]{2,1,0:T(8,128)} %get-tuple-element.33) | copy-start | bytes 497668
  118.7 6.2 %copy-start.14 = (f32[2,32,648]{2,1,0:T(8,128)S(1)}, f32[2,32,648]{2,1,0:T(8,128)}, u32[]{:S(2)}) copy-start(f32[2,32,648]{2,1,0:T(8,128)} %get-tuple-element.34) | copy-start | bytes 497668
  118.7 6.2 %copy-start.15 = (f32[2,32,648]{2,1,0:T(8,128)S(1)}, f32[2,32,648]{2,1,0:T(8,128)}, u32[]{:S(2)}) copy-start(f32[2,32,648]{2,1,0:T(8,128)} %convert_multiply_fusion.25) | copy-start | bytes 497668
  118.7 6.2 %copy-start.16 = (f32[8,648]{1,0:T(8,128)S(1)}, f32[8,648]{1,0:T(8,128)}, u32[]{:S(2)}) copy-start(f32[8,648]{1,0:T(8,128)} %get-tuple-element.62) | copy-start | bytes 62212
  118.8 6.2 %copy-start.17 = (f32[8,648]{1,0:T(8,128)S(1)}, f32[8,648]{1,0:T(8,128)}, u32[]{:S(2)}) copy-start(f32[8,648]{1,0:T(8,128)} %get-tuple-element.63) | copy-start | bytes 62212
  118.8 6.2 %copy-start.18 = (f32[8,648]{1,0:T(8,128)S(1)}, f32[8,648]{1,0:T(8,128)}, u32[]{:S(2)}) copy-start(f32[8,648]{1,0:T(8,128)} %get-tuple-element.64) | copy-start | bytes 62212
  118.8 6.2 %copy-start.19 = (f32[8,648]{1,0:T(8,128)S(1)}, f32[8,648]{1,0:T(8,128)}, u32[]{:S(2)}) copy-start(f32[8,648]{1,0:T(8,128)} %get-tuple-element.65) | copy-start | bytes 62212
  118.8 6.2 %copy-start.20 = (f32[8,648]{1,0:T(8,128)S(1)}, f32[8,648]{1,0:T(8,128)}, u32[]{:S(2)}) copy-start(f32[8,648]{1,0:T(8,128)} %get-tuple-element.66) | copy-start | bytes 62212
  118.8 6.2 %copy-start.21 = (f32[8,648]{1,0:T(8,128)S(1)}, f32[8,648]{1,0:T(8,128)}, u32[]{:S(2)}) copy-start(f32[8,648]{1,0:T(8,128)} %get-tuple-element.67) | copy-start | bytes 62212
  118.8 6.2 %copy-start.22 = (f32[8,648]{1,0:T(8,128)S(1)}, f32[8,648]{1,0:T(8,128)}, u32[]{:S(2)}) copy-start(f32[8,648]{1,0:T(8,128)} %get-tuple-element.68) | copy-start | bytes 62212
  118.8 6.2 %copy-start.46 = (pred[8]{0:T(512)(128)(4,1)S(1)}, pred[8]{0:T(512)(128)(4,1)}, u32[]{:S(2)}) copy-start(pred[8]{0:T(512)(128)(4,1)} %iota_compare_fusion) | copy-start | bytes 28
  128.2 3.8 %copy-start.31 = (f32[648]{0:T(1024)S(1)}, f32[648]{0:T(1024)}, u32[]{:S(2)}) copy-start(f32[648]{0:T(1024)} %get-tuple-element.50) | copy-start | bytes 7780
  128.2 3.8 %copy-start.32 = (f32[648]{0:T(1024)S(1)}, f32[648]{0:T(1024)}, u32[]{:S(2)}) copy-start(f32[648]{0:T(1024)} %get-tuple-element.51) | copy-start | bytes 7780
  128.2 3.8 %copy-start.33 = (f32[648]{0:T(1024)S(1)}, f32[648]{0:T(1024)}, u32[]{:S(2)}) copy-start(f32[648]{0:T(1024)} %get-tuple-element.52) | copy-start | bytes 7780
  128.2 3.8 %copy-start.34 = (f32[648]{0:T(1024)S(1)}, f32[648]{0:T(1024)}, u32[]{:S(2)}) copy-start(f32[648]{0:T(1024)} %get-tuple-element.53) | copy-start | bytes 7780
  128.2 3.8 %copy-start.35 = (f32[648]{0:T(1024)S(1)}, f32[648]{0:T(1024)}, u32[]{:S(2)}) copy-start(f32[648]{0:T(1024)} %get-tuple-element.54) | copy-start | bytes 7780
  128.2 3.8 %copy-start.36 = (f32[648]{0:T(1024)S(1)}, f32[648]{0:T(1024)}, u32[]{:S(2)}) copy-start(f32[648]{0:T(1024)} %get-tuple-element.55) | copy-start | bytes 7780
  128.2 3.8 %copy-start.37 = (f32[648]{0:T(1024)S(1)}, f32[648]{0:T(1024)}, u32[]{:S(2)}) copy-start(f32[648]{0:T(1024)} %get-tuple-element.56) | copy-start | bytes 7780
  128.3 3.8 %copy-start.38 = (f32[648]{0:T(1024)S(1)}, f32[648]{0:T(1024)}, u32[]{:S(2)}) copy-start(f32[648]{0:T(1024)} %get-tuple-element.57) | copy-start | bytes 7780
  128.3 3.8 %copy-start.39 = (f32[648]{0:T(1024)S(1)}, f32[648]{0:T(1024)}, u32[]{:S(2)}) copy-start(f32[648]{0:T(1024)} %get-tuple-element.58) | copy-start | bytes 7780
  128.3 3.8 %copy-start.40 = (f32[648]{0:T(1024)S(1)}, f32[648]{0:T(1024)}, u32[]{:S(2)}) copy-start(f32[648]{0:T(1024)} %get-tuple-element.59) | copy-start | bytes 7780
  128.3 3.8 %copy-start.41 = (f32[648]{0:T(1024)S(1)}, f32[648]{0:T(1024)}, u32[]{:S(2)}) copy-start(f32[648]{0:T(1024)} %get-tuple-element.60) | copy-start | bytes 7780
  128.3 3.8 %copy-start.42 = (f32[648]{0:T(1024)S(1)}, f32[648]{0:T(1024)}, u32[]{:S(2)}) copy-start(f32[648]{0:T(1024)} %get-tuple-element.61) | copy-start | bytes 7780
  132.1 6.1 %copy-start.1 = (bf16[1,16,8,8,648]{4,3,2,1,0:T(8,128)(2,1)S(1)}, bf16[1,16,8,8,648]{4,3,2,1,0:T(8,128)(2,1)}, u32[]{:S(2)}) copy-start(bf16[1,16,8,8,648]{4,3,2,1,0:T(8,128)(2,1)} %get-tuple-element.16) | copy-start | bytes 3981316
  132.1 6.1 %copy-start.2 = (bf16[1,16,8,8,648]{4,3,2,1,0:T(8,128)(2,1)S(1)}, bf16[1,16,8,8,648]{4,3,2,1,0:T(8,128)(2,1)}, u32[]{:S(2)}) copy-start(bf16[1,16,8,8,648]{4,3,2,1,0:T(8,128)(2,1)} %get-tuple-element.17) | copy-start | bytes 3981316
  132.1 6.1 %copy-start.3 = (bf16[1,16,8,8,648]{4,3,2,1,0:T(8,128)(2,1)S(1)}, bf16[1,16,8,8,648]{4,3,2,1,0:T(8,128)(2,1)}, u32[]{:S(2)}) copy-start(bf16[1,16,8,8,648]{4,3,2,1,0:T(8,128)(2,1)} %get-tuple-element.18) | copy-start | bytes 3981316
  132.1 6.1 %copy-start.4 = (bf16[1,16,8,8,648]{4,3,2,1,0:T(8,128)(2,1)S(1)}, bf16[1,16,8,8,648]{4,3,2,1,0:T(8,128)(2,1)}, u32[]{:S(2)}) copy-start(bf16[1,16,8,8,648]{4,3,2,1,0:T(8,128)(2,1)} %get-tuple-element.19) | copy-start | bytes 3981316
  132.1 6.1 %copy-start.5 = (bf16[1,16,8,8,648]{4,3,2,1,0:T(8,128)(2,1)S(1)}, bf16[1,16,8,8,648]{4,3,2,1,0:T(8,128)(2,1)}, u32[]{:S(2)}) copy-start(bf16[1,16,8,8,648]{4,3,2,1,0:T(8,128)(2,1)} %get-tuple-element.20) | copy-start | bytes 3981316
  138.3 5.7 %copy-start.10 = (bf16[361,1296]{0,1:T(8,128)(2,1)S(1)}, bf16[361,1296]{0,1:T(8,128)(2,1)}, u32[]{:S(2)}) copy-start(bf16[361,1296]{0,1:T(8,128)(2,1)} %param.11) | copy-start | bytes 2807140
  (7 other events, 4.8 us)

commit v3 on v1

--- a/solution.py
+++ b/solution.py
@@ -6,8 +6,8 @@
 BY = 8
 R = 2
 NOFF = 6
-TILE_ROWS = 16
-TILE = TILE_ROWS * 256
+TILE_ROWS = 8
+TILE = TILE_ROWS * 512
 
 
 def from_behind(value, axis, steps):
@@ -51,14 +51,14 @@
         flat = jnp.pad(values.reshape(-1), (0, padded - size), constant_values=fill)
         return flat.reshape(count, TILE_ROWS, chunk // TILE_ROWS)
 
-    held = lax.all_to_all(spread(outgoing.astype(jnp.bfloat16), 0), "gz", 0, 0, tiled=True)
-    held = held.reshape(count, chunk).astype(jnp.float32)
+    held = lax.all_to_all(spread(outgoing, 0.0), "gz", 0, 0, tiled=True)
+    held = held.reshape(count, chunk)
     my_rates = lax.dynamic_index_in_dim(spread(rate_full, 1.0).reshape(count, chunk), me, 0, False)
     sums = cyclic_decayed_sum(held, lambda steps: jnp.exp(-my_rates * (layers * steps)))
     sums = jnp.roll(sums, 1, axis=0) / (1.0 - jnp.exp(-my_rates * (layers * count)))
-    sums = sums.astype(jnp.bfloat16).reshape(count, TILE_ROWS, chunk // TILE_ROWS)
+    sums = sums.reshape(count, TILE_ROWS, chunk // TILE_ROWS)
     back = lax.all_to_all(sums, "gz", 0, 0, tiled=True)
-    return back.reshape(-1)[:size].reshape(shape).astype(jnp.float32)
+    return back.reshape(-1)[:size].reshape(shape)
 
 
 def body(moments, counts, m2x, x2l, decay_rate, wave_x, wave_y, offsets):

time: 115 us -> 117 us (1.017)
  the two profiles are of different devices: /device:TPU:0 before, /device:TPU:1 now
where the time goes in v3:
time: 117 us; the launch traced here: 116 us
  other arithmetic  28 us (24%)
  local copies, waits for them, and re-layouts  27.3 us (23%)
  between operations  23.2 us (20%)
  starting transfers between devices  20.8 us (18%)
  waiting for transfers between devices  11.6 us (10%)
  matrix products  5.04 us (4%)
    convert_element_type x2, other arithmetic, body(): shifted = acc.astype(jnp.bfloat16).reshape(columns * BY * layers, half_rows)  11.7 us
    all_to_all x1, starting transfers between devices, entering_sums(): held = lax.all_to_all(spread(outgoing, 0.0), 'gz', 0, 0, tiled=True)  10.6 us
    all_to_all x1, waiting for transfers between devices, entering_sums(): held = lax.all_to_all(spread(outgoing, 0.0), 'gz', 0, 0, tiled=True)  8.93 us
    convert_element_type x1, other arithmetic, body(): upward.astype(jnp.bfloat16).reshape(2, layers, ext_columns, BY, half_rows)  7.33 us
    unnamed x72, local copies, waits for them, and re-layouts  6.98 us
    ppermute x3, starting transfers between devices, from_behind(): return lax.ppermute(value, axis, pairs)  5.55 us
    mul x1, local copies, waits for them, and re-layouts, body(): upward = upward + coeff * box_terms[:, j:j + 1]  4.95 us
    all_to_all x1, starting transfers between devices, entering_sums(): back = lax.all_to_all(sums, 'gz', 0, 0, tiled=True)  4.67 us
  transfers between devices with their start and end apart: 5, of which 2 were waited for; matrix products, arithmetic and copies ran while one was open for 11% of the time, Pallas kernels for 0%

profile of v3, /device:TPU:1, one launch (start us, length us, event | category | flops | bytes accessed | tf_op | source)
XLA Modules:
  0.0 116.0 jit_solution(13789233399171886685)
XLA Ops:
  0.0 1.6 %copy.31 = bf16[361,8,128]{0,2,1:T(8,128)(2,1)S(1)} copy(bf16[361,8,128]{2,1,0:T(8,128)(2,1)} %param.8) | data formatting | bytes 1478656 | tf_op args[0]
  1.6 0.7 convert_element_type.205
  2.3 0.2 multiply_convert_fusion
  2.5 3.8 %collective-permute-start = (bf16[361,8,16]{0,2,1:T(8,128)(2,1)S(1)}, bf16[361,8,16]{0,2,1:T(8,128)(2,1)S(1)}, u32[]{:S(2)}, u32[]{:S(2)}) collective-permute-start(bf16[361,8,16]{0,2,1:T(8,128)(2,1)S(1)} %get-tuple-element.38), channel_id=1, source_target_pairs={{0,1},{1,0},{2,3},{3,2},{4,5},{5,4},{6,7},{7,6},{8,9},{9,8},{10,11... | collective-permute-start | bytes 277256 | tf_op jit(solution)/shard_map/ppermute | solution.py:16
  6.6 0.9 reshape.604
  7.6 0.2 reshape_reshape.3
  7.8 0.7 fusion.81
  8.5 0.2 subtract_reduce_fusion
  8.6 2.7 %collective-permute-done.1 = bf16[361,8,16]{0,2,1:T(8,128)(2,1)S(1)} collective-permute-done((bf16[361,8,16]{0,2,1:T(8,128)(2,1)S(1)}, bf16[361,8,16]{0,2,1:T(8,128)(2,1)S(1)}, u32[]{:S(2)}, u32[]{:S(2)}) %collective-permute-start.1) | collective-permute-done | bytes 92448 | tf_op jit(solution)/shard_map/ppermute | solution.py:16
  11.3 2.2 %convolution_bitcast_fusion.1 = f32[1,8,160,648]{3,2,1,0:T(8,128)S(1)} fusion(bf16[1296,361]{1,0:T(8,128)(2,1)} %param.10, bf16[361,8,16]{0,2,1:T(8,128)(2,1)S(1)} %collective-permute-done.1, bf16[361,8,128]{0,2,1:T(8,128)(2,1)S(1)} %multiply_convert_fusion, bf16[361,8,16]{0,2,1:T(8,128)(2,1)S(1)} %collective-permute-done), kind=kOutput, calls=%fused_computation.52 | convolution fusion | flops 601628160 | bytes 4739584 | tf_op jit(solution)/shard_map/dot_general | solution.py:81
  13.6 1.2 %convolution_bitcast_fusion = f32[1,8,160,648]{3,2,1,0:T(8,128)S(1)} fusion(bf16[1296,361]{1,0:T(8,128)(2,1)S(1)} %copy-done.7, bf16[361,8,16]{0,2,1:T(8,128)(2,1)S(1)} %collective-permute-done.1, bf16[361,8,128]{0,2,1:T(8,128)(2,1)S(1)} %multiply_convert_fusion, bf16[361,8,16]{0,2,1:T(8,128)(2,1)S(1)} %collective-permute-done), kind=kOutput, calls=%fused_computation.51 | convolution fusion | flops 601628160 | bytes 4798464 | tf_op jit(solution)/shard_map/dot_general | solution.py:81
  14.8 0.8 maximum_multiply_fusion
  15.6 3.1 %copy-done = f32[2,8,160,648]{3,2,1,0:T(8,128)} copy-done((f32[2,8,160,648]{3,2,1,0:T(8,128)}, f32[2,8,160,648]{3,2,1,0:T(8,128)S(1)}, u32[]{:S(2)}) %copy-start) | copy-done | bytes 6635544
  18.6 0.5 fusion.32
  19.2 0.9 reshape.601
  20.2 1.2 %reshape.602 = f32[64,8,512]{2,1,0:T(8,128)} reshape(f32[262144]{0:T(1024)S(1)} %pad.7) | data formatting | bytes 2097152 | tf_op jit(solution)/shard_map/reshape | solution.py:52
  21.4 10.6 %all-to-all-start = ((f32[64,8,512]{2,1,0:T(8,128)}), f32[64,8,512]{2,1,0:T(8,128)S(1)}, u32[]{:S(2)}, u32[]{:S(2)}) async-start(f32[64,8,512]{2,1,0:T(8,128)} %reshape.602), calls=%async_computation | async-start | bytes 2097152 | tf_op jit(solution)/shard_map/all_to_all | solution.py:54
  39.5 0.7 fusion.54
  40.2 0.7 multiply_exponential_fusion
  40.9 8.9 %all-to-all-done = f32[64,8,512]{2,1,0:T(8,128)S(1)} async-done(((f32[64,8,512]{2,1,0:T(8,128)}), f32[64,8,512]{2,1,0:T(8,128)S(1)}, u32[]{:S(2)}, u32[]{:S(2)}) %all-to-all-start) | async-done | bytes 1048608 | tf_op jit(solution)/shard_map/all_to_all | solution.py:54
  50.0 0.6 copy.55
  50.6 0.6 copy.53
  51.3 0.2 fusion.25
  51.5 0.2 fusion.26
  51.7 0.2 fusion.27
  51.9 0.1 fusion.28
  52.1 0.1 fusion.29
  52.5 0.6 copy.56
  53.2 1.2 %maximum_divide_fusion = f32[64,8,512]{2,1,0:T(8,128)} fusion(f32[63,8,512]{2,1,0:T(8,128)S(1)} %slice.297, f32[1,8,512]{2,1,0:T(8,128)S(1)} %concatenate.45, f32[8,512]{1,0:T(8,128)S(1)} %div.11), kind=kLoop, calls=%fused_computation.68 | loop fusion | flops 524288 | bytes 2113536 | tf_op jit(solution)/shard_map/div | solution.py:58
  54.4 4.7 %all-to-all-start.1 = ((f32[64,8,512]{2,1,0:T(8,128)}), f32[64,8,512]{2,1,0:T(8,128)S(1)}, u32[]{:S(2)}, u32[]{:S(2)}) async-start(f32[64,8,512]{2,1,0:T(8,128)} %maximum_divide_fusion), calls=%async_computation.1 | async-start | bytes 2097152 | tf_op jit(solution)/shard_map/all_to_all | solution.py:60
  59.1 2.0 %fusion.52 = bf16[2,160,648]{2,1,0:T(8,128)(2,1)} fusion(f32[2,8,160,648]{3,2,1,0:T(8,128)} %copy-done), kind=kLoop, calls=%fused_computation.107 | loop fusion | bytes 829440 | tf_op jit(solution)/shard_map/convert_element_type | solution.py:91
  61.1 1.6 %collective-permute-start.2 = (bf16[2,160,648]{2,1,0:T(8,128)(2,1)}, bf16[2,160,648]{2,1,0:T(8,128)(2,1)S(1)}, u32[]{:S(2)}, u32[]{:S(2)}) collective-permute-start(bf16[2,160,648]{2,1,0:T(8,128)(2,1)} %fusion.52), channel_id=1, source_target_pairs={{0,2},{2,4},{4,6},{6,8},{8,10},{10,12},{12,14},{14,16},{16,18},{18... | collective-permute-start | bytes 1244168 | tf_op jit(solution)/shard_map/ppermute | solution.py:16
  62.8 0.6 iota_compare_fusion
  78.3 5.0 %slice_bitcast_fusion.13 = (f32[2,20,8,648]{3,2,1,0:T(8,128)S(1)}, f32[2,20,8,648]{3,2,1,0:T(8,128)S(1)}, f32[2,20,8,648]{3,2,1,0:T(8,128)}, f32[2,20,8,648]{3,2...) fusion(f32[2,8,160,648]{3,2,1,0:T(8,128)} %copy-done), kind=kLoop, calls=%fused_computation.99 | loop fusion | bytes 9953280 | tf_op jit(solution)/shard_map/mul | solution.py:101
  83.3 1.0 multiply_bitcast_fusion
  84.4 0.3 copy.57
  84.6 1.0 slice.293
  85.6 2.2 %mul.798 = f32[2,20,8,648]{3,2,1,0:T(8,128)S(1)} reshape(f32[207360]{0:T(1024)} %slice.293) | data formatting | bytes 1658880 | tf_op jit(solution)/shard_map/mul | solution.py:97
  87.9 7.3 %subtract_convert_fusion = bf16[2,20,8,8,648]{4,3,2,1,0:T(8,128)(2,1)S(1)} fusion(f32[2,20,8,648]{3,2,1,0:T(8,128)} %multiply_bitcast_fusion, f32[2,20,8,648]{3,2,1,0:T(8,128)S(1)} %get-tuple-element.10, f32[8,648]{1,0:T(8,128)S(1)} %copy-done.11, f32[2,20,8,648]{3,2,1,0:T(8,128)} %get-tuple-element.11, f32[8,648]{1,0:T(8,128)S(1)} %copy-done.10, ...), kind=kLoop, calls=%fused_computation.1 | loop fusion | flops 26542080 | bytes 10098440 | tf_op jit(solution)/shard_map/convert_element_type | solution.py:105
  95.2 0.2 fusion.77
  95.4 1.4 %pad_maximum_fusion = bf16[2,20,12,8,648]{4,3,2,1,0:T(8,128)(2,1)S(1)} fusion(bf16[2,20,2,8,648]{4,3,2,1,0:T(8,128)(2,1)S(1)} %get-tuple-element.28, bf16[2,20,8,8,648]{4,3,2,1,0:T(8,128)(2,1)S(1)} %subtract_convert_fusion, bf16[2,20,2,8,648]{4,3,2,1,0:T(8,128)(2,1)S(1)} %get-tuple-element.27), kind=kLoop, calls=%fused_computation.2 | loop fusion | flops 4976640 | bytes 9953280 | tf_op jit(solution)/shard_map/concatenate | solution.py:107
  96.9 3.6 %constant_dynamic-slice_fusion.5 = (bf16[1,16,8,8,648]{4,3,2,1,0:T(8,128)(2,1)S(1)}, bf16[1,16,8,8,648]{4,3,2,1,0:T(8,128)(2,1)S(1)}, bf16[1,16,8,8,648]{4,3,2,1...) fusion(bf16[2,20,12,8,648]{4,3,2,1,0:T(8,128)(2,1)S(1)} %pad_ma, ...), kind=kLoop, calls=%fused_computation.143 | loop fusion | bytes 31850548 | tf_op jit(solution)/shard_map/slice | solution.py:119
  100.6 6.1 %fusion.23 = bf16[1024,648]{1,0:T(8,128)(2,1)S(1)} fusion(bf16[1,16,8,8,648]{4,3,2,1,0:T(8,128)(2,1)S(1)} %get-tuple-element.21, bf16[1,16,8,8,648]{4,3,2,1,0:T(8,128)(2,1)S(1)} %get-tuple-element.16, bf16[1,16,8,8,648]{4,3,2,1,0:T(8,128)(2,1)} %get-tuple-element.22, bf16[1,16,8,8,648]{4,3,2,1,0:T(8,128)(2,1)S(1)} %get-tuple-element.17, ...), kind=kLoop, calls=%fused_computation.50 | loop fusion | flops 23887872 | bytes 17283456 | tf_op jit(solution)/shard_map/convert_element_type | solution.py:125
  106.8 5.6 %fusion.11 = bf16[1024,648]{1,0:T(8,128)(2,1)S(1)} fusion(bf16[1,16,8,8,648]{4,3,2,1,0:T(8,128)(2,1)S(1)} %get-tuple-element.21, bf16[1,16,8,8,648]{4,3,2,1,0:T(8,128)(2,1)S(1)} %get-tuple-element.16, bf16[1,16,8,8,648]{4,3,2,1,0:T(8,128)(2,1)S(1)} %copy-done.1, bf16[1,16,8,8,648]{4,3,2,1,0:T(8,128)(2,1)S(1)} %get-tuple-element.17, ...), kind=kLoop, calls=%fused_computation.38 | loop fusion | flops 23887872 | bytes 17283456 | tf_op jit(solution)/shard_map/convert_element_type | solution.py:125
  112.4 0.8 fusion.48
  113.2 0.8 fusion.24
  114.1 0.4 copy.40
  114.4 1.5 %copy.42 = bf16[361,8,128]{2,1,0:T(8,128)(2,1)} copy(bf16[361,8,128]{0,1,2:T(8,128)(2,1)S(1)} %bitcast.233) | data formatting | bytes 1478656 | tf_op jit(solution)/shard_map/reshape | solution.py:134
  (95 shorter events, 1.2 us)
Async XLA Ops:
  0.0 6.5 %copy-start.28 = (f32[648]{0:T(1024)S(1)}, f32[648]{0:T(1024)}, u32[]{:S(2)}) copy-start(f32[648]{0:T(1024)} %param.12) | copy-start | bytes 7780
  2.5 6.1 %collective-permute-start = (bf16[361,8,16]{0,2,1:T(8,128)(2,1)S(1)}, bf16[361,8,16]{0,2,1:T(8,128)(2,1)S(1)}, u32[]{:S(2)}, u32[]{:S(2)}) collective-permute-start(bf16[361,8,16]{0,2,1:T(8,128)(2,1)S(1)} %get-tuple-element.38), channel_id=1, source_target_pairs={{0,1},{1,0},{2,3},{3,2},{4,5},{5,4},{6,7},{7,6},{8,9},{9,8},{10,11... | collective-permute-start | bytes 277256 | tf_op jit(solution)/shard_map/ppermute | solution.py:16
  6.4 5.0 %collective-permute-start.1 = (bf16[361,8,16]{0,2,1:T(8,128)(2,1)S(1)}, bf16[361,8,16]{0,2,1:T(8,128)(2,1)S(1)}, u32[]{:S(2)}, u32[]{:S(2)}) collective-permute-start(bf16[361,8,16]{0,2,1:T(8,128)(2,1)S(1)} %get-tuple-element.39), channel_id=1, source_target_pairs={{0,1},{1,0},{2,3},{3,2},{4,5},{5,4},{6,7},{7,6},{8,9},{9,8},{10,11... | collective-permute-start | bytes 277256 | tf_op jit(solution)/shard_map/ppermute | solution.py:16
  6.5 9.1 %copy-start.13 = (f32[648]{0:T(1024)}, f32[648]{0:T(1024)S(1)}, u32[]{:S(2)}) copy-start(f32[648]{0:T(1024)S(1)} %get-tuple-element.60) | copy-start | bytes 7780
  6.5 1.3 %copy-start.27 = (s32[6,2]{0,1:T(2,128)S(1)}, s32[6,2]{0,1:T(2,128)}, u32[]{:S(2)}) copy-start(s32[6,2]{0,1:T(2,128)} %param.15) | copy-start | bytes 148
  7.8 5.8 %copy-start.7 = (bf16[1296,361]{1,0:T(8,128)(2,1)S(1)}, bf16[1296,361]{1,0:T(8,128)(2,1)}, u32[]{:S(2)}) copy-start(bf16[1296,361]{1,0:T(8,128)(2,1)} %param.10) | copy-start | bytes 2807140
  15.6 3.1 %copy-start = (f32[2,8,160,648]{3,2,1,0:T(8,128)}, f32[2,8,160,648]{3,2,1,0:T(8,128)S(1)}, u32[]{:S(2)}) copy-start(f32[2,8,160,648]{3,2,1,0:T(8,128)S(1)} %maximum_multiply_fusion) | copy-start | bytes 19906564
  20.1 19.4 %copy-start.29 = (f32[648]{0:T(1024)S(1)}, f32[648]{0:T(1024)}, u32[]{:S(2)}) copy-start(f32[648]{0:T(1024)} %param.14) | copy-start | bytes 7780
  20.1 19.4 %copy-start.30 = (f32[648]{0:T(1024)S(1)}, f32[648]{0:T(1024)}, u32[]{:S(2)}) copy-start(f32[648]{0:T(1024)} %param.13) | copy-start | bytes 7780
  21.4 28.5 %all-to-all-start = ((f32[64,8,512]{2,1,0:T(8,128)}), f32[64,8,512]{2,1,0:T(8,128)S(1)}, u32[]{:S(2)}, u32[]{:S(2)}) async-start(f32[64,8,512]{2,1,0:T(8,128)} %reshape.602), calls=%async_computation | async-start | bytes 2097152 | tf_op jit(solution)/shard_map/all_to_all | solution.py:54
  54.4 29.9 %all-to-all-start.1 = ((f32[64,8,512]{2,1,0:T(8,128)}), f32[64,8,512]{2,1,0:T(8,128)S(1)}, u32[]{:S(2)}, u32[]{:S(2)}) async-start(f32[64,8,512]{2,1,0:T(8,128)} %maximum_divide_fusion), calls=%async_computation.1 | async-start | bytes 2097152 | tf_op jit(solution)/shard_map/all_to_all | solution.py:60
  61.1 22.1 %collective-permute-start.2 = (bf16[2,160,648]{2,1,0:T(8,128)(2,1)}, bf16[2,160,648]{2,1,0:T(8,128)(2,1)S(1)}, u32[]{:S(2)}, u32[]{:S(2)}) collective-permute-start(bf16[2,160,648]{2,1,0:T(8,128)(2,1)} %fusion.52), channel_id=1, source_target_pairs={{0,2},{2,4},{4,6},{6,8},{8,10},{10,12},{12,14},{14,16},{16,18},{18... | collective-permute-start | bytes 1244168 | tf_op jit(solution)/shard_map/ppermute | solution.py:16
  78.3 5.0 %copy-start.14 = (f32[648]{0:T(1024)S(1)}, f32[648]{0:T(1024)}, u32[]{:S(2)}) copy-start(f32[648]{0:T(1024)} %copy-done.13) | copy-start | bytes 7780
  84.3 3.5 %copy-start.8 = (f32[8,648]{1,0:T(8,128)S(1)}, f32[8,648]{1,0:T(8,128)}, u32[]{:S(2)}) copy-start(f32[8,648]{1,0:T(8,128)} %get-tuple-element.54) | copy-start | bytes 62212
  84.3 3.5 %copy-start.9 = (f32[8,648]{1,0:T(8,128)S(1)}, f32[8,648]{1,0:T(8,128)}, u32[]{:S(2)}) copy-start(f32[8,648]{1,0:T(8,128)} %get-tuple-element.55) | copy-start | bytes 62212
  84.3 3.5 %copy-start.10 = (f32[8,648]{1,0:T(8,128)S(1)}, f32[8,648]{1,0:T(8,128)}, u32[]{:S(2)}) copy-start(f32[8,648]{1,0:T(8,128)} %get-tuple-element.56) | copy-start | bytes 62212
  84.3 3.5 %copy-start.11 = (f32[8,648]{1,0:T(8,128)S(1)}, f32[8,648]{1,0:T(8,128)}, u32[]{:S(2)}) copy-start(f32[8,648]{1,0:T(8,128)} %get-tuple-element.57) | copy-start | bytes 62212
  84.3 3.5 %copy-start.12 = (f32[8,648]{1,0:T(8,128)S(1)}, f32[8,648]{1,0:T(8,128)}, u32[]{:S(2)}) copy-start(f32[8,648]{1,0:T(8,128)} %get-tuple-element.58) | copy-start | bytes 62212
  84.3 3.5 %copy-start.31 = (pred[8]{0:T(512)(128)(4,1)S(1)}, pred[8]{0:T(512)(128)(4,1)}, u32[]{:S(2)}) copy-start(pred[8]{0:T(512)(128)(4,1)} %iota_compare_fusion) | copy-start | bytes 28
  96.8 3.7 %copy-start.15 = (f32[648]{0:T(1024)S(1)}, f32[648]{0:T(1024)}, u32[]{:S(2)}) copy-start(f32[648]{0:T(1024)} %get-tuple-element.40) | copy-start | bytes 7780
  96.8 3.7 %copy-start.16 = (f32[648]{0:T(1024)S(1)}, f32[648]{0:T(1024)}, u32[]{:S(2)}) copy-start(f32[648]{0:T(1024)} %get-tuple-element.41) | copy-start | bytes 7780
  96.8 3.7 %copy-start.17 = (f32[648]{0:T(1024)S(1)}, f32[648]{0:T(1024)}, u32[]{:S(2)}) copy-start(f32[648]{0:T(1024)} %get-tuple-element.42) | copy-start | bytes 7780
  96.8 3.7 %copy-start.18 = (f32[648]{0:T(1024)S(1)}, f32[648]{0:T(1024)}, u32[]{:S(2)}) copy-start(f32[648]{0:T(1024)} %get-tuple-element.43) | copy-start | bytes 7780
  96.8 3.7 %copy-start.19 = (f32[648]{0:T(1024)S(1)}, f32[648]{0:T(1024)}, u32[]{:S(2)}) copy-start(f32[648]{0:T(1024)} %get-tuple-element.44) | copy-start | bytes 7780
  96.8 3.7 %copy-start.20 = (f32[648]{0:T(1024)S(1)}, f32[648]{0:T(1024)}, u32[]{:S(2)}) copy-start(f32[648]{0:T(1024)} %get-tuple-element.45) | copy-start | bytes 7780
  96.8 3.7 %copy-start.21 = (f32[648]{0:T(1024)S(1)}, f32[648]{0:T(1024)}, u32[]{:S(2)}) copy-start(f32[648]{0:T(1024)} %get-tuple-element.46) | copy-start | bytes 7780
  96.8 3.7 %copy-start.22 = (f32[648]{0:T(1024)S(1)}, f32[648]{0:T(1024)}, u32[]{:S(2)}) copy-start(f32[648]{0:T(1024)} %get-tuple-element.47) | copy-start | bytes 7780
  96.9 3.7 %copy-start.23 = (f32[648]{0:T(1024)S(1)}, f32[648]{0:T(1024)}, u32[]{:S(2)}) copy-start(f32[648]{0:T(1024)} %get-tuple-element.48) | copy-start | bytes 7780
  96.9 3.7 %copy-start.24 = (f32[648]{0:T(1024)S(1)}, f32[648]{0:T(1024)}, u32[]{:S(2)}) copy-start(f32[648]{0:T(1024)} %get-tuple-element.49) | copy-start | bytes 7780
  96.9 3.7 %copy-start.25 = (f32[648]{0:T(1024)S(1)}, f32[648]{0:T(1024)}, u32[]{:S(2)}) copy-start(f32[648]{0:T(1024)} %get-tuple-element.50) | copy-start | bytes 7780
  96.9 3.7 %copy-start.26 = (f32[648]{0:T(1024)S(1)}, f32[648]{0:T(1024)}, u32[]{:S(2)}) copy-start(f32[648]{0:T(1024)} %get-tuple-element.51) | copy-start | bytes 7780
  100.6 6.1 %copy-start.1 = (bf16[1,16,8,8,648]{4,3,2,1,0:T(8,128)(2,1)S(1)}, bf16[1,16,8,8,648]{4,3,2,1,0:T(8,128)(2,1)}, u32[]{:S(2)}) copy-start(bf16[1,16,8,8,648]{4,3,2,1,0:T(8,128)(2,1)} %get-tuple-element.22) | copy-start | bytes 3981316
  100.6 6.1 %copy-start.2 = (bf16[1,16,8,8,648]{4,3,2,1,0:T(8,128)(2,1)S(1)}, bf16[1,16,8,8,648]{4,3,2,1,0:T(8,128)(2,1)}, u32[]{:S(2)}) copy-start(bf16[1,16,8,8,648]{4,3,2,1,0:T(8,128)(2,1)} %get-tuple-element.23) | copy-start | bytes 3981316
  100.6 6.1 %copy-start.3 = (bf16[1,16,8,8,648]{4,3,2,1,0:T(8,128)(2,1)S(1)}, bf16[1,16,8,8,648]{4,3,2,1,0:T(8,128)(2,1)}, u32[]{:S(2)}) copy-start(bf16[1,16,8,8,648]{4,3,2,1,0:T(8,128)(2,1)} %get-tuple-element.24) | copy-start | bytes 3981316
  100.6 6.1 %copy-start.4 = (bf16[1,16,8,8,648]{4,3,2,1,0:T(8,128)(2,1)S(1)}, bf16[1,16,8,8,648]{4,3,2,1,0:T(8,128)(2,1)}, u32[]{:S(2)}) copy-start(bf16[1,16,8,8,648]{4,3,2,1,0:T(8,128)(2,1)} %get-tuple-element.25) | copy-start | bytes 3981316
  100.6 6.1 %copy-start.5 = (bf16[1,16,8,8,648]{4,3,2,1,0:T(8,128)(2,1)S(1)}, bf16[1,16,8,8,648]{4,3,2,1,0:T(8,128)(2,1)}, u32[]{:S(2)}) copy-start(bf16[1,16,8,8,648]{4,3,2,1,0:T(8,128)(2,1)} %get-tuple-element.26) | copy-start | bytes 3981316
  106.8 5.7 %copy-start.6 = (bf16[361,1296]{0,1:T(8,128)(2,1)S(1)}, bf16[361,1296]{0,1:T(8,128)(2,1)}, u32[]{:S(2)}) copy-start(bf16[361,1296]{0,1:T(8,128)(2,1)} %param.11) | copy-start | bytes 2807140

commit v4 on v3

--- a/solution.py
+++ b/solution.py
@@ -1,6 +1,8 @@
 import jax
 import jax.numpy as jnp
 from jax import lax
+from jax.experimental import pallas as pl
+from jax.experimental.pallas import tpu as pltpu
 from jax.sharding import PartitionSpec as P
 
 BY = 8
@@ -61,6 +63,61 @@
     return back.reshape(-1)[:size].reshape(shape)
 
 
+def shift_kernel(steps_ref, terms_ref, entering_ref, before_ref, coef_ref, lift_ref, factor_ref,
+                 cos_ref, sin_ref, out_ref, field_ref):
+    _, layers, boxes, width = terms_ref.shape
+    _, _, columns, rows, _ = out_ref.shape
+    for i in range(layers):
+        up = lift_ref[i] * entering_ref[...]
+        for j in range(i - 1):
+            up = up + coef_ref[i, j] * terms_ref[:, j]
+        if i == 0:
+            up = up - factor_ref[...] * before_ref[...].astype(jnp.float32)
+        up = up.astype(jnp.bfloat16).astype(jnp.float32)
+        field_ref[...] = up.reshape(2, boxes // rows, rows, width)
+        acc_real = jnp.zeros((columns, rows, width), jnp.float32)
+        acc_imag = jnp.zeros((columns, rows, width), jnp.float32)
+        for entry in range(NOFF):
+            start = jnp.clip(R - steps_ref[entry, 0], 0, 2 * R)
+            turn = lax.rem(steps_ref[entry, 1] + rows, rows)
+            moved = field_ref[:, pl.ds(start, columns), :, :]
+            moved = pltpu.roll(moved, turn, 2)
+            cosine = cos_ref[entry]
+            sine_part = sin_ref[entry]
+            acc_real = acc_real + moved[0] * cosine - moved[1] * sine_part
+            acc_imag = acc_imag + moved[0] * sine_part + moved[1] * cosine
+        out_ref[0, i] = acc_real.astype(out_ref.dtype)
+        out_ref[1, i] = acc_imag.astype(out_ref.dtype)
+
+
+def shift_layers(offsets, box_terms, entering, before_term, rate, wave_x, wave_y, columns):
+    _, layers, boxes, width = box_terms.shape
+    layer_pos = jnp.arange(layers, dtype=jnp.float32)
+    gap = layer_pos[:, None] - layer_pos[None, :]
+    coef = jnp.where(
+        gap[:, :, None] >= 2.0, jnp.exp(-rate * jnp.maximum(gap, 0.0)[:, :, None]), 0.0
+    )[:, :, None, :]
+    lift = jnp.exp(-rate * (layer_pos + 1.0)[:, None])[:, None, :]
+    factor = jnp.exp(-rate)[None, :]
+    steps = offsets.astype(jnp.float32)
+    phase_angle = steps[:, :1] * wave_x[None] + steps[:, 1:] * wave_y[None]
+    vmem = pl.BlockSpec(memory_space=pltpu.VMEM)
+    smem = pl.BlockSpec(memory_space=pltpu.SMEM)
+    return pl.pallas_call(
+        shift_kernel,
+        out_shape=jax.ShapeDtypeStruct((2, layers, columns, BY, width), jnp.bfloat16),
+        in_specs=[smem] + [vmem] * 8,
+        out_specs=vmem,
+        scratch_shapes=[pltpu.VMEM((2, boxes // BY, BY, width), jnp.float32)],
+        cost_estimate=pl.CostEstimate(
+            flops=2 * layers * boxes * width * 40,
+            transcendentals=0,
+            bytes_accessed=box_terms.size * 4 + 3 * entering.size * 4,
+        ),
+    )(offsets, box_terms, entering, before_term, coef, lift, factor,
+      jnp.cos(phase_angle)[:, None, :], jnp.sin(phase_angle)[:, None, :])
+
+
 def body(moments, counts, m2x, x2l, decay_rate, wave_x, wave_y, offsets):
     coeffs, layers, plane_size = moments.shape
     exp_rows = m2x.shape[0]
@@ -93,45 +150,19 @@
     rate_full = jnp.broadcast_to(decay_rate, outgoing.shape)
     entering = entering_sums(outgoing, rate_full, float(layers))
 
-    layer_pos = jnp.arange(layers, dtype=jnp.float32)[None, :, None, None]
-    upward = jnp.exp(-rate * (layer_pos + 1.0)) * entering[:, None]
-    for j in range(layers - 2):
-        gap = layer_pos - float(j)
-        coeff = jnp.where(gap >= 2.0, jnp.exp(-rate * jnp.maximum(gap, 0.0)), 0.0)
-        upward = upward + coeff * box_terms[:, j : j + 1]
-    first = layer_pos == 0.0
-    upward = upward - jnp.where(first, factor * before_term[:, None].astype(jnp.float32), 0.0)
-
-    field = upward.astype(jnp.bfloat16).reshape(2, layers, ext_columns, BY, half_rows)
-    field = jnp.transpose(field, (0, 2, 3, 1, 4))
-    field = jnp.concatenate([field[:, :, BY - R :], field, field[:, :, :R]], axis=2)
-    acc_real = jnp.zeros((columns, BY, layers, half_rows), jnp.float32)
-    acc_imag = jnp.zeros((columns, BY, layers, half_rows), jnp.float32)
-    for list_entry in range(NOFF):
-        step_x = offsets[list_entry, 0]
-        step_y = offsets[list_entry, 1]
-        moved = lax.dynamic_slice(
-            field, (0, R - step_x, R - step_y, 0, 0), (2, columns, BY, layers, half_rows)
-        )
-        phase_angle = wave_x * step_x.astype(jnp.float32) + wave_y * step_y.astype(jnp.float32)
-        cosine = jnp.cos(phase_angle)
-        sine_part = jnp.sin(phase_angle)
-        part_real = moved[0].astype(jnp.float32)
-        part_imag = moved[1].astype(jnp.float32)
-        acc_real = acc_real + part_real * cosine - part_imag * sine_part
-        acc_imag = acc_imag + part_real * sine_part + part_imag * cosine
+    shifted = shift_layers(
+        offsets, box_terms, entering, before_term, decay_rate, wave_x, wave_y, columns
+    ).reshape(2, layers * plane_size, half_rows)
     local_out = None
-    for part, acc in enumerate((acc_real, acc_imag)):
-        shifted = acc.astype(jnp.bfloat16).reshape(columns * BY * layers, half_rows)
+    for part in range(2):
         product = lax.dot_general(
             x2l[:, part * half_rows : (part + 1) * half_rows],
-            shifted,
+            shifted[part],
             (((1,), (1,)), ((), ())),
             preferred_element_type=jnp.float32,
         )
         local_out = product if local_out is None else local_out + product
-    local_out = local_out.astype(jnp.bfloat16).reshape(coeffs, columns, BY, layers)
-    return jnp.transpose(local_out, (0, 3, 1, 2)).reshape(coeffs, layers, plane_size)
+    return local_out.astype(jnp.bfloat16).reshape(coeffs, layers, plane_size)
 
 
 def solution(mesh):

time: 117 us -> 109 us (0.932)
  the two profiles are of different devices: /device:TPU:1 before, /device:TPU:0 now
where the time goes in v4:
time: 109 us
  waiting for transfers between devices  30.3 us (28%)
  local copies, waits for them, and re-layouts  26.6 us (24%)
  Pallas kernels  22.4 us (21%)
  starting transfers between devices  17.6 us (16%)
  other arithmetic  7.3 us (7%)
  matrix products  4 us (4%)
    pallas_call x1, Pallas kernels, shift_layers(): pl.pallas_call(shift_kernel, out_shape=jax.ShapeDtypeStruct((2, layers, c...  22.4 us
    all_to_all x1, waiting for transfers between devices, entering_sums(): held = lax.all_to_all(spread(outgoing, 0.0), 'gz', 0, 0, tiled=True)  15.1 us
    ppermute x3, waiting for transfers between devices, from_behind(): return lax.ppermute(value, axis, pairs)  9.08 us
    all_to_all x1, starting transfers between devices, entering_sums(): held = lax.all_to_all(spread(outgoing, 0.0), 'gz', 0, 0, tiled=True)  8.9 us
    unnamed x26, local copies, waits for them, and re-layouts  8.55 us
    optimization_barrier x1, local copies, waits for them, and re-layouts, body(): outgoing, box_terms = lax.optimization_barrier((outgoing, box_terms))  7.15 us
    all_to_all x1, waiting for transfers between devices, entering_sums(): back = lax.all_to_all(sums, 'gz', 0, 0, tiled=True)  6.17 us
    all_to_all x1, starting transfers between devices, entering_sums(): back = lax.all_to_all(sums, 'gz', 0, 0, tiled=True)  4.81 us
  transfers between devices with their start and end apart: 5, of which 5 were waited for; matrix products, arithmetic and copies ran while one was open for 15% of the time, Pallas kernels for 0%

profile of v4, /device:TPU:0, one launch (start us, length us, event | category | flops | bytes accessed | tf_op | source)
XLA Modules:
  0.0 108.6 jit_solution(836499591083275759)
XLA Ops:
  0.0 1.7 %copy.18 = bf16[361,8,128]{0,2,1:T(8,128)(2,1)S(1)} copy(bf16[361,8,128]{2,1,0:T(8,128)(2,1)} %param.8) | data formatting | bytes 1478656 | tf_op args[0]
  1.7 0.7 convert_element_type.23
  2.4 0.2 multiply_convert_fusion
  2.6 3.4 %collective-permute-start = (bf16[361,8,16]{0,2,1:T(8,128)(2,1)S(1)}, bf16[361,8,16]{0,2,1:T(8,128)(2,1)S(1)}, u32[]{:S(2)}, u32[]{:S(2)}) collective-permute-start(bf16[361,8,16]{0,2,1:T(8,128)(2,1)S(1)} %get-tuple-element.20), channel_id=1, source_target_pairs={{0,1},{1,0},{2,3},{3,2},{4,5},{5,4},{6,7},{7,6},{8,9},{9,8},{10,11... | collective-permute-start | bytes 277256 | tf_op jit(solution)/shard_map/ppermute | solution.py:18
  6.0 0.3 collective-permute-start.1
  6.3 2.8 %collective-permute-done = bf16[361,8,16]{0,2,1:T(8,128)(2,1)S(1)} collective-permute-done((bf16[361,8,16]{0,2,1:T(8,128)(2,1)S(1)}, bf16[361,8,16]{0,2,1:T(8,128)(2,1)S(1)}, u32[]{:S(2)}, u32[]{:S(2)}) %collective-permute-start) | collective-permute-done | bytes 92448 | tf_op jit(solution)/shard_map/ppermute | solution.py:18
  9.1 3.0 %collective-permute-done.1 = bf16[361,8,16]{0,2,1:T(8,128)(2,1)S(1)} collective-permute-done((bf16[361,8,16]{0,2,1:T(8,128)(2,1)S(1)}, bf16[361,8,16]{0,2,1:T(8,128)(2,1)S(1)}, u32[]{:S(2)}, u32[]{:S(2)}) %collective-permute-start.1) | collective-permute-done | bytes 92448 | tf_op jit(solution)/shard_map/ppermute | solution.py:18
  12.1 1.2 %convolution_bitcast_fusion.1 = f32[1,8,160,648]{3,2,0,1:T(8,128)S(1)} fusion(bf16[1296,361]{1,0:T(8,128)(2,1)S(1)} %copy-done.2, bf16[361,8,16]{0,2,1:T(8,128)(2,1)S(1)} %collective-permute-done.1, bf16[361,8,128]{0,2,1:T(8,128)(2,1)S(1)} %multiply_convert_fusion, bf16[361,8,16]{0,2,1:T(8,128)(2,1)S(1)} %collective-permute-done), kind=kOutput, calls=%fused_computation.2 | convolution fusion | flops 601628160 | bytes 4798464 | tf_op jit(solution)/shard_map/dot_general | solution.py:138
  13.3 1.2 %convolution_bitcast_fusion = f32[1,8,160,648]{3,2,0,1:T(8,128)S(1)} fusion(bf16[1296,361]{1,0:T(8,128)(2,1)S(1)} %copy-done.2, bf16[361,8,16]{0,2,1:T(8,128)(2,1)S(1)} %collective-permute-done.1, bf16[361,8,128]{0,2,1:T(8,128)(2,1)S(1)} %multiply_convert_fusion, bf16[361,8,16]{0,2,1:T(8,128)(2,1)S(1)} %collective-permute-done), kind=kOutput, calls=%fused_computation.1 | convolution fusion | flops 601628160 | bytes 4798464 | tf_op jit(solution)/shard_map/dot_general | solution.py:138
  14.5 0.8 maximum_multiply_fusion
  15.3 3.0 %copy-done = f32[2,8,160,648]{3,2,0,1:T(8,128)} copy-done((f32[2,8,160,648]{3,2,0,1:T(8,128)}, f32[2,8,160,648]{3,2,0,1:T(8,128)S(1)}, u32[]{:S(2)}) %copy-start) | copy-done | bytes 6635544
  18.3 0.5 fusion.7
  18.9 0.9 reshape.339
  19.9 1.2 %reshape.340 = f32[64,8,512]{2,1,0:T(8,128)} reshape(f32[262144]{0:T(1024)S(1)} %pad.7) | data formatting | bytes 2097152 | tf_op jit(solution)/shard_map/reshape | solution.py:54
  21.1 8.9 %all-to-all-start = ((f32[64,8,512]{2,1,0:T(8,128)}), f32[64,8,512]{2,1,0:T(8,128)S(1)}, u32[]{:S(2)}, u32[]{:S(2)}) async-start(f32[64,8,512]{2,1,0:T(8,128)} %reshape.340), calls=%async_computation | async-start | bytes 2097152 | tf_op jit(solution)/shard_map/all_to_all | solution.py:56
  30.0 0.6 broadcast_in_dim.15.factor_ref
  30.6 0.7 copy.20.steps_ref
  31.3 0.9 reshape.342
  32.3 0.2 reshape_reshape.3
  32.5 0.2 subtract_reduce_fusion
  32.7 15.1 %all-to-all-done = f32[64,8,512]{2,1,0:T(8,128)S(1)} async-done(((f32[64,8,512]{2,1,0:T(8,128)}), f32[64,8,512]{2,1,0:T(8,128)S(1)}, u32[]{:S(2)}, u32[]{:S(2)}) %all-to-all-start) | async-done | bytes 1048608 | tf_op jit(solution)/shard_map/all_to_all | solution.py:56
  47.9 0.6 copy.31
  48.5 0.6 copy.29
  49.2 0.2 fusion
  49.4 0.2 fusion.1
  49.6 0.2 fusion.2
  49.8 0.1 fusion.3
  50.0 0.1 fusion.4
  50.4 0.6 copy.32
  51.2 1.1 %maximum_divide_fusion = f32[64,8,512]{2,1,0:T(8,128)} fusion(f32[63,8,512]{2,1,0:T(8,128)S(1)} %slice.193, f32[1,8,512]{2,1,0:T(8,128)S(1)} %concatenate.42, f32[8,512]{1,0:T(8,128)S(1)} %div.11), kind=kLoop, calls=%fused_computation.17 | loop fusion | flops 524288 | bytes 2113536 | tf_op jit(solution)/shard_map/div | solution.py:60
  52.3 4.8 %all-to-all-start.1 = ((f32[64,8,512]{2,1,0:T(8,128)}), f32[64,8,512]{2,1,0:T(8,128)S(1)}, u32[]{:S(2)}, u32[]{:S(2)}) async-start(f32[64,8,512]{2,1,0:T(8,128)} %maximum_divide_fusion), calls=%async_computation.1 | async-start | bytes 2097152 | tf_op jit(solution)/shard_map/all_to_all | solution.py:62
  57.1 1.2 %fusion.32 = (f32[6,1,648]{2,1,0:T(1,128)}, f32[6,1,648]{2,1,0:T(1,128)}) fusion(f32[648]{0:T(1024)S(1)} %copy-done.5, f32[6]{0:T(128)S(1)} %get-tuple-element.34, f32[648]{0:T(1024)S(1)} %copy-done.6, f32[6]{0:T(128)S(1)} %get-tuple-element.33), kind=kLoop, calls=%fused_computation.79 | loop fusion | flops 11664 | bytes 36336 | tf_op jit(solution)/shard_map/sin | solution.py:118
  58.4 1.3 %fusion.27 = bf16[2,160,648]{2,1,0:T(8,128)(2,1)S(1)} fusion(f32[2,8,160,648]{3,2,0,1:T(8,128)} %copy-done), kind=kLoop, calls=%fused_computation.49 | loop fusion | bytes 829440 | tf_op jit(solution)/shard_map/convert_element_type | solution.py:148
  59.6 0.3 collective-permute-start.2
  59.9 0.7 multiply_exponential_fusion.lift_ref
  60.6 1.0 broadcast_select_fusion.coef_ref
  61.6 7.2 %copy.21.terms_ref = f32[2,8,160,648]{3,2,1,0:T(8,128)} copy(f32[2,8,160,648]{3,2,0,1:T(8,128)} %copy-done) | data formatting | bytes 13271040 | tf_op jit(solution)/shard_map/optimization_barrier | solution.py:147
  68.7 6.2 %all-to-all-done.1 = f32[64,8,512]{2,1,0:T(8,128)S(1)} async-done(((f32[64,8,512]{2,1,0:T(8,128)}), f32[64,8,512]{2,1,0:T(8,128)S(1)}, u32[]{:S(2)}, u32[]{:S(2)}) %all-to-all-start.1) | async-done | bytes 1048608 | tf_op jit(solution)/shard_map/all_to_all | solution.py:62
  74.9 0.3 copy.33
  75.3 2.0 %reshape.344.entering_ref = f32[2,160,648]{2,1,0:T(8,128)} reshape(f32[207360]{0:T(1024)S(1)} %slice.189) | data formatting | bytes 1658880 | tf_op jit(solution)/shard_map/reshape | solution.py:63
  77.3 3.2 %collective-permute-done.2.before_ref = bf16[2,160,648]{2,1,0:T(8,128)(2,1)S(1)} collective-permute-done((bf16[2,160,648]{2,1,0:T(8,128)(2,1)S(1)}, bf16[2,160,648]{2,1,0:T(8,128)(2,1)S(1)}, u32[]{:S(2)}, u32[]{:S(2)}) %collective-permute-start.2) | collective-permute-done | bytes 414752 | tf_op jit(solution)/shard_map/ppermute | solution.py:18
  80.5 0.8 copy-done.3
  81.3 22.4 %shard_map.82 = bf16[2,8,16,8,648]{4,3,2,1,0:T(8,128)(2,1)} custom-call(s32[6,2]{1,0:T(8,128)} %copy.20.steps_ref, f32[2,8,160,648]{3,2,1,0:T(8,128)} %copy.21.terms_ref, f32[2,160,648]{2,1,0:T(8,128)} %reshape.344.entering_ref, bf16[2,160,648]{2,1,0:T(8,128)(2,1)} %copy-done.3, f32[8,8,1,648]{3,2,1,0:T(1,128)} %broadcast_select_fusion.coef_ref, ...), custom_call_target="tpu_custom_call" | custom-call | flops 66355200 | bytes 9123840 | tf_op jit(solution)/shard_map/pallas_call | solution.py:106
  103.7 2.2 %fusion.34 = (bf16[1,8,16,8,648]{4,3,2,1,0:T(8,128)(2,1)S(1)}, bf16[1,8,16,8,648]{4,3,2,1,0:T(8,128)(2,1)S(1)}) fusion(bf16[2,8,16,8,648]{4,3,2,1,0:T(8,128)(2,1)} %shard_map.82), kind=kLoop, calls=%fused_computation.81 | loop fusion | bytes 5308416 | tf_op jit(solution)/shard_map/slice | solution.py:160
  105.9 0.8 fusion.22
  106.7 0.8 add_convert_fusion
  107.5 0.2 copy.34
  107.7 0.9 slice.194
  (41 shorter events, 1.0 us)
Async XLA Ops:
  0.0 6.2 %copy-start.4 = (f32[648]{0:T(1024)S(1)}, f32[648]{0:T(1024)}, u32[]{:S(2)}) copy-start(f32[648]{0:T(1024)} %param.12) | copy-start | bytes 7780
  0.0 12.1 %copy-start.2 = (bf16[1296,361]{1,0:T(8,128)(2,1)S(1)}, bf16[1296,361]{1,0:T(8,128)(2,1)}, u32[]{:S(2)}) copy-start(bf16[1296,361]{1,0:T(8,128)(2,1)} %param.10) | copy-start | bytes 2807140
  2.6 6.5 %collective-permute-start = (bf16[361,8,16]{0,2,1:T(8,128)(2,1)S(1)}, bf16[361,8,16]{0,2,1:T(8,128)(2,1)S(1)}, u32[]{:S(2)}, u32[]{:S(2)}) collective-permute-start(bf16[361,8,16]{0,2,1:T(8,128)(2,1)S(1)} %get-tuple-element.20), channel_id=1, source_target_pairs={{0,1},{1,0},{2,3},{3,2},{4,5},{5,4},{6,7},{7,6},{8,9},{9,8},{10,11... | collective-permute-start | bytes 277256 | tf_op jit(solution)/shard_map/ppermute | solution.py:18
  6.0 6.1 %collective-permute-start.1 = (bf16[361,8,16]{0,2,1:T(8,128)(2,1)S(1)}, bf16[361,8,16]{0,2,1:T(8,128)(2,1)S(1)}, u32[]{:S(2)}, u32[]{:S(2)}) collective-permute-start(bf16[361,8,16]{0,2,1:T(8,128)(2,1)S(1)} %get-tuple-element.21), channel_id=1, source_target_pairs={{0,1},{1,0},{2,3},{3,2},{4,5},{5,4},{6,7},{7,6},{8,9},{9,8},{10,11... | collective-permute-start | bytes 277256 | tf_op jit(solution)/shard_map/ppermute | solution.py:18
  15.3 3.1 %copy-start = (f32[2,8,160,648]{3,2,0,1:T(8,128)}, f32[2,8,160,648]{3,2,0,1:T(8,128)S(1)}, u32[]{:S(2)}) copy-start(f32[2,8,160,648]{3,2,0,1:T(8,128)S(1)} %maximum_multiply_fusion) | copy-start | bytes 19906564
  19.8 10.7 %copy-start.7 = (s32[6,2]{0,1:T(2,128)S(1)}, s32[6,2]{0,1:T(2,128)}, u32[]{:S(2)}) copy-start(s32[6,2]{0,1:T(2,128)} %param.15) | copy-start | bytes 148
  21.1 26.7 %all-to-all-start = ((f32[64,8,512]{2,1,0:T(8,128)}), f32[64,8,512]{2,1,0:T(8,128)S(1)}, u32[]{:S(2)}, u32[]{:S(2)}) async-start(f32[64,8,512]{2,1,0:T(8,128)} %reshape.340), calls=%async_computation | async-start | bytes 2097152 | tf_op jit(solution)/shard_map/all_to_all | solution.py:56
  51.1 6.0 %copy-start.5 = (f32[648]{0:T(1024)S(1)}, f32[648]{0:T(1024)}, u32[]{:S(2)}) copy-start(f32[648]{0:T(1024)} %param.14) | copy-start | bytes 7780
  51.1 6.0 %copy-start.6 = (f32[648]{0:T(1024)S(1)}, f32[648]{0:T(1024)}, u32[]{:S(2)}) copy-start(f32[648]{0:T(1024)} %param.13) | copy-start | bytes 7780
  52.3 22.6 %all-to-all-start.1 = ((f32[64,8,512]{2,1,0:T(8,128)}), f32[64,8,512]{2,1,0:T(8,128)S(1)}, u32[]{:S(2)}, u32[]{:S(2)}) async-start(f32[64,8,512]{2,1,0:T(8,128)} %maximum_divide_fusion), calls=%async_computation.1 | async-start | bytes 2097152 | tf_op jit(solution)/shard_map/all_to_all | solution.py:62
  59.6 20.9 %collective-permute-start.2 = (bf16[2,160,648]{2,1,0:T(8,128)(2,1)S(1)}, bf16[2,160,648]{2,1,0:T(8,128)(2,1)S(1)}, u32[]{:S(2)}, u32[]{:S(2)}) collective-permute-start(bf16[2,160,648]{2,1,0:T(8,128)(2,1)S(1)} %fusion.27), channel_id=1, source_target_pairs={{0,2},{2,4},{4,6},{6,8},{8,10},{10,12},{12,14},{14,16},{16,18},{18... | collective-permute-start | bytes 1244168 | tf_op jit(solution)/shard_map/ppermute | solution.py:18
  80.5 0.8 copy-start.3
  103.7 2.2 %copy-start.1 = (bf16[361,1296]{0,1:T(8,128)(2,1)S(1)}, bf16[361,1296]{0,1:T(8,128)(2,1)}, u32[]{:S(2)}) copy-start(bf16[361,1296]{0,1:T(8,128)(2,1)} %param.11) | copy-start | bytes 2807140

commit v5 on v4

--- a/solution.py
+++ b/solution.py
@@ -63,16 +63,18 @@
     return back.reshape(-1)[:size].reshape(shape)
 
 
-def shift_kernel(steps_ref, terms_ref, entering_ref, before_ref, coef_ref, lift_ref, factor_ref,
-                 cos_ref, sin_ref, out_ref, field_ref):
+def shift_kernel(steps_ref, terms_ref, entering_ref, before_ref, factor_ref, cos_ref, sin_ref,
+                 real_ref, imag_ref, field_ref):
     _, layers, boxes, width = terms_ref.shape
-    _, _, columns, rows, _ = out_ref.shape
+    _, columns, rows, _ = real_ref.shape
+    factor = factor_ref[...]
+    state = entering_ref[...]
+    prev_term = before_ref[...].astype(jnp.float32)
     for i in range(layers):
-        up = lift_ref[i] * entering_ref[...]
-        for j in range(i - 1):
-            up = up + coef_ref[i, j] * terms_ref[:, j]
-        if i == 0:
-            up = up - factor_ref[...] * before_ref[...].astype(jnp.float32)
+        up = factor * (state - prev_term)
+        fresh = terms_ref[:, i]
+        state = factor * state + fresh
+        prev_term = fresh
         up = up.astype(jnp.bfloat16).astype(jnp.float32)
         field_ref[...] = up.reshape(2, boxes // rows, rows, width)
         acc_real = jnp.zeros((columns, rows, width), jnp.float32)
@@ -86,35 +88,30 @@
             sine_part = sin_ref[entry]
             acc_real = acc_real + moved[0] * cosine - moved[1] * sine_part
             acc_imag = acc_imag + moved[0] * sine_part + moved[1] * cosine
-        out_ref[0, i] = acc_real.astype(out_ref.dtype)
-        out_ref[1, i] = acc_imag.astype(out_ref.dtype)
+        real_ref[i] = acc_real.astype(real_ref.dtype)
+        imag_ref[i] = acc_imag.astype(imag_ref.dtype)
 
 
 def shift_layers(offsets, box_terms, entering, before_term, rate, wave_x, wave_y, columns):
     _, layers, boxes, width = box_terms.shape
-    layer_pos = jnp.arange(layers, dtype=jnp.float32)
-    gap = layer_pos[:, None] - layer_pos[None, :]
-    coef = jnp.where(
-        gap[:, :, None] >= 2.0, jnp.exp(-rate * jnp.maximum(gap, 0.0)[:, :, None]), 0.0
-    )[:, :, None, :]
-    lift = jnp.exp(-rate * (layer_pos + 1.0)[:, None])[:, None, :]
     factor = jnp.exp(-rate)[None, :]
     steps = offsets.astype(jnp.float32)
     phase_angle = steps[:, :1] * wave_x[None] + steps[:, 1:] * wave_y[None]
     vmem = pl.BlockSpec(memory_space=pltpu.VMEM)
     smem = pl.BlockSpec(memory_space=pltpu.SMEM)
+    half = jax.ShapeDtypeStruct((layers, columns, BY, width), jnp.bfloat16)
     return pl.pallas_call(
         shift_kernel,
-        out_shape=jax.ShapeDtypeStruct((2, layers, columns, BY, width), jnp.bfloat16),
-        in_specs=[smem] + [vmem] * 8,
-        out_specs=vmem,
+        out_shape=(half, half),
+        in_specs=[smem] + [vmem] * 6,
+        out_specs=(vmem, vmem),
         scratch_shapes=[pltpu.VMEM((2, boxes // BY, BY, width), jnp.float32)],
         cost_estimate=pl.CostEstimate(
-            flops=2 * layers * boxes * width * 40,
+            flops=2 * layers * boxes * width * 30,
             transcendentals=0,
             bytes_accessed=box_terms.size * 4 + 3 * entering.size * 4,
         ),
-    )(offsets, box_terms, entering, before_term, coef, lift, factor,
+    )(offsets, box_terms, entering, before_term, factor,
       jnp.cos(phase_angle)[:, None, :], jnp.sin(phase_angle)[:, None, :])
 
 
@@ -152,12 +149,12 @@
 
     shifted = shift_layers(
         offsets, box_terms, entering, before_term, decay_rate, wave_x, wave_y, columns
-    ).reshape(2, layers * plane_size, half_rows)
+    )
     local_out = None
     for part in range(2):
         product = lax.dot_general(
             x2l[:, part * half_rows : (part + 1) * half_rows],
-            shifted[part],
+            shifted[part].reshape(layers * plane_size, half_rows),
             (((1,), (1,)), ((), ())),
             preferred_element_type=jnp.float32,
         )

time: 109 us -> 107 us (0.982)
  local copies, waits for them, and re-layouts: 26.6 us -> 24.3 us
  waiting for transfers between devices: 30.3 us -> 32.2 us
  other arithmetic: 7.3 us -> 5.6 us
  matrix products: 4 us -> 5.54 us
  Pallas kernels: 22.4 us -> 21.3 us
    slice x1 -> x0, local copies, waits for them, and re-layouts: 2.18 us -> none  [body(): shifted[part]]
    dot_general x2, matrix products: 1.6 us -> 3.14 us  [body(): lax.dot_general(x2l[:, part * half_rows:(part + 1) * half_rows], shifted[...]
    all_to_all x1, waiting for transfers between devices: 15.1 us -> 16.4 us  [entering_sums(): held = lax.all_to_all(spread(outgoing, 0.0), 'gz', 0, 0, tiled=True)]
    unnamed x26 -> x28, local copies, waits for them, and re-layouts: 8.55 us -> 8.66 us
  transfers between devices with their start and end apart: 5 -> 5, of which waited for: 5 -> 5; matrix products, arithmetic and copies ran while one was open for 15% -> 14% of each run, Pallas kernels for 0% -> 0%
where the time goes in v5:
time: 107 us
  waiting for transfers between devices  32.2 us (30%)
  local copies, waits for them, and re-layouts  24.3 us (23%)
  Pallas kernels  21.3 us (20%)
  starting transfers between devices  17.7 us (17%)
  other arithmetic  5.6 us (5%)
  matrix products  5.54 us (5%)
    pallas_call x1, Pallas kernels, shift_layers(): pl.pallas_call(shift_kernel, out_shape=(half, half), in_specs=[smem] + [v...  21.3 us
    all_to_all x1, waiting for transfers between devices, entering_sums(): held = lax.all_to_all(spread(outgoing, 0.0), 'gz', 0, 0, tiled=True)  16.4 us
    ppermute x3, waiting for transfers between devices, from_behind(): return lax.ppermute(value, axis, pairs)  9.1 us
    all_to_all x1, starting transfers between devices, entering_sums(): held = lax.all_to_all(spread(outgoing, 0.0), 'gz', 0, 0, tiled=True)  8.9 us
    unnamed x28, local copies, waits for them, and re-layouts  8.66 us
    optimization_barrier x1, local copies, waits for them, and re-layouts, body(): outgoing, box_terms = lax.optimization_barrier((outgoing, box_terms))  7.05 us
    all_to_all x1, waiting for transfers between devices, entering_sums(): back = lax.all_to_all(sums, 'gz', 0, 0, tiled=True)  6.69 us
    all_to_all x1, starting transfers between devices, entering_sums(): back = lax.all_to_all(sums, 'gz', 0, 0, tiled=True)  4.94 us
  transfers between devices with their start and end apart: 5, of which 5 were waited for; matrix products, arithmetic and copies ran while one was open for 14% of the time, Pallas kernels for 0%

profile of v5, /device:TPU:0, one launch (start us, length us, event | category | flops | bytes accessed | tf_op | source)
XLA Modules:
  0.0 107.0 jit_solution(13104037597877655197)
XLA Ops:
  0.0 1.7 %copy.15 = bf16[361,8,128]{0,2,1:T(8,128)(2,1)S(1)} copy(bf16[361,8,128]{2,1,0:T(8,128)(2,1)} %param.8) | data formatting | bytes 1478656 | tf_op args[0]
  1.7 0.7 convert_element_type.23
  2.4 0.2 multiply_convert_fusion
  2.6 3.4 %collective-permute-start = (bf16[361,8,16]{0,2,1:T(8,128)(2,1)S(1)}, bf16[361,8,16]{0,2,1:T(8,128)(2,1)S(1)}, u32[]{:S(2)}, u32[]{:S(2)}) collective-permute-start(bf16[361,8,16]{0,2,1:T(8,128)(2,1)S(1)} %get-tuple-element.22), channel_id=1, source_target_pairs={{0,1},{1,0},{2,3},{3,2},{4,5},{5,4},{6,7},{7,6},{8,9},{9,8},{10,11... | collective-permute-start | bytes 277256 | tf_op jit(solution)/shard_map/ppermute | solution.py:18
  6.0 0.3 collective-permute-start.1
  6.3 2.8 %collective-permute-done = bf16[361,8,16]{0,2,1:T(8,128)(2,1)S(1)} collective-permute-done((bf16[361,8,16]{0,2,1:T(8,128)(2,1)S(1)}, bf16[361,8,16]{0,2,1:T(8,128)(2,1)S(1)}, u32[]{:S(2)}, u32[]{:S(2)}) %collective-permute-start) | collective-permute-done | bytes 92448 | tf_op jit(solution)/shard_map/ppermute | solution.py:18
  9.1 3.0 %collective-permute-done.1 = bf16[361,8,16]{0,2,1:T(8,128)(2,1)S(1)} collective-permute-done((bf16[361,8,16]{0,2,1:T(8,128)(2,1)S(1)}, bf16[361,8,16]{0,2,1:T(8,128)(2,1)S(1)}, u32[]{:S(2)}, u32[]{:S(2)}) %collective-permute-start.1) | collective-permute-done | bytes 92448 | tf_op jit(solution)/shard_map/ppermute | solution.py:18
  12.1 1.2 %convolution_bitcast_fusion.1 = f32[1,8,160,648]{3,2,0,1:T(8,128)S(1)} fusion(bf16[1296,361]{1,0:T(8,128)(2,1)S(1)} %copy-done.3, bf16[361,8,16]{0,2,1:T(8,128)(2,1)S(1)} %collective-permute-done.1, bf16[361,8,128]{0,2,1:T(8,128)(2,1)S(1)} %multiply_convert_fusion, bf16[361,8,16]{0,2,1:T(8,128)(2,1)S(1)} %collective-permute-done), kind=kOutput, calls=%fused_computation.2 | convolution fusion | flops 601628160 | bytes 4798464 | tf_op jit(solution)/shard_map/dot_general | solution.py:135
  13.3 1.2 %convolution_bitcast_fusion = f32[1,8,160,648]{3,2,0,1:T(8,128)S(1)} fusion(bf16[1296,361]{1,0:T(8,128)(2,1)S(1)} %copy-done.3, bf16[361,8,16]{0,2,1:T(8,128)(2,1)S(1)} %collective-permute-done.1, bf16[361,8,128]{0,2,1:T(8,128)(2,1)S(1)} %multiply_convert_fusion, bf16[361,8,16]{0,2,1:T(8,128)(2,1)S(1)} %collective-permute-done), kind=kOutput, calls=%fused_computation.1 | convolution fusion | flops 601628160 | bytes 4798464 | tf_op jit(solution)/shard_map/dot_general | solution.py:135
  14.5 0.8 maximum_multiply_fusion
  15.3 3.2 %copy-done = f32[2,8,160,648]{3,2,0,1:T(8,128)} copy-done((f32[2,8,160,648]{3,2,0,1:T(8,128)}, f32[2,8,160,648]{3,2,0,1:T(8,128)S(1)}, u32[]{:S(2)}) %copy-start) | copy-done | bytes 6635544
  18.5 0.5 fusion.7
  19.0 0.9 reshape.260
  19.9 0.1 pad.7
  20.0 1.1 %reshape.261 = f32[64,8,512]{2,1,0:T(8,128)} reshape(f32[262144]{0:T(1024)S(1)} %pad.7) | data formatting | bytes 2097152 | tf_op jit(solution)/shard_map/reshape | solution.py:54
  21.1 8.9 %all-to-all-start = ((f32[64,8,512]{2,1,0:T(8,128)}), f32[64,8,512]{2,1,0:T(8,128)S(1)}, u32[]{:S(2)}, u32[]{:S(2)}) async-start(f32[64,8,512]{2,1,0:T(8,128)} %reshape.261), calls=%async_computation | async-start | bytes 2097152 | tf_op jit(solution)/shard_map/all_to_all | solution.py:56
  30.1 0.9 reshape.263
  31.0 0.1 pad.8
  31.1 0.2 reshape_reshape.3
  31.3 0.2 subtract_reduce_fusion
  31.4 16.4 %all-to-all-done = f32[64,8,512]{2,1,0:T(8,128)S(1)} async-done(((f32[64,8,512]{2,1,0:T(8,128)}), f32[64,8,512]{2,1,0:T(8,128)S(1)}, u32[]{:S(2)}, u32[]{:S(2)}) %all-to-all-start) | async-done | bytes 1048608 | tf_op jit(solution)/shard_map/all_to_all | solution.py:56
  48.0 0.6 copy.20
  48.6 0.6 copy.18
  49.2 0.2 fusion
  49.4 0.2 fusion.1
  49.6 0.2 fusion.2
  49.9 0.1 fusion.3
  50.1 0.1 fusion.4
  50.3 0.1 fusion.5
  50.5 0.6 copy.21
  51.2 1.1 %maximum_divide_fusion = f32[64,8,512]{2,1,0:T(8,128)} fusion(f32[63,8,512]{2,1,0:T(8,128)S(1)} %slice.181, f32[1,8,512]{2,1,0:T(8,128)S(1)} %concatenate.42, f32[8,512]{1,0:T(8,128)S(1)} %div.11), kind=kLoop, calls=%fused_computation.17 | loop fusion | flops 524288 | bytes 2113536 | tf_op jit(solution)/shard_map/div | solution.py:60
  52.3 4.9 %all-to-all-start.1 = ((f32[64,8,512]{2,1,0:T(8,128)}), f32[64,8,512]{2,1,0:T(8,128)S(1)}, u32[]{:S(2)}, u32[]{:S(2)}) async-start(f32[64,8,512]{2,1,0:T(8,128)} %maximum_divide_fusion), calls=%async_computation.1 | async-start | bytes 2097152 | tf_op jit(solution)/shard_map/all_to_all | solution.py:62
  57.3 0.6 broadcast_in_dim.5.factor_ref
  57.9 0.7 copy.16.steps_ref
  58.5 1.3 %fusion.27 = bf16[2,160,648]{2,1,0:T(8,128)(2,1)S(1)} fusion(f32[2,8,160,648]{3,2,0,1:T(8,128)} %copy-done), kind=kLoop, calls=%fused_computation.49 | loop fusion | bytes 829440 | tf_op jit(solution)/shard_map/convert_element_type | solution.py:145
  59.8 0.3 collective-permute-start.2
  60.1 1.2 %fusion.30 = (f32[6,1,648]{2,1,0:T(1,128)}, f32[6,1,648]{2,1,0:T(1,128)}) fusion(f32[648]{0:T(1024)S(1)} %copy-done.6, f32[6]{0:T(128)S(1)} %get-tuple-element.35, f32[648]{0:T(1024)S(1)} %copy-done.7, f32[6]{0:T(128)S(1)} %get-tuple-element.34), kind=kLoop, calls=%fused_computation.73 | loop fusion | flops 11664 | bytes 36336 | tf_op jit(solution)/shard_map/sin | solution.py:115
  61.3 7.0 %copy.17.terms_ref = f32[2,8,160,648]{3,2,1,0:T(8,128)} copy(f32[2,8,160,648]{3,2,0,1:T(8,128)} %copy-done) | data formatting | bytes 13271040 | tf_op jit(solution)/shard_map/optimization_barrier | solution.py:144
  68.4 6.7 %all-to-all-done.1 = f32[64,8,512]{2,1,0:T(8,128)S(1)} async-done(((f32[64,8,512]{2,1,0:T(8,128)}), f32[64,8,512]{2,1,0:T(8,128)S(1)}, u32[]{:S(2)}, u32[]{:S(2)}) %all-to-all-start.1) | async-done | bytes 1048608 | tf_op jit(solution)/shard_map/all_to_all | solution.py:62
  75.1 0.3 copy.22
  75.4 2.0 %reshape.265.entering_ref = f32[2,160,648]{2,1,0:T(8,128)} reshape(f32[207360]{0:T(1024)S(1)} %slice.179) | data formatting | bytes 1658880 | tf_op jit(solution)/shard_map/reshape | solution.py:63
  77.4 3.3 %collective-permute-done.2.before_ref = bf16[2,160,648]{2,1,0:T(8,128)(2,1)S(1)} collective-permute-done((bf16[2,160,648]{2,1,0:T(8,128)(2,1)S(1)}, bf16[2,160,648]{2,1,0:T(8,128)(2,1)S(1)}, u32[]{:S(2)}, u32[]{:S(2)}) %collective-permute-start.2) | collective-permute-done | bytes 414752 | tf_op jit(solution)/shard_map/ppermute | solution.py:18
  80.7 0.8 copy-done.4
  81.5 21.3 %shard_map.82 = (bf16[8,16,8,648]{3,2,1,0:T(8,128)(2,1)}, bf16[8,16,8,648]{3,2,1,0:T(8,128)(2,1)}) custom-call(s32[6,2]{1,0:T(8,128)} %copy.16.steps_ref, f32[2,8,160,648]{3,2,1,0:T(8,128)} %copy.17.terms_ref, f32[2,160,648]{2,1,0:T(8,128)} %reshape.265.entering_ref, bf16[2,160,648]{2,1,0:T(8,128)(2,1)} %copy-done.4, f32[1,648]{1,0:T(1,128)} %broadcast_in_dim.5.factor_ref, ...), custom_call_target="tpu_custom_call" | custom-call | flops 49766400 | bytes 9123840 | tf_op jit(solution)/shard_map/pallas_call | solution.py:103
  102.8 2.3 %fusion.22 = f32[1024,361]{0,1:T(8,128)S(1)} fusion(bf16[1024,648]{1,0:T(8,128)(2,1)} %bitcast.125, bf16[361,1296]{0,1:T(8,128)(2,1)S(1)} %copy-done.2), kind=kOutput, calls=%fused_computation.44 | convolution fusion | flops 479084544 | bytes 3303424 | tf_op jit(solution)/shard_map/dot_general | solution.py:155
  105.1 0.8 add_convert_fusion
  105.9 0.2 copy.23
  106.1 0.9 slice.182
  (37 shorter events, 0.7 us)
Async XLA Ops:
  0.0 6.2 %copy-start.5 = (f32[648]{0:T(1024)S(1)}, f32[648]{0:T(1024)}, u32[]{:S(2)}) copy-start(f32[648]{0:T(1024)} %param.12) | copy-start | bytes 7780
  0.0 12.1 %copy-start.3 = (bf16[1296,361]{1,0:T(8,128)(2,1)S(1)}, bf16[1296,361]{1,0:T(8,128)(2,1)}, u32[]{:S(2)}) copy-start(bf16[1296,361]{1,0:T(8,128)(2,1)} %param.10) | copy-start | bytes 2807140
  2.6 6.5 %collective-permute-start = (bf16[361,8,16]{0,2,1:T(8,128)(2,1)S(1)}, bf16[361,8,16]{0,2,1:T(8,128)(2,1)S(1)}, u32[]{:S(2)}, u32[]{:S(2)}) collective-permute-start(bf16[361,8,16]{0,2,1:T(8,128)(2,1)S(1)} %get-tuple-element.22), channel_id=1, source_target_pairs={{0,1},{1,0},{2,3},{3,2},{4,5},{5,4},{6,7},{7,6},{8,9},{9,8},{10,11... | collective-permute-start | bytes 277256 | tf_op jit(solution)/shard_map/ppermute | solution.py:18
  6.0 6.1 %collective-permute-start.1 = (bf16[361,8,16]{0,2,1:T(8,128)(2,1)S(1)}, bf16[361,8,16]{0,2,1:T(8,128)(2,1)S(1)}, u32[]{:S(2)}, u32[]{:S(2)}) collective-permute-start(bf16[361,8,16]{0,2,1:T(8,128)(2,1)S(1)} %get-tuple-element.23), channel_id=1, source_target_pairs={{0,1},{1,0},{2,3},{3,2},{4,5},{5,4},{6,7},{7,6},{8,9},{9,8},{10,11... | collective-permute-start | bytes 277256 | tf_op jit(solution)/shard_map/ppermute | solution.py:18
  15.3 3.2 %copy-start = (f32[2,8,160,648]{3,2,0,1:T(8,128)}, f32[2,8,160,648]{3,2,0,1:T(8,128)S(1)}, u32[]{:S(2)}) copy-start(f32[2,8,160,648]{3,2,0,1:T(8,128)S(1)} %maximum_multiply_fusion) | copy-start | bytes 19906564
  21.1 26.7 %all-to-all-start = ((f32[64,8,512]{2,1,0:T(8,128)}), f32[64,8,512]{2,1,0:T(8,128)S(1)}, u32[]{:S(2)}, u32[]{:S(2)}) async-start(f32[64,8,512]{2,1,0:T(8,128)} %reshape.261), calls=%async_computation | async-start | bytes 2097152 | tf_op jit(solution)/shard_map/all_to_all | solution.py:56
  51.2 6.7 %copy-start.8 = (s32[6,2]{0,1:T(2,128)S(1)}, s32[6,2]{0,1:T(2,128)}, u32[]{:S(2)}) copy-start(s32[6,2]{0,1:T(2,128)} %param.15) | copy-start | bytes 148
  52.3 7.8 %copy-start.6 = (f32[648]{0:T(1024)S(1)}, f32[648]{0:T(1024)}, u32[]{:S(2)}) copy-start(f32[648]{0:T(1024)} %param.14) | copy-start | bytes 7780
  52.3 7.8 %copy-start.7 = (f32[648]{0:T(1024)S(1)}, f32[648]{0:T(1024)}, u32[]{:S(2)}) copy-start(f32[648]{0:T(1024)} %param.13) | copy-start | bytes 7780
  52.3 22.8 %all-to-all-start.1 = ((f32[64,8,512]{2,1,0:T(8,128)}), f32[64,8,512]{2,1,0:T(8,128)S(1)}, u32[]{:S(2)}, u32[]{:S(2)}) async-start(f32[64,8,512]{2,1,0:T(8,128)} %maximum_divide_fusion), calls=%async_computation.1 | async-start | bytes 2097152 | tf_op jit(solution)/shard_map/all_to_all | solution.py:62
  59.8 20.9 %collective-permute-start.2 = (bf16[2,160,648]{2,1,0:T(8,128)(2,1)S(1)}, bf16[2,160,648]{2,1,0:T(8,128)(2,1)S(1)}, u32[]{:S(2)}, u32[]{:S(2)}) collective-permute-start(bf16[2,160,648]{2,1,0:T(8,128)(2,1)S(1)} %fusion.27), channel_id=1, source_target_pairs={{0,2},{2,4},{4,6},{6,8},{8,10},{10,12},{12,14},{14,16},{16,18},{18... | collective-permute-start | bytes 1244168 | tf_op jit(solution)/shard_map/ppermute | solution.py:18
  80.7 0.8 copy-start.4
  81.5 21.3 %copy-start.2 = (bf16[361,1296]{0,1:T(8,128)(2,1)S(1)}, bf16[361,1296]{0,1:T(8,128)(2,1)}, u32[]{:S(2)}) copy-start(bf16[361,1296]{0,1:T(8,128)(2,1)} %param.11) | copy-start | bytes 2807140
  102.8 2.3 %copy-start.1 = (bf16[8,16,8,648]{3,2,1,0:T(8,128)(2,1)S(1)}, bf16[8,16,8,648]{3,2,1,0:T(8,128)(2,1)}, u32[]{:S(2)}) copy-start(bf16[8,16,8,648]{3,2,1,0:T(8,128)(2,1)} %get-tuple-element.11) | copy-start | bytes 3981316

commit v6 on v5

--- a/solution.py
+++ b/solution.py
@@ -70,6 +70,8 @@
     factor = factor_ref[...]
     state = entering_ref[...]
     prev_term = before_ref[...].astype(jnp.float32)
+    starts = [jnp.clip(R - steps_ref[entry, 0], 0, 2 * R) for entry in range(NOFF)]
+    turns = [lax.rem(steps_ref[entry, 1] + rows, rows) for entry in range(NOFF)]
     for i in range(layers):
         up = factor * (state - prev_term)
         fresh = terms_ref[:, i]
@@ -77,19 +79,22 @@
         prev_term = fresh
         up = up.astype(jnp.bfloat16).astype(jnp.float32)
         field_ref[...] = up.reshape(2, boxes // rows, rows, width)
-        acc_real = jnp.zeros((columns, rows, width), jnp.float32)
-        acc_imag = jnp.zeros((columns, rows, width), jnp.float32)
-        for entry in range(NOFF):
-            start = jnp.clip(R - steps_ref[entry, 0], 0, 2 * R)
-            turn = lax.rem(steps_ref[entry, 1] + rows, rows)
-            moved = field_ref[:, pl.ds(start, columns), :, :]
-            moved = pltpu.roll(moved, turn, 2)
-            cosine = cos_ref[entry]
-            sine_part = sin_ref[entry]
-            acc_real = acc_real + moved[0] * cosine - moved[1] * sine_part
-            acc_imag = acc_imag + moved[0] * sine_part + moved[1] * cosine
-        real_ref[i] = acc_real.astype(real_ref.dtype)
-        imag_ref[i] = acc_imag.astype(imag_ref.dtype)
+
+        def column(x, carry, i=i):
+            acc_real = jnp.zeros((rows, width), jnp.float32)
+            acc_imag = jnp.zeros((rows, width), jnp.float32)
+            for entry in range(NOFF):
+                moved = field_ref[:, starts[entry] + x, :, :]
+                moved = pltpu.roll(moved, turns[entry], 1)
+                cosine = cos_ref[entry]
+                sine_part = sin_ref[entry]
+                acc_real = acc_real + moved[0] * cosine - moved[1] * sine_part
+                acc_imag = acc_imag + moved[0] * sine_part + moved[1] * cosine
+            real_ref[i, x] = acc_real.astype(real_ref.dtype)
+            imag_ref[i, x] = acc_imag.astype(imag_ref.dtype)
+            return carry
+
+        lax.fori_loop(0, columns, column, 0)
 
 
 def shift_layers(offsets, box_terms, entering, before_term, rate, wave_x, wave_y, columns):

time: 107 us -> 102 us (0.953)
  Pallas kernels: 21.3 us -> 16.1 us
    pallas_call x1, Pallas kernels: 21.3 us -> 16.1 us  [shift_layers(): pl.pallas_call(shift_kernel, out_shape=(half, half), in_specs=[smem] + [v...]
where the time goes in v6:
time: 102 us
  waiting for transfers between devices  32.4 us (32%)
  local copies, waits for them, and re-layouts  24.3 us (24%)
  starting transfers between devices  17.7 us (17%)
  Pallas kernels  16.1 us (16%)
  other arithmetic  5.6 us (5%)
  matrix products  5.53 us (5%)
    all_to_all x1, waiting for transfers between devices, entering_sums(): held = lax.all_to_all(spread(outgoing, 0.0), 'gz', 0, 0, tiled=True)  16.4 us
    pallas_call x1, Pallas kernels, shift_layers(): pl.pallas_call(shift_kernel, out_shape=(half, half), in_specs=[smem] + [v...  16.1 us
    ppermute x3, waiting for transfers between devices, from_behind(): return lax.ppermute(value, axis, pairs)  9.1 us
    all_to_all x1, starting transfers between devices, entering_sums(): held = lax.all_to_all(spread(outgoing, 0.0), 'gz', 0, 0, tiled=True)  8.9 us
    unnamed x28, local copies, waits for them, and re-layouts  8.66 us
    optimization_barrier x1, local copies, waits for them, and re-layouts, body(): outgoing, box_terms = lax.optimization_barrier((outgoing, box_terms))  7.05 us
    all_to_all x1, waiting for transfers between devices, entering_sums(): back = lax.all_to_all(sums, 'gz', 0, 0, tiled=True)  6.87 us
    all_to_all x1, starting transfers between devices, entering_sums(): back = lax.all_to_all(sums, 'gz', 0, 0, tiled=True)  5.12 us
  transfers between devices with their start and end apart: 5, of which 5 were waited for; matrix products, arithmetic and copies ran while one was open for 14% of the time, Pallas kernels for 0%

profile of v6, /device:TPU:0, one launch (start us, length us, event | category | flops | bytes accessed | tf_op | source)
XLA Modules:
  0.0 102.0 jit_solution(15797336683229891443)
XLA Ops:
  0.0 1.7 %copy.15 = bf16[361,8,128]{0,2,1:T(8,128)(2,1)S(1)} copy(bf16[361,8,128]{2,1,0:T(8,128)(2,1)} %param.8) | data formatting | bytes 1478656 | tf_op args[0]
  1.7 0.7 convert_element_type.23
  2.4 0.2 multiply_convert_fusion
  2.6 3.4 %collective-permute-start = (bf16[361,8,16]{0,2,1:T(8,128)(2,1)S(1)}, bf16[361,8,16]{0,2,1:T(8,128)(2,1)S(1)}, u32[]{:S(2)}, u32[]{:S(2)}) collective-permute-start(bf16[361,8,16]{0,2,1:T(8,128)(2,1)S(1)} %get-tuple-element.22), channel_id=1, source_target_pairs={{0,1},{1,0},{2,3},{3,2},{4,5},{5,4},{6,7},{7,6},{8,9},{9,8},{10,11... | collective-permute-start | bytes 277256 | tf_op jit(solution)/shard_map/ppermute | solution.py:18
  6.0 0.3 collective-permute-start.1
  6.3 2.8 %collective-permute-done = bf16[361,8,16]{0,2,1:T(8,128)(2,1)S(1)} collective-permute-done((bf16[361,8,16]{0,2,1:T(8,128)(2,1)S(1)}, bf16[361,8,16]{0,2,1:T(8,128)(2,1)S(1)}, u32[]{:S(2)}, u32[]{:S(2)}) %collective-permute-start) | collective-permute-done | bytes 92448 | tf_op jit(solution)/shard_map/ppermute | solution.py:18
  9.1 3.0 %collective-permute-done.1 = bf16[361,8,16]{0,2,1:T(8,128)(2,1)S(1)} collective-permute-done((bf16[361,8,16]{0,2,1:T(8,128)(2,1)S(1)}, bf16[361,8,16]{0,2,1:T(8,128)(2,1)S(1)}, u32[]{:S(2)}, u32[]{:S(2)}) %collective-permute-start.1) | collective-permute-done | bytes 92448 | tf_op jit(solution)/shard_map/ppermute | solution.py:18
  12.1 1.2 %convolution_bitcast_fusion.1 = f32[1,8,160,648]{3,2,0,1:T(8,128)S(1)} fusion(bf16[1296,361]{1,0:T(8,128)(2,1)S(1)} %copy-done.3, bf16[361,8,16]{0,2,1:T(8,128)(2,1)S(1)} %collective-permute-done.1, bf16[361,8,128]{0,2,1:T(8,128)(2,1)S(1)} %multiply_convert_fusion, bf16[361,8,16]{0,2,1:T(8,128)(2,1)S(1)} %collective-permute-done), kind=kOutput, calls=%fused_computation.2 | convolution fusion | flops 601628160 | bytes 4798464 | tf_op jit(solution)/shard_map/dot_general | solution.py:140
  13.3 1.2 %convolution_bitcast_fusion = f32[1,8,160,648]{3,2,0,1:T(8,128)S(1)} fusion(bf16[1296,361]{1,0:T(8,128)(2,1)S(1)} %copy-done.3, bf16[361,8,16]{0,2,1:T(8,128)(2,1)S(1)} %collective-permute-done.1, bf16[361,8,128]{0,2,1:T(8,128)(2,1)S(1)} %multiply_convert_fusion, bf16[361,8,16]{0,2,1:T(8,128)(2,1)S(1)} %collective-permute-done), kind=kOutput, calls=%fused_computation.1 | convolution fusion | flops 601628160 | bytes 4798464 | tf_op jit(solution)/shard_map/dot_general | solution.py:140
  14.5 0.8 maximum_multiply_fusion
  15.3 3.2 %copy-done = f32[2,8,160,648]{3,2,0,1:T(8,128)} copy-done((f32[2,8,160,648]{3,2,0,1:T(8,128)}, f32[2,8,160,648]{3,2,0,1:T(8,128)S(1)}, u32[]{:S(2)}) %copy-start) | copy-done | bytes 6635544
  18.5 0.5 fusion.7
  19.0 0.9 reshape.260
  19.9 0.1 pad.7
  20.0 1.1 %reshape.261 = f32[64,8,512]{2,1,0:T(8,128)} reshape(f32[262144]{0:T(1024)S(1)} %pad.7) | data formatting | bytes 2097152 | tf_op jit(solution)/shard_map/reshape | solution.py:54
  21.1 8.9 %all-to-all-start = ((f32[64,8,512]{2,1,0:T(8,128)}), f32[64,8,512]{2,1,0:T(8,128)S(1)}, u32[]{:S(2)}, u32[]{:S(2)}) async-start(f32[64,8,512]{2,1,0:T(8,128)} %reshape.261), calls=%async_computation | async-start | bytes 2097152 | tf_op jit(solution)/shard_map/all_to_all | solution.py:56
  30.1 0.9 reshape.263
  31.0 0.1 pad.8
  31.1 0.2 reshape_reshape.3
  31.3 0.2 subtract_reduce_fusion
  31.4 16.4 %all-to-all-done = f32[64,8,512]{2,1,0:T(8,128)S(1)} async-done(((f32[64,8,512]{2,1,0:T(8,128)}), f32[64,8,512]{2,1,0:T(8,128)S(1)}, u32[]{:S(2)}, u32[]{:S(2)}) %all-to-all-start) | async-done | bytes 1048608 | tf_op jit(solution)/shard_map/all_to_all | solution.py:56
  48.0 0.6 copy.20
  48.6 0.6 copy.18
  49.2 0.2 fusion
  49.4 0.2 fusion.1
  49.6 0.2 fusion.2
  49.9 0.1 fusion.3
  50.1 0.1 fusion.4
  50.3 0.1 fusion.5
  50.5 0.6 copy.21
  51.2 1.1 %maximum_divide_fusion = f32[64,8,512]{2,1,0:T(8,128)} fusion(f32[63,8,512]{2,1,0:T(8,128)S(1)} %slice.181, f32[1,8,512]{2,1,0:T(8,128)S(1)} %concatenate.42, f32[8,512]{1,0:T(8,128)S(1)} %div.11), kind=kLoop, calls=%fused_computation.17 | loop fusion | flops 524288 | bytes 2113536 | tf_op jit(solution)/shard_map/div | solution.py:60
  52.3 5.1 %all-to-all-start.1 = ((f32[64,8,512]{2,1,0:T(8,128)}), f32[64,8,512]{2,1,0:T(8,128)S(1)}, u32[]{:S(2)}, u32[]{:S(2)}) async-start(f32[64,8,512]{2,1,0:T(8,128)} %maximum_divide_fusion), calls=%async_computation.1 | async-start | bytes 2097152 | tf_op jit(solution)/shard_map/all_to_all | solution.py:62
  57.4 0.6 broadcast_in_dim.5.factor_ref
  58.0 0.7 copy.16.steps_ref
  58.7 1.3 %fusion.27 = bf16[2,160,648]{2,1,0:T(8,128)(2,1)S(1)} fusion(f32[2,8,160,648]{3,2,0,1:T(8,128)} %copy-done), kind=kLoop, calls=%fused_computation.49 | loop fusion | bytes 829440 | tf_op jit(solution)/shard_map/convert_element_type | solution.py:150
  60.0 0.1 collective-permute-start.2
  60.1 1.2 %fusion.30 = (f32[6,1,648]{2,1,0:T(1,128)}, f32[6,1,648]{2,1,0:T(1,128)}) fusion(f32[648]{0:T(1024)S(1)} %copy-done.6, f32[6]{0:T(128)S(1)} %get-tuple-element.35, f32[648]{0:T(1024)S(1)} %copy-done.7, f32[6]{0:T(128)S(1)} %get-tuple-element.34), kind=kLoop, calls=%fused_computation.73 | loop fusion | flops 11664 | bytes 36336 | tf_op jit(solution)/shard_map/sin | solution.py:120
  61.3 7.0 %copy.17.terms_ref = f32[2,8,160,648]{3,2,1,0:T(8,128)} copy(f32[2,8,160,648]{3,2,0,1:T(8,128)} %copy-done) | data formatting | bytes 13271040 | tf_op jit(solution)/shard_map/optimization_barrier | solution.py:149
  68.4 6.9 %all-to-all-done.1 = f32[64,8,512]{2,1,0:T(8,128)S(1)} async-done(((f32[64,8,512]{2,1,0:T(8,128)}), f32[64,8,512]{2,1,0:T(8,128)S(1)}, u32[]{:S(2)}, u32[]{:S(2)}) %all-to-all-start.1) | async-done | bytes 1048608 | tf_op jit(solution)/shard_map/all_to_all | solution.py:62
  75.3 0.3 copy.22
  75.6 2.0 %reshape.265.entering_ref = f32[2,160,648]{2,1,0:T(8,128)} reshape(f32[207360]{0:T(1024)S(1)} %slice.179) | data formatting | bytes 1658880 | tf_op jit(solution)/shard_map/reshape | solution.py:63
  77.6 3.3 %collective-permute-done.2.before_ref = bf16[2,160,648]{2,1,0:T(8,128)(2,1)S(1)} collective-permute-done((bf16[2,160,648]{2,1,0:T(8,128)(2,1)S(1)}, bf16[2,160,648]{2,1,0:T(8,128)(2,1)S(1)}, u32[]{:S(2)}, u32[]{:S(2)}) %collective-permute-start.2) | collective-permute-done | bytes 414752 | tf_op jit(solution)/shard_map/ppermute | solution.py:18
  80.9 0.8 copy-done.4
  81.7 16.1 %shard_map.82 = (bf16[8,16,8,648]{3,2,1,0:T(8,128)(2,1)}, bf16[8,16,8,648]{3,2,1,0:T(8,128)(2,1)}) custom-call(s32[6,2]{1,0:T(8,128)} %copy.16.steps_ref, f32[2,8,160,648]{3,2,1,0:T(8,128)} %copy.17.terms_ref, f32[2,160,648]{2,1,0:T(8,128)} %reshape.265.entering_ref, bf16[2,160,648]{2,1,0:T(8,128)(2,1)} %copy-done.4, f32[1,648]{1,0:T(1,128)} %broadcast_in_dim.5.factor_ref, ...), custom_call_target="tpu_custom_call" | custom-call | flops 49766400 | bytes 9123840 | tf_op jit(solution)/shard_map/pallas_call | solution.py:108
  97.8 2.3 %fusion.22 = f32[1024,361]{0,1:T(8,128)S(1)} fusion(bf16[1024,648]{1,0:T(8,128)(2,1)} %bitcast.125, bf16[361,1296]{0,1:T(8,128)(2,1)S(1)} %copy-done.2), kind=kOutput, calls=%fused_computation.44 | convolution fusion | flops 479084544 | bytes 3303424 | tf_op jit(solution)/shard_map/dot_general | solution.py:160
  100.1 0.8 add_convert_fusion
  100.9 0.2 copy.23
  101.1 0.9 slice.182
  (37 shorter events, 0.7 us)
Async XLA Ops:
  0.0 6.2 %copy-start.5 = (f32[648]{0:T(1024)S(1)}, f32[648]{0:T(1024)}, u32[]{:S(2)}) copy-start(f32[648]{0:T(1024)} %param.12) | copy-start | bytes 7780
  0.0 12.1 %copy-start.3 = (bf16[1296,361]{1,0:T(8,128)(2,1)S(1)}, bf16[1296,361]{1,0:T(8,128)(2,1)}, u32[]{:S(2)}) copy-start(bf16[1296,361]{1,0:T(8,128)(2,1)} %param.10) | copy-start | bytes 2807140
  2.6 6.5 %collective-permute-start = (bf16[361,8,16]{0,2,1:T(8,128)(2,1)S(1)}, bf16[361,8,16]{0,2,1:T(8,128)(2,1)S(1)}, u32[]{:S(2)}, u32[]{:S(2)}) collective-permute-start(bf16[361,8,16]{0,2,1:T(8,128)(2,1)S(1)} %get-tuple-element.22), channel_id=1, source_target_pairs={{0,1},{1,0},{2,3},{3,2},{4,5},{5,4},{6,7},{7,6},{8,9},{9,8},{10,11... | collective-permute-start | bytes 277256 | tf_op jit(solution)/shard_map/ppermute | solution.py:18
  6.0 6.1 %collective-permute-start.1 = (bf16[361,8,16]{0,2,1:T(8,128)(2,1)S(1)}, bf16[361,8,16]{0,2,1:T(8,128)(2,1)S(1)}, u32[]{:S(2)}, u32[]{:S(2)}) collective-permute-start(bf16[361,8,16]{0,2,1:T(8,128)(2,1)S(1)} %get-tuple-element.23), channel_id=1, source_target_pairs={{0,1},{1,0},{2,3},{3,2},{4,5},{5,4},{6,7},{7,6},{8,9},{9,8},{10,11... | collective-permute-start | bytes 277256 | tf_op jit(solution)/shard_map/ppermute | solution.py:18
  15.3 3.2 %copy-start = (f32[2,8,160,648]{3,2,0,1:T(8,128)}, f32[2,8,160,648]{3,2,0,1:T(8,128)S(1)}, u32[]{:S(2)}) copy-start(f32[2,8,160,648]{3,2,0,1:T(8,128)S(1)} %maximum_multiply_fusion) | copy-start | bytes 19906564
  21.1 26.7 %all-to-all-start = ((f32[64,8,512]{2,1,0:T(8,128)}), f32[64,8,512]{2,1,0:T(8,128)S(1)}, u32[]{:S(2)}, u32[]{:S(2)}) async-start(f32[64,8,512]{2,1,0:T(8,128)} %reshape.261), calls=%async_computation | async-start | bytes 2097152 | tf_op jit(solution)/shard_map/all_to_all | solution.py:56
  51.2 6.9 %copy-start.8 = (s32[6,2]{0,1:T(2,128)S(1)}, s32[6,2]{0,1:T(2,128)}, u32[]{:S(2)}) copy-start(s32[6,2]{0,1:T(2,128)} %param.15) | copy-start | bytes 148
  52.3 7.8 %copy-start.6 = (f32[648]{0:T(1024)S(1)}, f32[648]{0:T(1024)}, u32[]{:S(2)}) copy-start(f32[648]{0:T(1024)} %param.14) | copy-start | bytes 7780
  52.3 7.8 %copy-start.7 = (f32[648]{0:T(1024)S(1)}, f32[648]{0:T(1024)}, u32[]{:S(2)}) copy-start(f32[648]{0:T(1024)} %param.13) | copy-start | bytes 7780
  52.3 22.9 %all-to-all-start.1 = ((f32[64,8,512]{2,1,0:T(8,128)}), f32[64,8,512]{2,1,0:T(8,128)S(1)}, u32[]{:S(2)}, u32[]{:S(2)}) async-start(f32[64,8,512]{2,1,0:T(8,128)} %maximum_divide_fusion), calls=%async_computation.1 | async-start | bytes 2097152 | tf_op jit(solution)/shard_map/all_to_all | solution.py:62
  60.0 20.9 %collective-permute-start.2 = (bf16[2,160,648]{2,1,0:T(8,128)(2,1)S(1)}, bf16[2,160,648]{2,1,0:T(8,128)(2,1)S(1)}, u32[]{:S(2)}, u32[]{:S(2)}) collective-permute-start(bf16[2,160,648]{2,1,0:T(8,128)(2,1)S(1)} %fusion.27), channel_id=1, source_target_pairs={{0,2},{2,4},{4,6},{6,8},{8,10},{10,12},{12,14},{14,16},{16,18},{18... | collective-permute-start | bytes 1244168 | tf_op jit(solution)/shard_map/ppermute | solution.py:18
  80.9 0.8 copy-start.4
  81.7 16.1 %copy-start.2 = (bf16[361,1296]{0,1:T(8,128)(2,1)S(1)}, bf16[361,1296]{0,1:T(8,128)(2,1)}, u32[]{:S(2)}) copy-start(bf16[361,1296]{0,1:T(8,128)(2,1)} %param.11) | copy-start | bytes 2807140
  97.8 2.3 %copy-start.1 = (bf16[8,16,8,648]{3,2,1,0:T(8,128)(2,1)S(1)}, bf16[8,16,8,648]{3,2,1,0:T(8,128)(2,1)}, u32[]{:S(2)}) copy-start(bf16[8,16,8,648]{3,2,1,0:T(8,128)(2,1)} %get-tuple-element.11) | copy-start | bytes 3981316

commit v7 on v6

--- a/solution.py
+++ b/solution.py
@@ -146,7 +146,6 @@
     outgoing = box_terms[:, layers - 1]
     for j in range(layers - 1):
         outgoing = outgoing + jnp.exp(-rate[0] * float(layers - 1 - j)) * box_terms[:, j]
-    outgoing, box_terms = lax.optimization_barrier((outgoing, box_terms))
     before_term = from_behind(box_terms[:, layers - 1].astype(jnp.bfloat16), "gz", 1)
 
     rate_full = jnp.broadcast_to(decay_rate, outgoing.shape)

time: 102 us -> 136 us (1.33)
  local copies, waits for them, and re-layouts: 24.3 us -> 58.5 us
  waiting for transfers between devices: 32.4 us -> 25.9 us
  other arithmetic: 5.6 us -> 9.68 us
    squeeze x0 -> x8, local copies, waits for them, and re-layouts: none -> 20.5 us  [the longest x7 17.5 us: body(): box_terms[:, j]]
    mul x0 -> x15, local copies, waits for them, and re-layouts: none -> 20.2 us  [the longest x14 13.1 us: body(): jnp.exp(-rate[0] * float(layers - 1 - j)) * box_terms[:, j]]
    optimization_barrier x1 -> x0, local copies, waits for them, and re-layouts: 7.05 us -> none  [body(): outgoing, box_terms = lax.optimization_barrier((outgoing, box_terms))]
    ppermute x3, waiting for transfers between devices: 9.1 us -> 3.23 us  [from_behind(): return lax.ppermute(value, axis, pairs)]
    add x1, other arithmetic: 0.52 us -> 4.63 us  [body(): outgoing + jnp.exp(-rate[0] * float(layers - 1 - j)) * box_terms[:, j]]
    slice x0 -> x1, local copies, waits for them, and re-layouts: none -> 2.72 us  [body(): box_terms[:, j]]
    unnamed x28 -> x32, local copies, waits for them, and re-layouts: 8.66 us -> 7.28 us
  transfers between devices with their start and end apart: 5 -> 5, of which waited for: 5 -> 3; matrix products, arithmetic and copies ran while one was open for 14% -> 21% of each run, Pallas kernels for 0% -> 0%
where the time goes in v7:
time: 136 us; the launch traced here: 135 us
  local copies, waits for them, and re-layouts  58.5 us (43%)
  waiting for transfers between devices  25.9 us (19%)
  starting transfers between devices  19 us (14%)
  Pallas kernels  16 us (12%)
  other arithmetic  9.68 us (7%)
  matrix products  5.54 us (4%)
    squeeze x7, local copies, waits for them, and re-layouts, body(): box_terms[:, j]  17.5 us
    all_to_all x1, waiting for transfers between devices, entering_sums(): held = lax.all_to_all(spread(outgoing, 0.0), 'gz', 0, 0, tiled=True)  16.2 us
    pallas_call x1, Pallas kernels, shift_layers(): pl.pallas_call(shift_kernel, out_shape=(half, half), in_specs=[smem] + [v...  16 us
    mul x14, local copies, waits for them, and re-layouts, body(): jnp.exp(-rate[0] * float(layers - 1 - j)) * box_terms[:, j]  13.1 us
    all_to_all x1, starting transfers between devices, entering_sums(): held = lax.all_to_all(spread(outgoing, 0.0), 'gz', 0, 0, tiled=True)  10.1 us
    unnamed x32, local copies, waits for them, and re-layouts  7.28 us
    mul x1, local copies, waits for them, and re-layouts, body(): box_terms = weight * jnp.stack(halves)  7.15 us
    all_to_all x1, waiting for transfers between devices, entering_sums(): back = lax.all_to_all(sums, 'gz', 0, 0, tiled=True)  6.5 us
  transfers between devices with their start and end apart: 5, of which 3 were waited for; matrix products, arithmetic and copies ran while one was open for 21% of the time, Pallas kernels for 0%

profile of v7, /device:TPU:0, one launch (start us, length us, event | category | flops | bytes accessed | tf_op | source)
XLA Modules:
  0.0 135.1 jit_solution(7170454660927917503)
XLA Ops:
  0.0 1.6 %copy.15 = bf16[361,8,128]{0,2,1:T(8,128)(2,1)S(1)} copy(bf16[361,8,128]{2,1,0:T(8,128)(2,1)} %param.8) | data formatting | bytes 1478656 | tf_op args[0]
  1.6 0.7 convert_element_type.25
  2.5 3.4 %collective-permute-start = (bf16[361,8,16]{0,2,1:T(8,128)(2,1)S(1)}, bf16[361,8,16]{0,2,1:T(8,128)(2,1)S(1)}, u32[]{:S(2)}, u32[]{:S(2)}) collective-permute-start(bf16[361,8,16]{0,2,1:T(8,128)(2,1)S(1)} %get-tuple-element.26), channel_id=1, source_target_pairs={{0,1},{1,0},{2,3},{3,2},{4,5},{5,4},{6,7},{7,6},{8,9},{9,8},{10,11... | collective-permute-start | bytes 277256 | tf_op jit(solution)/shard_map/ppermute | solution.py:18
  6.3 1.8 %mul.332 = f32[207360]{0:T(1024)} reshape(f32[2,160,648]{2,1,0:T(8,128)S(1)} %mul.331) | data formatting | bytes 1658880 | tf_op jit(solution)/shard_map/mul | solution.py:148
  8.2 1.8 %mul.304 = f32[207360]{0:T(1024)} reshape(f32[2,160,648]{2,1,0:T(8,128)S(1)} %mul.303) | data formatting | bytes 1658880 | tf_op jit(solution)/shard_map/mul | solution.py:148
  10.0 1.8 %mul.309 = f32[207360]{0:T(1024)} reshape(f32[2,160,648]{2,1,0:T(8,128)S(1)} %mul.308) | data formatting | bytes 1658880 | tf_op jit(solution)/shard_map/mul | solution.py:148
  11.9 1.8 %mul.314 = f32[207360]{0:T(1024)} reshape(f32[2,160,648]{2,1,0:T(8,128)S(1)} %mul.313) | data formatting | bytes 1658880 | tf_op jit(solution)/shard_map/mul | solution.py:148
  13.8 1.8 %mul.319 = f32[207360]{0:T(1024)} reshape(f32[2,160,648]{2,1,0:T(8,128)S(1)} %mul.318) | data formatting | bytes 1658880 | tf_op jit(solution)/shard_map/mul | solution.py:148
  15.6 1.8 %mul.324 = f32[207360]{0:T(1024)} reshape(f32[2,160,648]{2,1,0:T(8,128)S(1)} %mul.323) | data formatting | bytes 1658880 | tf_op jit(solution)/shard_map/mul | solution.py:148
  17.5 1.8 %mul.329 = f32[207360]{0:T(1024)} reshape(f32[2,160,648]{2,1,0:T(8,128)S(1)} %mul.328) | data formatting | bytes 1658880 | tf_op jit(solution)/shard_map/mul | solution.py:148
  19.3 1.2 convolution_bitcast_fusion.1
  20.5 1.2 convolution_bitcast_fusion
  21.7 0.8 maximum_multiply_fusion
  22.5 2.7 %fusion.17 = (f32[2,1,160,648]{3,2,0,1:T(8,128)}, f32[2,1,160,648]{3,2,0,1:T(8,128)S(1)}, f32[2,1,160,648]{3,2,0,1:T(8,128)S(1)}, f32[2,1,160,648]{3,2,0,1:T(8,1...) fusion(f32[2,8,160,648]{3,2,0,1:T(8,128)S(1)} %maximum_multiply, ...), kind=kLoop, calls=%fused_computation.53 | loop fusion | bytes 13271040 | tf_op jit(solution)/shard_map/slice | solution.py:148
  25.2 1.8 %copy-done = f32[2,8,160,648]{3,2,0,1:T(8,128)} copy-done((f32[2,8,160,648]{3,2,0,1:T(8,128)}, f32[2,8,160,648]{3,2,0,1:T(8,128)S(1)}, u32[]{:S(2)}) %copy-start) | copy-done | bytes 6635544
  27.1 3.0 %squeeze.27 = f32[207360]{0:T(1024)} reshape(f32[2,1,160,648]{3,2,0,1:T(8,128)} %get-tuple-element.16) | data formatting | bytes 1658880 | tf_op jit(solution)/shard_map/squeeze | solution.py:146
  30.0 3.2 %squeeze.28 = f32[207360]{0:T(1024)} reshape(f32[2,1,160,648]{3,2,0,1:T(8,128)} %get-tuple-element.9) | data formatting | bytes 1658880 | tf_op jit(solution)/shard_map/squeeze | solution.py:148
  33.2 3.0 %squeeze.29 = f32[207360]{0:T(1024)} reshape(f32[2,1,160,648]{3,2,0,1:T(8,128)} %get-tuple-element.15) | data formatting | bytes 1658880 | tf_op jit(solution)/shard_map/squeeze | solution.py:148
  36.2 3.0 %squeeze.30 = f32[207360]{0:T(1024)} reshape(f32[2,1,160,648]{3,2,0,1:T(8,128)} %get-tuple-element.14) | data formatting | bytes 1658880 | tf_op jit(solution)/shard_map/squeeze | solution.py:148
  39.2 3.0 %squeeze.31 = f32[207360]{0:T(1024)} reshape(f32[2,1,160,648]{3,2,0,1:T(8,128)} %get-tuple-element.13) | data formatting | bytes 1658880 | tf_op jit(solution)/shard_map/squeeze | solution.py:148
  42.2 1.8 %squeeze.32 = f32[207360]{0:T(1024)} reshape(f32[2,1,160,648]{3,2,0,1:T(8,128)S(1)} %get-tuple-element.12) | data formatting | bytes 1658880 | tf_op jit(solution)/shard_map/squeeze | solution.py:148
  44.0 1.8 %squeeze.33 = f32[207360]{0:T(1024)} reshape(f32[2,1,160,648]{3,2,0,1:T(8,128)S(1)} %get-tuple-element.11) | data formatting | bytes 1658880 | tf_op jit(solution)/shard_map/squeeze | solution.py:148
  45.8 1.8 %squeeze.34 = f32[207360]{0:T(1024)} reshape(f32[2,1,160,648]{3,2,0,1:T(8,128)S(1)} %get-tuple-element.10) | data formatting | bytes 1658880 | tf_op jit(solution)/shard_map/squeeze | solution.py:148
  47.6 4.6 %multiply_add_fusion = f32[207360]{0:T(1024)S(1)} fusion(f32[207360]{0:T(1024)S(1)} %copy-done.1, f32[207360]{0:T(1024)} %squeeze.34, f32[207360]{0:T(1024)} %mul.329, f32[207360]{0:T(1024)} %squeeze.33, f32[207360]{0:T(1024)} %mul.324, f32[207360]{0:T(1024)} %squeeze.32, f32[207360]{0:T(1024)} %mul.319, f32[207360]{0:T(1024)} %squeeze.31, f32[207360]{0:T(1024)} %mul.314, ...), kind=kLoop, calls=%fused_computation.19 | loop fusion | flops 2903040 | bytes 13271040 | tf_op jit(solution)/shard_map/add | solution.py:148
  52.3 1.2 reshape.273
  53.5 10.1 %all-to-all-start = ((f32[64,8,512]{2,1,0:T(8,128)}), f32[64,8,512]{2,1,0:T(8,128)S(1)}, u32[]{:S(2)}, u32[]{:S(2)}) async-start(f32[64,8,512]{2,1,0:T(8,128)} %reshape.273), calls=%async_computation | async-start | bytes 2097152 | tf_op jit(solution)/shard_map/all_to_all | solution.py:56
  63.6 0.9 reshape.275
  65.0 16.2 %all-to-all-done = f32[64,8,512]{2,1,0:T(8,128)S(1)} async-done(((f32[64,8,512]{2,1,0:T(8,128)}), f32[64,8,512]{2,1,0:T(8,128)S(1)}, u32[]{:S(2)}, u32[]{:S(2)}) %all-to-all-start) | async-done | bytes 1048608 | tf_op jit(solution)/shard_map/all_to_all | solution.py:56
  81.3 0.6 copy.20
  81.9 0.6 copy.18
  83.8 0.6 copy.21
  84.5 1.1 maximum_divide_fusion
  85.6 4.9 %all-to-all-start.1 = ((f32[64,8,512]{2,1,0:T(8,128)}), f32[64,8,512]{2,1,0:T(8,128)S(1)}, u32[]{:S(2)}, u32[]{:S(2)}) async-start(f32[64,8,512]{2,1,0:T(8,128)} %maximum_divide_fusion), calls=%async_computation.1 | async-start | bytes 2097152 | tf_op jit(solution)/shard_map/all_to_all | solution.py:62
  90.6 0.6 broadcast_in_dim.5.factor_ref
  91.2 0.7 copy.16.steps_ref
  91.9 1.3 convert_bitcast_fusion
  93.1 0.4 collective-permute-start.2
  93.5 1.2 fusion.15
  94.7 7.2 %copy.17.terms_ref = f32[2,8,160,648]{3,2,1,0:T(8,128)} copy(f32[2,8,160,648]{3,2,0,1:T(8,128)} %copy-done) | data formatting | bytes 13271040 | tf_op jit(solution)/shard_map/mul | solution.py:144
  101.9 6.5 %all-to-all-done.1 = f32[64,8,512]{2,1,0:T(8,128)S(1)} async-done(((f32[64,8,512]{2,1,0:T(8,128)}), f32[64,8,512]{2,1,0:T(8,128)S(1)}, u32[]{:S(2)}, u32[]{:S(2)}) %all-to-all-start.1) | async-done | bytes 1048608 | tf_op jit(solution)/shard_map/all_to_all | solution.py:62
  108.4 0.3 copy.22
  108.7 2.1 %reshape.277.entering_ref = f32[2,160,648]{2,1,0:T(8,128)} reshape(f32[207360]{0:T(1024)S(1)} %slice.175) | data formatting | bytes 1658880 | tf_op jit(solution)/shard_map/reshape | solution.py:63
  110.8 3.2 %collective-permute-done.2.before_ref = bf16[2,160,648]{2,1,0:T(8,128)(2,1)S(1)} collective-permute-done((bf16[2,160,648]{2,1,0:T(8,128)(2,1)S(1)}, bf16[2,160,648]{2,1,0:T(8,128)(2,1)S(1)}, u32[]{:S(2)}, u32[]{:S(2)}) %collective-permute-start.2) | collective-permute-done | bytes 414752 | tf_op jit(solution)/shard_map/ppermute | solution.py:18
  114.0 0.8 copy-done.6
  114.8 16.0 %shard_map.82 = (bf16[8,16,8,648]{3,2,1,0:T(8,128)(2,1)}, bf16[8,16,8,648]{3,2,1,0:T(8,128)(2,1)}) custom-call(s32[6,2]{1,0:T(8,128)} %copy.16.steps_ref, f32[2,8,160,648]{3,2,1,0:T(8,128)} %copy.17.terms_ref, f32[2,160,648]{2,1,0:T(8,128)} %reshape.277.entering_ref, bf16[2,160,648]{2,1,0:T(8,128)(2,1)} %copy-done.6, f32[1,648]{1,0:T(1,128)} %broadcast_in_dim.5.factor_ref, ...), custom_call_target="tpu_custom_call" | custom-call | flops 49766400 | bytes 9123840 | tf_op jit(solution)/shard_map/pallas_call | solution.py:108
  130.8 2.3 %fusion.8 = f32[1024,361]{0,1:T(8,128)S(1)} fusion(bf16[1024,648]{1,0:T(8,128)(2,1)} %bitcast.99, bf16[361,1296]{0,1:T(8,128)(2,1)S(1)} %copy-done.4), kind=kOutput, calls=%fused_computation.22 | convolution fusion | flops 479084544 | bytes 3303424 | tf_op jit(solution)/shard_map/dot_general | solution.py:159
  133.2 0.8 add_convert_fusion
  134.1 0.9 slice.177
  (63 shorter events, 3.2 us)
Async XLA Ops:
  0.0 6.2 %copy-start.7 = (f32[648]{0:T(1024)S(1)}, f32[648]{0:T(1024)}, u32[]{:S(2)}) copy-start(f32[648]{0:T(1024)} %param.12) | copy-start | bytes 7780
  2.5 16.8 %collective-permute-start = (bf16[361,8,16]{0,2,1:T(8,128)(2,1)S(1)}, bf16[361,8,16]{0,2,1:T(8,128)(2,1)S(1)}, u32[]{:S(2)}, u32[]{:S(2)}) collective-permute-start(bf16[361,8,16]{0,2,1:T(8,128)(2,1)S(1)} %get-tuple-element.26), channel_id=1, source_target_pairs={{0,1},{1,0},{2,3},{3,2},{4,5},{5,4},{6,7},{7,6},{8,9},{9,8},{10,11... | collective-permute-start | bytes 277256 | tf_op jit(solution)/shard_map/ppermute | solution.py:18
  5.9 13.4 %collective-permute-start.1 = (bf16[361,8,16]{0,2,1:T(8,128)(2,1)S(1)}, bf16[361,8,16]{0,2,1:T(8,128)(2,1)S(1)}, u32[]{:S(2)}, u32[]{:S(2)}) collective-permute-start(bf16[361,8,16]{0,2,1:T(8,128)(2,1)S(1)} %get-tuple-element.27), channel_id=1, source_target_pairs={{0,1},{1,0},{2,3},{3,2},{4,5},{5,4},{6,7},{7,6},{8,9},{9,8},{10,11... | collective-permute-start | bytes 277256 | tf_op jit(solution)/shard_map/ppermute | solution.py:18
  15.6 3.7 %copy-start.5 = (bf16[1296,361]{1,0:T(8,128)(2,1)S(1)}, bf16[1296,361]{1,0:T(8,128)(2,1)}, u32[]{:S(2)}) copy-start(bf16[1296,361]{1,0:T(8,128)(2,1)} %param.10) | copy-start | bytes 2807140
  22.5 4.6 %copy-start = (f32[2,8,160,648]{3,2,0,1:T(8,128)}, f32[2,8,160,648]{3,2,0,1:T(8,128)S(1)}, u32[]{:S(2)}) copy-start(f32[2,8,160,648]{3,2,0,1:T(8,128)S(1)} %maximum_multiply_fusion) | copy-start | bytes 19906564
  44.0 3.6 %copy-start.1 = (f32[207360]{0:T(1024)S(1)}, f32[207360]{0:T(1024)}, u32[]{:S(2)}) copy-start(f32[207360]{0:T(1024)} %mul.332) | copy-start | bytes 2488324
  45.8 1.8 %copy-start.2 = (f32[207360]{0:T(1024)S(1)}, f32[207360]{0:T(1024)}, u32[]{:S(2)}) copy-start(f32[207360]{0:T(1024)} %mul.304) | copy-start | bytes 2488324
  53.5 27.7 %all-to-all-start = ((f32[64,8,512]{2,1,0:T(8,128)}), f32[64,8,512]{2,1,0:T(8,128)S(1)}, u32[]{:S(2)}, u32[]{:S(2)}) async-start(f32[64,8,512]{2,1,0:T(8,128)} %reshape.273), calls=%async_computation | async-start | bytes 2097152 | tf_op jit(solution)/shard_map/all_to_all | solution.py:56
  84.5 6.7 %copy-start.10 = (s32[6,2]{0,1:T(2,128)S(1)}, s32[6,2]{0,1:T(2,128)}, u32[]{:S(2)}) copy-start(s32[6,2]{0,1:T(2,128)} %param.15) | copy-start | bytes 148
  85.6 7.9 %copy-start.8 = (f32[648]{0:T(1024)S(1)}, f32[648]{0:T(1024)}, u32[]{:S(2)}) copy-start(f32[648]{0:T(1024)} %param.14) | copy-start | bytes 7780
  85.6 7.9 %copy-start.9 = (f32[648]{0:T(1024)S(1)}, f32[648]{0:T(1024)}, u32[]{:S(2)}) copy-start(f32[648]{0:T(1024)} %param.13) | copy-start | bytes 7780
  85.6 22.8 %all-to-all-start.1 = ((f32[64,8,512]{2,1,0:T(8,128)}), f32[64,8,512]{2,1,0:T(8,128)S(1)}, u32[]{:S(2)}, u32[]{:S(2)}) async-start(f32[64,8,512]{2,1,0:T(8,128)} %maximum_divide_fusion), calls=%async_computation.1 | async-start | bytes 2097152 | tf_op jit(solution)/shard_map/all_to_all | solution.py:62
  93.1 20.9 %collective-permute-start.2 = (bf16[2,160,648]{2,1,0:T(8,128)(2,1)S(1)}, bf16[2,160,648]{2,1,0:T(8,128)(2,1)S(1)}, u32[]{:S(2)}, u32[]{:S(2)}) collective-permute-start(bf16[2,160,648]{2,1,0:T(8,128)(2,1)S(1)} %convert_bitcast_fusion), channel_id=1, source_target_pairs={{0,2},{2,4},{4,6},{6,8},{8,10},{10,12},{12,14},{14,16},{16,18},{18... | collective-permute-start | bytes 1244168 | tf_op jit(solution)/shard_map/ppermute | solution.py:18
  114.0 0.8 copy-start.6
  114.8 16.0 %copy-start.4 = (bf16[361,1296]{0,1:T(8,128)(2,1)S(1)}, bf16[361,1296]{0,1:T(8,128)(2,1)}, u32[]{:S(2)}) copy-start(bf16[361,1296]{0,1:T(8,128)(2,1)} %param.11) | copy-start | bytes 2807140
  130.8 2.3 %copy-start.3 = (bf16[8,16,8,648]{3,2,1,0:T(8,128)(2,1)S(1)}, bf16[8,16,8,648]{3,2,1,0:T(8,128)(2,1)}, u32[]{:S(2)}) copy-start(bf16[8,16,8,648]{3,2,1,0:T(8,128)(2,1)} %get-tuple-element.7) | copy-start | bytes 3981316

commit v8 on v6

--- a/solution.py
+++ b/solution.py
@@ -65,26 +65,31 @@
 
 def shift_kernel(steps_ref, terms_ref, entering_ref, before_ref, factor_ref, cos_ref, sin_ref,
                  real_ref, imag_ref, field_ref):
-    _, layers, boxes, width = terms_ref.shape
-    _, columns, rows, _ = real_ref.shape
+    _, layers, ext_columns, rows, width = terms_ref.shape
+    _, columns, _, _ = real_ref.shape
     factor = factor_ref[...]
-    state = entering_ref[...]
-    prev_term = before_ref[...].astype(jnp.float32)
     starts = [jnp.clip(R - steps_ref[entry, 0], 0, 2 * R) for entry in range(NOFF)]
     turns = [lax.rem(steps_ref[entry, 1] + rows, rows) for entry in range(NOFF)]
+
+    def build(c, carry):
+        state = entering_ref[:, c]
+        prev_term = before_ref[:, c].astype(jnp.float32)
+        for i in range(layers):
+            up = factor * (state - prev_term)
+            fresh = terms_ref[:, i, c]
+            state = factor * state + fresh
+            prev_term = fresh
+            field_ref[i, :, c] = up.astype(jnp.bfloat16).astype(jnp.float32)
+        return carry
+
+    lax.fori_loop(0, ext_columns, build, 0)
     for i in range(layers):
-        up = factor * (state - prev_term)
-        fresh = terms_ref[:, i]
-        state = factor * state + fresh
-        prev_term = fresh
-        up = up.astype(jnp.bfloat16).astype(jnp.float32)
-        field_ref[...] = up.reshape(2, boxes // rows, rows, width)
 
         def column(x, carry, i=i):
             acc_real = jnp.zeros((rows, width), jnp.float32)
             acc_imag = jnp.zeros((rows, width), jnp.float32)
             for entry in range(NOFF):
-                moved = field_ref[:, starts[entry] + x, :, :]
+                moved = field_ref[i, :, starts[entry] + x, :, :]
                 moved = pltpu.roll(moved, turns[entry], 1)
                 cosine = cos_ref[entry]
                 sine_part = sin_ref[entry]
@@ -110,13 +115,14 @@
         out_shape=(half, half),
         in_specs=[smem] + [vmem] * 6,
         out_specs=(vmem, vmem),
-        scratch_shapes=[pltpu.VMEM((2, boxes // BY, BY, width), jnp.float32)],
+        scratch_shapes=[pltpu.VMEM((layers, 2, boxes // BY, BY, width), jnp.float32)],
         cost_estimate=pl.CostEstimate(
             flops=2 * layers * boxes * width * 30,
             transcendentals=0,
             bytes_accessed=box_terms.size * 4 + 3 * entering.size * 4,
         ),
-    )(offsets, box_terms, entering, before_term, factor,
+    )(offsets, box_terms.reshape(2, layers, boxes // BY, BY, width),
+      entering.reshape(2, boxes // BY, BY, width), before_term.reshape(2, boxes // BY, BY, width), factor,
       jnp.cos(phase_angle)[:, None, :], jnp.sin(phase_angle)[:, None, :])
 
 

time: 102 us -> 102 us (level)
  local copies, waits for them, and re-layouts: 24.3 us -> 17.2 us
  waiting for transfers between devices: 32.4 us -> 39.4 us
    all_to_all x1, waiting for transfers between devices: 6.87 us -> 13.9 us  [entering_sums(): back = lax.all_to_all(sums, 'gz', 0, 0, tiled=True)]
    optimization_barrier x1 -> x0, local copies, waits for them, and re-layouts: 7.05 us -> none  [body(): outgoing, box_terms = lax.optimization_barrier((outgoing, box_terms))]
    another operation x0 -> x1, local copies, waits for them, and re-layouts: none -> 2.03 us  [shift_layers(): entering.reshape(2, boxes // BY, BY, width)]
    reshape x1 -> x0, local copies, waits for them, and re-layouts: 2.03 us -> none  [entering_sums(): return back.reshape(-1)[:size].reshape(shape)]
  transfers between devices with their start and end apart: 5 -> 5, of which waited for: 5 -> 5; matrix products, arithmetic and copies ran while one was open for 14% -> 7% of each run, Pallas kernels for 0% -> 0%
where the time goes in v8:
time: 102 us
  waiting for transfers between devices  39.4 us (39%)
  starting transfers between devices  17.7 us (17%)
  local copies, waits for them, and re-layouts  17.2 us (17%)
  Pallas kernels  15.6 us (15%)
  other arithmetic  5.63 us (6%)
  matrix products  5.54 us (5%)
    all_to_all x1, waiting for transfers between devices, entering_sums(): held = lax.all_to_all(spread(outgoing, 0.0), 'gz', 0, 0, tiled=True)  16.4 us
    pallas_call x1, Pallas kernels, shift_layers(): pl.pallas_call(shift_kernel, out_shape=(half, half), in_specs=[smem] + [v...  15.6 us
    all_to_all x1, waiting for transfers between devices, entering_sums(): back = lax.all_to_all(sums, 'gz', 0, 0, tiled=True)  13.9 us
    ppermute x3, waiting for transfers between devices, from_behind(): return lax.ppermute(value, axis, pairs)  9.1 us
    all_to_all x1, starting transfers between devices, entering_sums(): held = lax.all_to_all(spread(outgoing, 0.0), 'gz', 0, 0, tiled=True)  8.9 us
    unnamed x28, local copies, waits for them, and re-layouts  8.54 us
    all_to_all x1, starting transfers between devices, entering_sums(): back = lax.all_to_all(sums, 'gz', 0, 0, tiled=True)  5.12 us
    ppermute x3, starting transfers between devices, from_behind(): return lax.ppermute(value, axis, pairs)  3.73 us
  transfers between devices with their start and end apart: 5, of which 5 were waited for; matrix products, arithmetic and copies ran while one was open for 7% of the time, Pallas kernels for 0%

profile of v8, /device:TPU:0, one launch (start us, length us, event | category | flops | bytes accessed | tf_op | source)
XLA Modules:
  0.0 101.5 jit_solution(12126649129887449661)
XLA Ops:
  0.0 1.7 %copy.27 = bf16[361,8,128]{0,2,1:T(8,128)(2,1)S(1)} copy(bf16[361,8,128]{2,1,0:T(8,128)(2,1)} %param.8) | data formatting | bytes 1478656 | tf_op args[0]
  1.7 0.7 convert_element_type.23
  2.4 0.2 multiply_convert_fusion
  2.6 3.4 %collective-permute-start = (bf16[361,8,16]{0,2,1:T(8,128)(2,1)S(1)}, bf16[361,8,16]{0,2,1:T(8,128)(2,1)S(1)}, u32[]{:S(2)}, u32[]{:S(2)}) collective-permute-start(bf16[361,8,16]{0,2,1:T(8,128)(2,1)S(1)} %get-tuple-element.22), channel_id=1, source_target_pairs={{0,1},{1,0},{2,3},{3,2},{4,5},{5,4},{6,7},{7,6},{8,9},{9,8},{10,11... | collective-permute-start | bytes 277256 | tf_op jit(solution)/shard_map/ppermute | solution.py:18
  6.0 0.3 collective-permute-start.1
  6.3 2.8 %collective-permute-done = bf16[361,8,16]{0,2,1:T(8,128)(2,1)S(1)} collective-permute-done((bf16[361,8,16]{0,2,1:T(8,128)(2,1)S(1)}, bf16[361,8,16]{0,2,1:T(8,128)(2,1)S(1)}, u32[]{:S(2)}, u32[]{:S(2)}) %collective-permute-start) | collective-permute-done | bytes 92448 | tf_op jit(solution)/shard_map/ppermute | solution.py:18
  9.1 3.0 %collective-permute-done.1 = bf16[361,8,16]{0,2,1:T(8,128)(2,1)S(1)} collective-permute-done((bf16[361,8,16]{0,2,1:T(8,128)(2,1)S(1)}, bf16[361,8,16]{0,2,1:T(8,128)(2,1)S(1)}, u32[]{:S(2)}, u32[]{:S(2)}) %collective-permute-start.1) | collective-permute-done | bytes 92448 | tf_op jit(solution)/shard_map/ppermute | solution.py:18
  12.1 1.2 %convolution_bitcast_fusion.1 = f32[1,8,160,648]{3,2,1,0:T(8,128)S(1)} fusion(bf16[1296,361]{1,0:T(8,128)(2,1)S(1)} %copy-done.3, bf16[361,8,16]{0,2,1:T(8,128)(2,1)S(1)} %collective-permute-done.1, bf16[361,8,128]{0,2,1:T(8,128)(2,1)S(1)} %multiply_convert_fusion, bf16[361,8,16]{0,2,1:T(8,128)(2,1)S(1)} %collective-permute-done), kind=kOutput, calls=%fused_computation.2 | convolution fusion | flops 601628160 | bytes 4798464 | tf_op jit(solution)/shard_map/dot_general | solution.py:146
  13.3 1.2 %convolution_bitcast_fusion = f32[1,8,160,648]{3,2,1,0:T(8,128)S(1)} fusion(bf16[1296,361]{1,0:T(8,128)(2,1)S(1)} %copy-done.3, bf16[361,8,16]{0,2,1:T(8,128)(2,1)S(1)} %collective-permute-done.1, bf16[361,8,128]{0,2,1:T(8,128)(2,1)S(1)} %multiply_convert_fusion, bf16[361,8,16]{0,2,1:T(8,128)(2,1)S(1)} %collective-permute-done), kind=kOutput, calls=%fused_computation.1 | convolution fusion | flops 601628160 | bytes 4798464 | tf_op jit(solution)/shard_map/dot_general | solution.py:146
  14.5 0.8 maximum_multiply_fusion
  15.3 3.0 %copy-done = f32[2,8,160,648]{3,2,1,0:T(8,128)} copy-done((f32[2,8,160,648]{3,2,1,0:T(8,128)}, f32[2,8,160,648]{3,2,1,0:T(8,128)S(1)}, u32[]{:S(2)}) %copy-start) | copy-done | bytes 6635544
  18.3 0.5 fusion.7
  18.9 0.9 reshape.264
  19.8 0.1 pad.7
  19.8 1.2 %reshape.265 = f32[64,8,512]{2,1,0:T(8,128)} reshape(f32[262144]{0:T(1024)S(1)} %pad.7) | data formatting | bytes 2097152 | tf_op jit(solution)/shard_map/reshape | solution.py:54
  21.0 8.9 %all-to-all-start = ((f32[64,8,512]{2,1,0:T(8,128)}), f32[64,8,512]{2,1,0:T(8,128)S(1)}, u32[]{:S(2)}, u32[]{:S(2)}) async-start(f32[64,8,512]{2,1,0:T(8,128)} %reshape.265), calls=%async_computation | async-start | bytes 2097152 | tf_op jit(solution)/shard_map/all_to_all | solution.py:56
  30.0 0.9 reshape.267
  30.9 0.1 pad.8
  31.0 0.2 reshape_reshape.6
  31.2 0.2 subtract_reduce_fusion
  31.4 16.4 %all-to-all-done = f32[64,8,512]{2,1,0:T(8,128)S(1)} async-done(((f32[64,8,512]{2,1,0:T(8,128)}), f32[64,8,512]{2,1,0:T(8,128)S(1)}, u32[]{:S(2)}, u32[]{:S(2)}) %all-to-all-start) | async-done | bytes 1048608 | tf_op jit(solution)/shard_map/all_to_all | solution.py:56
  47.8 0.1 pad.28
  47.9 0.6 copy.45
  48.5 0.6 copy.43
  49.2 0.2 fusion
  49.4 0.2 fusion.1
  49.5 0.2 fusion.2
  49.8 0.1 fusion.3
  50.0 0.1 fusion.4
  50.2 0.1 fusion.5
  50.4 0.6 copy.46
  51.1 1.2 %maximum_divide_fusion = f32[64,8,512]{2,1,0:T(8,128)} fusion(f32[63,8,512]{2,1,0:T(8,128)S(1)} %slice.181, f32[1,8,512]{2,1,0:T(8,128)S(1)} %concatenate.42, f32[8,512]{1,0:T(8,128)S(1)} %div.11), kind=kLoop, calls=%fused_computation.17 | loop fusion | flops 524288 | bytes 2113536 | tf_op jit(solution)/shard_map/div | solution.py:60
  52.3 5.1 %all-to-all-start.1 = ((f32[64,8,512]{2,1,0:T(8,128)}), f32[64,8,512]{2,1,0:T(8,128)S(1)}, u32[]{:S(2)}, u32[]{:S(2)}) async-start(f32[64,8,512]{2,1,0:T(8,128)} %maximum_divide_fusion), calls=%async_computation.1 | async-start | bytes 2097152 | tf_op jit(solution)/shard_map/all_to_all | solution.py:62
  57.4 0.6 broadcast_in_dim.5.factor_ref
  58.0 0.7 copy.35.steps_ref
  58.7 1.3 %fusion.27 = bf16[2,160,648]{2,1,0:T(8,128)(2,1)S(1)} fusion(f32[2,8,160,648]{3,2,1,0:T(8,128)} %copy-done), kind=kLoop, calls=%fused_computation.49 | loop fusion | bytes 829440 | tf_op jit(solution)/shard_map/convert_element_type | solution.py:156
  60.0 0.1 collective-permute-start.2
  60.1 1.2 %fusion.30 = (f32[6,1,648]{2,1,0:T(1,128)}, f32[6,1,648]{2,1,0:T(1,128)}) fusion(f32[648]{0:T(1024)S(1)} %copy-done.6, f32[6]{0:T(128)S(1)} %get-tuple-element.35, f32[648]{0:T(1024)S(1)} %copy-done.7, f32[6]{0:T(128)S(1)} %get-tuple-element.34), kind=kLoop, calls=%fused_computation.73 | loop fusion | flops 11664 | bytes 36336 | tf_op jit(solution)/shard_map/sin | solution.py:126
  61.3 13.9 %all-to-all-done.1 = f32[64,8,512]{2,1,0:T(8,128)S(1)} async-done(((f32[64,8,512]{2,1,0:T(8,128)}), f32[64,8,512]{2,1,0:T(8,128)S(1)}, u32[]{:S(2)}, u32[]{:S(2)}) %all-to-all-start.1) | async-done | bytes 1048608 | tf_op jit(solution)/shard_map/all_to_all | solution.py:62
  75.2 0.3 copy.47
  75.6 2.0 %reshape_reshape.7.entering_ref = f32[2,20,8,648]{3,2,1,0:T(8,128)} reshape(f32[207360]{0:T(1024)S(1)} %slice.179) | data formatting | bytes 1658880 | tf_op jit(solution)/shard_map/reshape;reshape | solution.py:125
  77.6 3.3 %collective-permute-done.2 = bf16[2,160,648]{2,1,0:T(8,128)(2,1)S(1)} collective-permute-done((bf16[2,160,648]{2,1,0:T(8,128)(2,1)S(1)}, bf16[2,160,648]{2,1,0:T(8,128)(2,1)S(1)}, u32[]{:S(2)}, u32[]{:S(2)}) %collective-permute-start.2) | collective-permute-done | bytes 414752 | tf_op jit(solution)/shard_map/ppermute | solution.py:18
  80.9 0.8 copy-done.4
  81.6 15.6 %shard_map.82 = (bf16[8,16,8,648]{3,2,1,0:T(8,128)(2,1)}, bf16[8,16,8,648]{3,2,1,0:T(8,128)(2,1)}) custom-call(s32[6,2]{1,0:T(8,128)} %copy.35.steps_ref, f32[2,8,20,8,648]{4,3,2,1,0:T(8,128)} %bitcast.128, f32[2,20,8,648]{3,2,1,0:T(8,128)} %reshape_reshape.7.entering_ref, bf16[2,20,8,648]{3,2,1,0:T(8,128)(2,1)} %bitcast.143, ...), custom_call_target="tpu_custom_call" | custom-call | flops 49766400 | bytes 9123840 | tf_op jit(solution)/shard_map/pallas_call | solution.py:113
  97.3 2.3 %fusion.22 = f32[1024,361]{0,1:T(8,128)S(1)} fusion(bf16[1024,648]{1,0:T(8,128)(2,1)} %bitcast.142, bf16[361,1296]{0,1:T(8,128)(2,1)S(1)} %copy-done.2), kind=kOutput, calls=%fused_computation.44 | convolution fusion | flops 479084544 | bytes 3303424 | tf_op jit(solution)/shard_map/dot_general | solution.py:166
  99.6 0.8 add_convert_fusion
  100.4 0.2 copy.48
  100.6 0.9 slice.182
  (36 shorter events, 0.7 us)
Async XLA Ops:
  0.0 6.2 %copy-start.5 = (f32[648]{0:T(1024)S(1)}, f32[648]{0:T(1024)}, u32[]{:S(2)}) copy-start(f32[648]{0:T(1024)} %param.12) | copy-start | bytes 7780
  0.0 12.1 %copy-start.3 = (bf16[1296,361]{1,0:T(8,128)(2,1)S(1)}, bf16[1296,361]{1,0:T(8,128)(2,1)}, u32[]{:S(2)}) copy-start(bf16[1296,361]{1,0:T(8,128)(2,1)} %param.10) | copy-start | bytes 2807140
  2.6 6.5 %collective-permute-start = (bf16[361,8,16]{0,2,1:T(8,128)(2,1)S(1)}, bf16[361,8,16]{0,2,1:T(8,128)(2,1)S(1)}, u32[]{:S(2)}, u32[]{:S(2)}) collective-permute-start(bf16[361,8,16]{0,2,1:T(8,128)(2,1)S(1)} %get-tuple-element.22), channel_id=1, source_target_pairs={{0,1},{1,0},{2,3},{3,2},{4,5},{5,4},{6,7},{7,6},{8,9},{9,8},{10,11... | collective-permute-start | bytes 277256 | tf_op jit(solution)/shard_map/ppermute | solution.py:18
  6.0 6.1 %collective-permute-start.1 = (bf16[361,8,16]{0,2,1:T(8,128)(2,1)S(1)}, bf16[361,8,16]{0,2,1:T(8,128)(2,1)S(1)}, u32[]{:S(2)}, u32[]{:S(2)}) collective-permute-start(bf16[361,8,16]{0,2,1:T(8,128)(2,1)S(1)} %get-tuple-element.23), channel_id=1, source_target_pairs={{0,1},{1,0},{2,3},{3,2},{4,5},{5,4},{6,7},{7,6},{8,9},{9,8},{10,11... | collective-permute-start | bytes 277256 | tf_op jit(solution)/shard_map/ppermute | solution.py:18
  15.3 3.0 %copy-start = (f32[2,8,160,648]{3,2,1,0:T(8,128)}, f32[2,8,160,648]{3,2,1,0:T(8,128)S(1)}, u32[]{:S(2)}) copy-start(f32[2,8,160,648]{3,2,1,0:T(8,128)S(1)} %maximum_multiply_fusion) | copy-start | bytes 19906564
  21.0 26.7 %all-to-all-start = ((f32[64,8,512]{2,1,0:T(8,128)}), f32[64,8,512]{2,1,0:T(8,128)S(1)}, u32[]{:S(2)}, u32[]{:S(2)}) async-start(f32[64,8,512]{2,1,0:T(8,128)} %reshape.265), calls=%async_computation | async-start | bytes 2097152 | tf_op jit(solution)/shard_map/all_to_all | solution.py:56
  51.1 6.9 %copy-start.8 = (s32[6,2]{0,1:T(2,128)S(1)}, s32[6,2]{0,1:T(2,128)}, u32[]{:S(2)}) copy-start(s32[6,2]{0,1:T(2,128)} %param.15) | copy-start | bytes 148
  52.3 7.8 %copy-start.6 = (f32[648]{0:T(1024)S(1)}, f32[648]{0:T(1024)}, u32[]{:S(2)}) copy-start(f32[648]{0:T(1024)} %param.14) | copy-start | bytes 7780
  52.3 7.8 %copy-start.7 = (f32[648]{0:T(1024)S(1)}, f32[648]{0:T(1024)}, u32[]{:S(2)}) copy-start(f32[648]{0:T(1024)} %param.13) | copy-start | bytes 7780
  52.3 22.9 %all-to-all-start.1 = ((f32[64,8,512]{2,1,0:T(8,128)}), f32[64,8,512]{2,1,0:T(8,128)S(1)}, u32[]{:S(2)}, u32[]{:S(2)}) async-start(f32[64,8,512]{2,1,0:T(8,128)} %maximum_divide_fusion), calls=%async_computation.1 | async-start | bytes 2097152 | tf_op jit(solution)/shard_map/all_to_all | solution.py:62
  60.0 20.9 %collective-permute-start.2 = (bf16[2,160,648]{2,1,0:T(8,128)(2,1)S(1)}, bf16[2,160,648]{2,1,0:T(8,128)(2,1)S(1)}, u32[]{:S(2)}, u32[]{:S(2)}) collective-permute-start(bf16[2,160,648]{2,1,0:T(8,128)(2,1)S(1)} %fusion.27), channel_id=1, source_target_pairs={{0,2},{2,4},{4,6},{6,8},{8,10},{10,12},{12,14},{14,16},{16,18},{18... | collective-permute-start | bytes 1244168 | tf_op jit(solution)/shard_map/ppermute | solution.py:18
  80.9 0.8 copy-start.4
  81.6 15.6 %copy-start.2 = (bf16[361,1296]{0,1:T(8,128)(2,1)S(1)}, bf16[361,1296]{0,1:T(8,128)(2,1)}, u32[]{:S(2)}) copy-start(bf16[361,1296]{0,1:T(8,128)(2,1)} %param.11) | copy-start | bytes 2807140
  97.3 2.3 %copy-start.1 = (bf16[8,16,8,648]{3,2,1,0:T(8,128)(2,1)S(1)}, bf16[8,16,8,648]{3,2,1,0:T(8,128)(2,1)}, u32[]{:S(2)}) copy-start(bf16[8,16,8,648]{3,2,1,0:T(8,128)(2,1)} %get-tuple-element.11) | copy-start | bytes 3981316

commit v9 on v8

--- a/solution.py
+++ b/solution.py
@@ -99,7 +99,7 @@
             imag_ref[i, x] = acc_imag.astype(imag_ref.dtype)
             return carry
 
-        lax.fori_loop(0, columns, column, 0)
+        lax.fori_loop(0, columns, column, 0, unroll=2)
 
 
 def shift_layers(offsets, box_terms, entering, before_term, rate, wave_x, wave_y, columns):
@@ -123,7 +123,8 @@
         ),
     )(offsets, box_terms.reshape(2, layers, boxes // BY, BY, width),
       entering.reshape(2, boxes // BY, BY, width), before_term.reshape(2, boxes // BY, BY, width), factor,
-      jnp.cos(phase_angle)[:, None, :], jnp.sin(phase_angle)[:, None, :])
+      jnp.broadcast_to(jnp.cos(phase_angle)[:, None, :], (NOFF, BY, width)),
+      jnp.broadcast_to(jnp.sin(phase_angle)[:, None, :], (NOFF, BY, width)))
 
 
 def body(moments, counts, m2x, x2l, decay_rate, wave_x, wave_y, offsets):

time: 102 us -> 102 us (level)
  waiting for transfers between devices: 39.4 us -> 40.5 us
  other arithmetic: 5.63 us -> 4.59 us
    broadcast_in_dim x0 -> x2, local copies, waits for them, and re-layouts: none -> 1.4 us  [the longest x1 0.72 us: shift_layers(): jnp.broadcast_to(jnp.cos(phase_angle)[:, None, :], (NOFF, BY, width))]
    all_to_all x1, waiting for transfers between devices: 13.9 us -> 15 us  [entering_sums(): back = lax.all_to_all(sums, 'gz', 0, 0, tiled=True)]
    sin x1, other arithmetic: 1.21 us -> 0.17 us  [shift_layers(): jnp.sin(phase_angle)[:, None, :]]
  transfers between devices with their start and end apart: 5 -> 5, of which waited for: 5 -> 5; matrix products, arithmetic and copies ran while one was open for 7% -> 6% of each run, Pallas kernels for 0% -> 0%
where the time goes in v9:
time: 102 us
  waiting for transfers between devices  40.5 us (40%)
  local copies, waits for them, and re-layouts  17.8 us (17%)
  starting transfers between devices  17.7 us (17%)
  Pallas kernels  15.1 us (15%)
  matrix products  5.54 us (5%)
  other arithmetic  4.59 us (4%)
    all_to_all x1, waiting for transfers between devices, entering_sums(): held = lax.all_to_all(spread(outgoing, 0.0), 'gz', 0, 0, tiled=True)  16.4 us
    pallas_call x1, Pallas kernels, shift_layers(): pl.pallas_call(shift_kernel, out_shape=(half, half), in_specs=[smem] + [v...  15.1 us
    all_to_all x1, waiting for transfers between devices, entering_sums(): back = lax.all_to_all(sums, 'gz', 0, 0, tiled=True)  15 us
    ppermute x3, waiting for transfers between devices, from_behind(): return lax.ppermute(value, axis, pairs)  9.1 us
    all_to_all x1, starting transfers between devices, entering_sums(): held = lax.all_to_all(spread(outgoing, 0.0), 'gz', 0, 0, tiled=True)  8.9 us
    unnamed x28, local copies, waits for them, and re-layouts  7.76 us
    all_to_all x1, starting transfers between devices, entering_sums(): back = lax.all_to_all(sums, 'gz', 0, 0, tiled=True)  5.12 us
    ppermute x3, starting transfers between devices, from_behind(): return lax.ppermute(value, axis, pairs)  3.73 us
  transfers between devices with their start and end apart: 5, of which 5 were waited for; matrix products, arithmetic and copies ran while one was open for 6% of the time, Pallas kernels for 0%

profile of v9, /device:TPU:0, one launch (start us, length us, event | category | flops | bytes accessed | tf_op | source)
XLA Modules:
  0.0 101.6 jit_solution(11569705558212355945)
XLA Ops:
  0.0 1.7 %copy.27 = bf16[361,8,128]{0,2,1:T(8,128)(2,1)S(1)} copy(bf16[361,8,128]{2,1,0:T(8,128)(2,1)} %param.8) | data formatting | bytes 1478656 | tf_op args[0]
  1.7 0.7 convert_element_type.23
  2.4 0.2 multiply_convert_fusion
  2.6 3.4 %collective-permute-start = (bf16[361,8,16]{0,2,1:T(8,128)(2,1)S(1)}, bf16[361,8,16]{0,2,1:T(8,128)(2,1)S(1)}, u32[]{:S(2)}, u32[]{:S(2)}) collective-permute-start(bf16[361,8,16]{0,2,1:T(8,128)(2,1)S(1)} %get-tuple-element.22), channel_id=1, source_target_pairs={{0,1},{1,0},{2,3},{3,2},{4,5},{5,4},{6,7},{7,6},{8,9},{9,8},{10,11... | collective-permute-start | bytes 277256 | tf_op jit(solution)/shard_map/ppermute | solution.py:18
  6.0 0.3 collective-permute-start.1
  6.3 2.8 %collective-permute-done = bf16[361,8,16]{0,2,1:T(8,128)(2,1)S(1)} collective-permute-done((bf16[361,8,16]{0,2,1:T(8,128)(2,1)S(1)}, bf16[361,8,16]{0,2,1:T(8,128)(2,1)S(1)}, u32[]{:S(2)}, u32[]{:S(2)}) %collective-permute-start) | collective-permute-done | bytes 92448 | tf_op jit(solution)/shard_map/ppermute | solution.py:18
  9.1 3.0 %collective-permute-done.1 = bf16[361,8,16]{0,2,1:T(8,128)(2,1)S(1)} collective-permute-done((bf16[361,8,16]{0,2,1:T(8,128)(2,1)S(1)}, bf16[361,8,16]{0,2,1:T(8,128)(2,1)S(1)}, u32[]{:S(2)}, u32[]{:S(2)}) %collective-permute-start.1) | collective-permute-done | bytes 92448 | tf_op jit(solution)/shard_map/ppermute | solution.py:18
  12.1 1.2 %convolution_bitcast_fusion.1 = f32[1,8,160,648]{3,2,1,0:T(8,128)S(1)} fusion(bf16[1296,361]{1,0:T(8,128)(2,1)S(1)} %copy-done.3, bf16[361,8,16]{0,2,1:T(8,128)(2,1)S(1)} %collective-permute-done.1, bf16[361,8,128]{0,2,1:T(8,128)(2,1)S(1)} %multiply_convert_fusion, bf16[361,8,16]{0,2,1:T(8,128)(2,1)S(1)} %collective-permute-done), kind=kOutput, calls=%fused_computation.2 | convolution fusion | flops 601628160 | bytes 4798464 | tf_op jit(solution)/shard_map/dot_general | solution.py:147
  13.3 1.2 %convolution_bitcast_fusion = f32[1,8,160,648]{3,2,1,0:T(8,128)S(1)} fusion(bf16[1296,361]{1,0:T(8,128)(2,1)S(1)} %copy-done.3, bf16[361,8,16]{0,2,1:T(8,128)(2,1)S(1)} %collective-permute-done.1, bf16[361,8,128]{0,2,1:T(8,128)(2,1)S(1)} %multiply_convert_fusion, bf16[361,8,16]{0,2,1:T(8,128)(2,1)S(1)} %collective-permute-done), kind=kOutput, calls=%fused_computation.1 | convolution fusion | flops 601628160 | bytes 4798464 | tf_op jit(solution)/shard_map/dot_general | solution.py:147
  14.5 0.8 maximum_multiply_fusion
  15.3 3.0 %copy-done = f32[2,8,160,648]{3,2,1,0:T(8,128)} copy-done((f32[2,8,160,648]{3,2,1,0:T(8,128)}, f32[2,8,160,648]{3,2,1,0:T(8,128)S(1)}, u32[]{:S(2)}) %copy-start) | copy-done | bytes 6635544
  18.3 0.5 fusion.7
  18.9 0.9 reshape.178
  19.8 0.1 pad.7
  19.8 1.2 %reshape.179 = f32[64,8,512]{2,1,0:T(8,128)} reshape(f32[262144]{0:T(1024)S(1)} %pad.7) | data formatting | bytes 2097152 | tf_op jit(solution)/shard_map/reshape | solution.py:54
  21.0 8.9 %all-to-all-start = ((f32[64,8,512]{2,1,0:T(8,128)}), f32[64,8,512]{2,1,0:T(8,128)S(1)}, u32[]{:S(2)}, u32[]{:S(2)}) async-start(f32[64,8,512]{2,1,0:T(8,128)} %reshape.179), calls=%async_computation | async-start | bytes 2097152 | tf_op jit(solution)/shard_map/all_to_all | solution.py:56
  30.0 0.9 reshape.181
  30.9 0.1 pad.8
  31.0 0.2 reshape_reshape.6
  31.2 0.2 subtract_reduce_fusion
  31.4 16.4 %all-to-all-done = f32[64,8,512]{2,1,0:T(8,128)S(1)} async-done(((f32[64,8,512]{2,1,0:T(8,128)}), f32[64,8,512]{2,1,0:T(8,128)S(1)}, u32[]{:S(2)}, u32[]{:S(2)}) %all-to-all-start) | async-done | bytes 1048608 | tf_op jit(solution)/shard_map/all_to_all | solution.py:56
  47.9 0.6 copy.45
  48.5 0.6 copy.43
  49.2 0.2 fusion
  49.4 0.2 fusion.1
  49.5 0.2 fusion.2
  49.8 0.1 fusion.3
  50.0 0.1 fusion.4
  50.2 0.1 fusion.5
  50.4 0.6 copy.46
  51.1 1.2 %maximum_divide_fusion = f32[64,8,512]{2,1,0:T(8,128)} fusion(f32[63,8,512]{2,1,0:T(8,128)S(1)} %slice.175, f32[1,8,512]{2,1,0:T(8,128)S(1)} %concatenate.42, f32[8,512]{1,0:T(8,128)S(1)} %div.11), kind=kLoop, calls=%fused_computation.17 | loop fusion | flops 524288 | bytes 2113536 | tf_op jit(solution)/shard_map/div | solution.py:60
  52.3 5.1 %all-to-all-start.1 = ((f32[64,8,512]{2,1,0:T(8,128)}), f32[64,8,512]{2,1,0:T(8,128)S(1)}, u32[]{:S(2)}, u32[]{:S(2)}) async-start(f32[64,8,512]{2,1,0:T(8,128)} %maximum_divide_fusion), calls=%async_computation.1 | async-start | bytes 2097152 | tf_op jit(solution)/shard_map/all_to_all | solution.py:62
  57.4 0.6 broadcast_in_dim.9.factor_ref
  58.0 0.7 copy.35.steps_ref
  58.7 1.3 %fusion.27 = bf16[2,160,648]{2,1,0:T(8,128)(2,1)S(1)} fusion(f32[2,8,160,648]{3,2,1,0:T(8,128)} %copy-done), kind=kLoop, calls=%fused_computation.49 | loop fusion | bytes 829440 | tf_op jit(solution)/shard_map/convert_element_type | solution.py:157
  60.0 0.1 collective-permute-start.2
  60.1 0.2 fusion.28
  60.3 15.0 %all-to-all-done.1 = f32[64,8,512]{2,1,0:T(8,128)S(1)} async-done(((f32[64,8,512]{2,1,0:T(8,128)}), f32[64,8,512]{2,1,0:T(8,128)S(1)}, u32[]{:S(2)}, u32[]{:S(2)}) %all-to-all-start.1) | async-done | bytes 1048608 | tf_op jit(solution)/shard_map/all_to_all | solution.py:62
  75.2 0.3 copy.47
  75.6 2.0 %reshape_reshape.7.entering_ref = f32[2,20,8,648]{3,2,1,0:T(8,128)} reshape(f32[207360]{0:T(1024)S(1)} %slice.173) | data formatting | bytes 1658880 | tf_op jit(solution)/shard_map/reshape;reshape | solution.py:125
  77.6 3.3 %collective-permute-done.2 = bf16[2,160,648]{2,1,0:T(8,128)(2,1)S(1)} collective-permute-done((bf16[2,160,648]{2,1,0:T(8,128)(2,1)S(1)}, bf16[2,160,648]{2,1,0:T(8,128)(2,1)S(1)}, u32[]{:S(2)}, u32[]{:S(2)}) %collective-permute-start.2) | collective-permute-done | bytes 414752 | tf_op jit(solution)/shard_map/ppermute | solution.py:18
  80.9 0.7 broadcast_in_dim.10.cos_ref
  81.6 0.7 broadcast_in_dim.11.sin_ref
  82.3 15.1 %shard_map.82 = (bf16[8,16,8,648]{3,2,1,0:T(8,128)(2,1)}, bf16[8,16,8,648]{3,2,1,0:T(8,128)(2,1)}) custom-call(s32[6,2]{1,0:T(8,128)} %copy.35.steps_ref, f32[2,8,20,8,648]{4,3,2,1,0:T(8,128)} %bitcast.128, f32[2,20,8,648]{3,2,1,0:T(8,128)} %reshape_reshape.7.entering_ref, bf16[2,20,8,648]{3,2,1,0:T(8,128)(2,1)} %bitcast.143, ...), custom_call_target="tpu_custom_call" | custom-call | flops 49766400 | bytes 9123840 | tf_op jit(solution)/shard_map/pallas_call | solution.py:113
  97.4 2.3 %fusion.22 = f32[1024,361]{0,1:T(8,128)S(1)} fusion(bf16[1024,648]{1,0:T(8,128)(2,1)} %bitcast.142, bf16[361,1296]{0,1:T(8,128)(2,1)S(1)} %copy-done.2), kind=kOutput, calls=%fused_computation.44 | convolution fusion | flops 479084544 | bytes 3303424 | tf_op jit(solution)/shard_map/dot_general | solution.py:167
  99.7 0.8 add_convert_fusion
  100.5 0.2 copy.48
  100.7 0.9 slice.176
  (38 shorter events, 0.7 us)
Async XLA Ops:
  0.0 6.2 %copy-start.5 = (f32[648]{0:T(1024)S(1)}, f32[648]{0:T(1024)}, u32[]{:S(2)}) copy-start(f32[648]{0:T(1024)} %param.12) | copy-start | bytes 7780
  0.0 12.1 %copy-start.3 = (bf16[1296,361]{1,0:T(8,128)(2,1)S(1)}, bf16[1296,361]{1,0:T(8,128)(2,1)}, u32[]{:S(2)}) copy-start(bf16[1296,361]{1,0:T(8,128)(2,1)} %param.10) | copy-start | bytes 2807140
  2.6 6.5 %collective-permute-start = (bf16[361,8,16]{0,2,1:T(8,128)(2,1)S(1)}, bf16[361,8,16]{0,2,1:T(8,128)(2,1)S(1)}, u32[]{:S(2)}, u32[]{:S(2)}) collective-permute-start(bf16[361,8,16]{0,2,1:T(8,128)(2,1)S(1)} %get-tuple-element.22), channel_id=1, source_target_pairs={{0,1},{1,0},{2,3},{3,2},{4,5},{5,4},{6,7},{7,6},{8,9},{9,8},{10,11... | collective-permute-start | bytes 277256 | tf_op jit(solution)/shard_map/ppermute | solution.py:18
  6.0 6.1 %collective-permute-start.1 = (bf16[361,8,16]{0,2,1:T(8,128)(2,1)S(1)}, bf16[361,8,16]{0,2,1:T(8,128)(2,1)S(1)}, u32[]{:S(2)}, u32[]{:S(2)}) collective-permute-start(bf16[361,8,16]{0,2,1:T(8,128)(2,1)S(1)} %get-tuple-element.23), channel_id=1, source_target_pairs={{0,1},{1,0},{2,3},{3,2},{4,5},{5,4},{6,7},{7,6},{8,9},{9,8},{10,11... | collective-permute-start | bytes 277256 | tf_op jit(solution)/shard_map/ppermute | solution.py:18
  15.3 3.0 %copy-start = (f32[2,8,160,648]{3,2,1,0:T(8,128)}, f32[2,8,160,648]{3,2,1,0:T(8,128)S(1)}, u32[]{:S(2)}) copy-start(f32[2,8,160,648]{3,2,1,0:T(8,128)S(1)} %maximum_multiply_fusion) | copy-start | bytes 19906564
  21.0 26.7 %all-to-all-start = ((f32[64,8,512]{2,1,0:T(8,128)}), f32[64,8,512]{2,1,0:T(8,128)S(1)}, u32[]{:S(2)}, u32[]{:S(2)}) async-start(f32[64,8,512]{2,1,0:T(8,128)} %reshape.179), calls=%async_computation | async-start | bytes 2097152 | tf_op jit(solution)/shard_map/all_to_all | solution.py:56
  51.1 6.9 %copy-start.8 = (s32[6,2]{0,1:T(2,128)S(1)}, s32[6,2]{0,1:T(2,128)}, u32[]{:S(2)}) copy-start(s32[6,2]{0,1:T(2,128)} %param.15) | copy-start | bytes 148
  52.3 7.8 %copy-start.6 = (f32[648]{0:T(1024)S(1)}, f32[648]{0:T(1024)}, u32[]{:S(2)}) copy-start(f32[648]{0:T(1024)} %param.14) | copy-start | bytes 7780
  52.3 7.8 %copy-start.7 = (f32[648]{0:T(1024)S(1)}, f32[648]{0:T(1024)}, u32[]{:S(2)}) copy-start(f32[648]{0:T(1024)} %param.13) | copy-start | bytes 7780
  52.3 22.9 %all-to-all-start.1 = ((f32[64,8,512]{2,1,0:T(8,128)}), f32[64,8,512]{2,1,0:T(8,128)S(1)}, u32[]{:S(2)}, u32[]{:S(2)}) async-start(f32[64,8,512]{2,1,0:T(8,128)} %maximum_divide_fusion), calls=%async_computation.1 | async-start | bytes 2097152 | tf_op jit(solution)/shard_map/all_to_all | solution.py:62
  60.0 20.9 %collective-permute-start.2 = (bf16[2,160,648]{2,1,0:T(8,128)(2,1)S(1)}, bf16[2,160,648]{2,1,0:T(8,128)(2,1)S(1)}, u32[]{:S(2)}, u32[]{:S(2)}) collective-permute-start(bf16[2,160,648]{2,1,0:T(8,128)(2,1)S(1)} %fusion.27), channel_id=1, source_target_pairs={{0,2},{2,4},{4,6},{6,8},{8,10},{10,12},{12,14},{14,16},{16,18},{18... | collective-permute-start | bytes 1244168 | tf_op jit(solution)/shard_map/ppermute | solution.py:18
  80.9 1.4 %copy-start.4 = (bf16[2,160,648]{2,1,0:T(8,128)(2,1)}, bf16[2,160,648]{2,1,0:T(8,128)(2,1)S(1)}, u32[]{:S(2)}) copy-start(bf16[2,160,648]{2,1,0:T(8,128)(2,1)S(1)} %collective-permute-done.2) | copy-start | bytes 1244164
  82.3 15.1 %copy-start.2 = (bf16[361,1296]{0,1:T(8,128)(2,1)S(1)}, bf16[361,1296]{0,1:T(8,128)(2,1)}, u32[]{:S(2)}) copy-start(bf16[361,1296]{0,1:T(8,128)(2,1)} %param.11) | copy-start | bytes 2807140
  97.4 2.3 %copy-start.1 = (bf16[8,16,8,648]{3,2,1,0:T(8,128)(2,1)S(1)}, bf16[8,16,8,648]{3,2,1,0:T(8,128)(2,1)}, u32[]{:S(2)}) copy-start(bf16[8,16,8,648]{3,2,1,0:T(8,128)(2,1)} %get-tuple-element.11) | copy-start | bytes 3981316

commit v10 on v9

--- a/solution.py
+++ b/solution.py
@@ -19,8 +19,15 @@
 
 
 def with_halo(block, axis, dim, width):
-    low = from_behind(lax.slice_in_dim(block, block.shape[dim] - width, None, axis=dim), axis, 1)
-    high = from_behind(lax.slice_in_dim(block, 0, width, axis=dim), axis, -1)
+    tail = lax.slice_in_dim(block, block.shape[dim] - width, None, axis=dim)
+    head = lax.slice_in_dim(block, 0, width, axis=dim)
+    if lax.axis_size(axis) == 2:
+        both = from_behind(jnp.concatenate([tail, head], axis=dim), axis, 1)
+        low = lax.slice_in_dim(both, 0, width, axis=dim)
+        high = lax.slice_in_dim(both, width, None, axis=dim)
+    else:
+        low = from_behind(tail, axis, 1)
+        high = from_behind(head, axis, -1)
     return jnp.concatenate([low, block, high], axis=dim)
 
 

time: 102 us -> 102 us (level)
    ppermute x3 -> x2, waiting for transfers between devices: 9.1 us -> 8.14 us  [from_behind(): return lax.ppermute(value, axis, pairs)]
    ppermute x3 -> x2, starting transfers between devices: 3.73 us -> 3.45 us  [from_behind(): return lax.ppermute(value, axis, pairs)]
  transfers between devices with their start and end apart: 5 -> 4, of which waited for: 5 -> 4; matrix products, arithmetic and copies ran while one was open for 6% -> 6% of each run, Pallas kernels for 0% -> 0%
where the time goes in v10:
time: 102 us; the launch traced here: 101 us
  waiting for transfers between devices  39.5 us (39%)
  starting transfers between devices  18.3 us (18%)
  local copies, waits for them, and re-layouts  17.9 us (18%)
  Pallas kernels  15 us (15%)
  matrix products  5.54 us (5%)
  other arithmetic  4.62 us (5%)
    all_to_all x1, waiting for transfers between devices, entering_sums(): held = lax.all_to_all(spread(outgoing, 0.0), 'gz', 0, 0, tiled=True)  16.4 us
    pallas_call x1, Pallas kernels, shift_layers(): pl.pallas_call(shift_kernel, out_shape=(half, half), in_specs=[smem] + [v...  15 us
    all_to_all x1, waiting for transfers between devices, entering_sums(): back = lax.all_to_all(sums, 'gz', 0, 0, tiled=True)  15 us
    all_to_all x1, starting transfers between devices, entering_sums(): held = lax.all_to_all(spread(outgoing, 0.0), 'gz', 0, 0, tiled=True)  9.84 us
    ppermute x2, waiting for transfers between devices, from_behind(): return lax.ppermute(value, axis, pairs)  8.14 us
    unnamed x28, local copies, waits for them, and re-layouts  7.76 us
    all_to_all x1, starting transfers between devices, entering_sums(): back = lax.all_to_all(sums, 'gz', 0, 0, tiled=True)  4.96 us
    ppermute x2, starting transfers between devices, from_behind(): return lax.ppermute(value, axis, pairs)  3.45 us
  transfers between devices with their start and end apart: 4, of which 4 were waited for; matrix products, arithmetic and copies ran while one was open for 6% of the time, Pallas kernels for 0%

profile of v10, /device:TPU:0, one launch (start us, length us, event | category | flops | bytes accessed | tf_op | source)
XLA Modules:
  0.0 101.2 jit_solution(12578212630247462262)
XLA Ops:
  0.0 1.7 %copy.27 = bf16[361,8,128]{0,2,1:T(8,128)(2,1)S(1)} copy(bf16[361,8,128]{2,1,0:T(8,128)(2,1)} %param.8) | data formatting | bytes 1478656 | tf_op args[0]
  1.7 0.7 convert_element_type.23
  2.4 0.2 multiply_convert_fusion
  2.7 3.4 %collective-permute-start = (bf16[361,8,32]{0,2,1:T(8,128)(2,1)S(1)}, bf16[361,8,32]{0,2,1:T(8,128)(2,1)S(1)}, u32[]{:S(2)}, u32[]{:S(2)}) collective-permute-start(bf16[361,8,32]{0,2,1:T(8,128)(2,1)S(1)} %pad_maximum_fusion), channel_id=1, source_target_pairs={{0,1},{1,0},{2,3},{3,2},{4,5},{5,4},{6,7},{7,6},{8,9},{9,8},{10,11... | collective-permute-start | bytes 554504 | tf_op jit(solution)/shard_map/ppermute | solution.py:18
  6.0 4.9 %collective-permute-done = bf16[361,8,32]{0,2,1:T(8,128)(2,1)S(1)} collective-permute-done((bf16[361,8,32]{0,2,1:T(8,128)(2,1)S(1)}, bf16[361,8,32]{0,2,1:T(8,128)(2,1)S(1)}, u32[]{:S(2)}, u32[]{:S(2)}) %collective-permute-start) | collective-permute-done | bytes 184864 | tf_op jit(solution)/shard_map/ppermute | solution.py:18
  10.9 1.2 %convolution_bitcast_fusion.1 = f32[1,8,160,648]{3,2,1,0:T(8,128)S(1)} fusion(bf16[1296,361]{1,0:T(8,128)(2,1)S(1)} %copy-done.3, bf16[361,8,16]{0,2,1:T(8,128)(2,1)S(1)} %get-tuple-element.25, bf16[361,8,128]{0,2,1:T(8,128)(2,1)S(1)} %multiply_convert_fusion, bf16[361,8,16]{0,2,1:T(8,128)(2,1)S(1)} %get-tuple-element.24), kind=kOutput, calls=%fused_computation.2 | convolution fusion | flops 601628160 | bytes 4798464 | tf_op jit(solution)/shard_map/dot_general | solution.py:154
  12.2 1.2 %convolution_bitcast_fusion = f32[1,8,160,648]{3,2,1,0:T(8,128)S(1)} fusion(bf16[1296,361]{1,0:T(8,128)(2,1)S(1)} %copy-done.3, bf16[361,8,16]{0,2,1:T(8,128)(2,1)S(1)} %get-tuple-element.25, bf16[361,8,128]{0,2,1:T(8,128)(2,1)S(1)} %multiply_convert_fusion, bf16[361,8,16]{0,2,1:T(8,128)(2,1)S(1)} %get-tuple-element.24), kind=kOutput, calls=%fused_computation.1 | convolution fusion | flops 601628160 | bytes 4798464 | tf_op jit(solution)/shard_map/dot_general | solution.py:154
  13.4 0.8 maximum_multiply_fusion
  14.2 3.0 %copy-done = f32[2,8,160,648]{3,2,1,0:T(8,128)} copy-done((f32[2,8,160,648]{3,2,1,0:T(8,128)}, f32[2,8,160,648]{3,2,1,0:T(8,128)S(1)}, u32[]{:S(2)}) %copy-start) | copy-done | bytes 6635544
  17.2 0.5 fusion.7
  17.7 0.9 reshape.178
  18.6 0.1 pad.7
  18.7 1.2 %reshape.179 = f32[64,8,512]{2,1,0:T(8,128)} reshape(f32[262144]{0:T(1024)S(1)} %pad.7) | data formatting | bytes 2097152 | tf_op jit(solution)/shard_map/reshape | solution.py:61
  19.9 9.8 %all-to-all-start = ((f32[64,8,512]{2,1,0:T(8,128)}), f32[64,8,512]{2,1,0:T(8,128)S(1)}, u32[]{:S(2)}, u32[]{:S(2)}) async-start(f32[64,8,512]{2,1,0:T(8,128)} %reshape.179), calls=%async_computation | async-start | bytes 2097152 | tf_op jit(solution)/shard_map/all_to_all | solution.py:63
  29.8 0.9 reshape.181
  30.7 0.1 pad.8
  30.8 0.2 reshape_reshape.6
  31.0 0.2 subtract_reduce_fusion
  31.2 16.4 %all-to-all-done = f32[64,8,512]{2,1,0:T(8,128)S(1)} async-done(((f32[64,8,512]{2,1,0:T(8,128)}), f32[64,8,512]{2,1,0:T(8,128)S(1)}, u32[]{:S(2)}, u32[]{:S(2)}) %all-to-all-start) | async-done | bytes 1048608 | tf_op jit(solution)/shard_map/all_to_all | solution.py:63
  47.6 0.1 pad.30
  47.7 0.6 copy.45
  48.3 0.6 copy.43
  49.0 0.2 fusion
  49.1 0.2 fusion.1
  49.3 0.2 fusion.2
  49.6 0.1 fusion.3
  49.8 0.1 fusion.4
  49.9 0.1 fusion.32
  50.0 0.1 fusion.5
  50.2 0.6 copy.46
  50.9 1.2 %maximum_divide_fusion = f32[64,8,512]{2,1,0:T(8,128)} fusion(f32[63,8,512]{2,1,0:T(8,128)S(1)} %slice.185, f32[1,8,512]{2,1,0:T(8,128)S(1)} %concatenate.46, f32[8,512]{1,0:T(8,128)S(1)} %div.11), kind=kLoop, calls=%fused_computation.17 | loop fusion | flops 524288 | bytes 2113536 | tf_op jit(solution)/shard_map/div | solution.py:67
  52.1 5.0 %all-to-all-start.1 = ((f32[64,8,512]{2,1,0:T(8,128)}), f32[64,8,512]{2,1,0:T(8,128)S(1)}, u32[]{:S(2)}, u32[]{:S(2)}) async-start(f32[64,8,512]{2,1,0:T(8,128)} %maximum_divide_fusion), calls=%async_computation.1 | async-start | bytes 2097152 | tf_op jit(solution)/shard_map/all_to_all | solution.py:69
  57.1 0.6 broadcast_in_dim.9.factor_ref
  57.7 0.7 copy.35.steps_ref
  58.3 1.3 %fusion.27 = bf16[2,160,648]{2,1,0:T(8,128)(2,1)S(1)} fusion(f32[2,8,160,648]{3,2,1,0:T(8,128)} %copy-done), kind=kLoop, calls=%fused_computation.49 | loop fusion | bytes 829440 | tf_op jit(solution)/shard_map/convert_element_type | solution.py:164
  59.6 0.1 collective-permute-start.1
  59.7 0.2 fusion.28
  59.9 15.0 %all-to-all-done.1 = f32[64,8,512]{2,1,0:T(8,128)S(1)} async-done(((f32[64,8,512]{2,1,0:T(8,128)}), f32[64,8,512]{2,1,0:T(8,128)S(1)}, u32[]{:S(2)}, u32[]{:S(2)}) %all-to-all-start.1) | async-done | bytes 1048608 | tf_op jit(solution)/shard_map/all_to_all | solution.py:69
  74.9 0.3 copy.47
  75.2 2.0 %reshape_reshape.7.entering_ref = f32[2,20,8,648]{3,2,1,0:T(8,128)} reshape(f32[207360]{0:T(1024)S(1)} %slice.183) | data formatting | bytes 1658880 | tf_op jit(solution)/shard_map/reshape;reshape | solution.py:132
  77.2 3.3 %collective-permute-done.1 = bf16[2,160,648]{2,1,0:T(8,128)(2,1)S(1)} collective-permute-done((bf16[2,160,648]{2,1,0:T(8,128)(2,1)S(1)}, bf16[2,160,648]{2,1,0:T(8,128)(2,1)S(1)}, u32[]{:S(2)}, u32[]{:S(2)}) %collective-permute-start.1) | collective-permute-done | bytes 414752 | tf_op jit(solution)/shard_map/ppermute | solution.py:18
  80.5 0.7 broadcast_in_dim.10.cos_ref
  81.2 0.7 broadcast_in_dim.11.sin_ref
  81.9 15.0 %shard_map.82 = (bf16[8,16,8,648]{3,2,1,0:T(8,128)(2,1)}, bf16[8,16,8,648]{3,2,1,0:T(8,128)(2,1)}) custom-call(s32[6,2]{1,0:T(8,128)} %copy.35.steps_ref, f32[2,8,20,8,648]{4,3,2,1,0:T(8,128)} %bitcast.128, f32[2,20,8,648]{3,2,1,0:T(8,128)} %reshape_reshape.7.entering_ref, bf16[2,20,8,648]{3,2,1,0:T(8,128)(2,1)} %bitcast.143, ...), custom_call_target="tpu_custom_call" | custom-call | flops 49766400 | bytes 9123840 | tf_op jit(solution)/shard_map/pallas_call | solution.py:120
  97.0 2.3 %fusion.22 = f32[1024,361]{0,1:T(8,128)S(1)} fusion(bf16[1024,648]{1,0:T(8,128)(2,1)} %bitcast.142, bf16[361,1296]{0,1:T(8,128)(2,1)S(1)} %copy-done.2), kind=kOutput, calls=%fused_computation.44 | convolution fusion | flops 479084544 | bytes 3303424 | tf_op jit(solution)/shard_map/dot_general | solution.py:174
  99.3 0.8 add_convert_fusion
  100.1 0.2 copy.48
  100.3 0.9 slice.186
  (38 shorter events, 0.6 us)
Async XLA Ops:
  0.0 6.0 %copy-start.5 = (f32[648]{0:T(1024)S(1)}, f32[648]{0:T(1024)}, u32[]{:S(2)}) copy-start(f32[648]{0:T(1024)} %param.12) | copy-start | bytes 7780
  0.0 10.9 %copy-start.3 = (bf16[1296,361]{1,0:T(8,128)(2,1)S(1)}, bf16[1296,361]{1,0:T(8,128)(2,1)}, u32[]{:S(2)}) copy-start(bf16[1296,361]{1,0:T(8,128)(2,1)} %param.10) | copy-start | bytes 2807140
  2.7 8.3 %collective-permute-start = (bf16[361,8,32]{0,2,1:T(8,128)(2,1)S(1)}, bf16[361,8,32]{0,2,1:T(8,128)(2,1)S(1)}, u32[]{:S(2)}, u32[]{:S(2)}) collective-permute-start(bf16[361,8,32]{0,2,1:T(8,128)(2,1)S(1)} %pad_maximum_fusion), channel_id=1, source_target_pairs={{0,1},{1,0},{2,3},{3,2},{4,5},{5,4},{6,7},{7,6},{8,9},{9,8},{10,11... | collective-permute-start | bytes 554504 | tf_op jit(solution)/shard_map/ppermute | solution.py:18
  14.1 3.0 %copy-start = (f32[2,8,160,648]{3,2,1,0:T(8,128)}, f32[2,8,160,648]{3,2,1,0:T(8,128)S(1)}, u32[]{:S(2)}) copy-start(f32[2,8,160,648]{3,2,1,0:T(8,128)S(1)} %maximum_multiply_fusion) | copy-start | bytes 19906564
  19.9 27.7 %all-to-all-start = ((f32[64,8,512]{2,1,0:T(8,128)}), f32[64,8,512]{2,1,0:T(8,128)S(1)}, u32[]{:S(2)}, u32[]{:S(2)}) async-start(f32[64,8,512]{2,1,0:T(8,128)} %reshape.179), calls=%async_computation | async-start | bytes 2097152 | tf_op jit(solution)/shard_map/all_to_all | solution.py:63
  50.9 6.8 %copy-start.8 = (s32[6,2]{0,1:T(2,128)S(1)}, s32[6,2]{0,1:T(2,128)}, u32[]{:S(2)}) copy-start(s32[6,2]{0,1:T(2,128)} %param.15) | copy-start | bytes 148
  52.1 7.6 %copy-start.6 = (f32[648]{0:T(1024)S(1)}, f32[648]{0:T(1024)}, u32[]{:S(2)}) copy-start(f32[648]{0:T(1024)} %param.14) | copy-start | bytes 7780
  52.1 7.6 %copy-start.7 = (f32[648]{0:T(1024)S(1)}, f32[648]{0:T(1024)}, u32[]{:S(2)}) copy-start(f32[648]{0:T(1024)} %param.13) | copy-start | bytes 7780
  52.1 22.8 %all-to-all-start.1 = ((f32[64,8,512]{2,1,0:T(8,128)}), f32[64,8,512]{2,1,0:T(8,128)S(1)}, u32[]{:S(2)}, u32[]{:S(2)}) async-start(f32[64,8,512]{2,1,0:T(8,128)} %maximum_divide_fusion), calls=%async_computation.1 | async-start | bytes 2097152 | tf_op jit(solution)/shard_map/all_to_all | solution.py:69
  59.6 20.9 %collective-permute-start.1 = (bf16[2,160,648]{2,1,0:T(8,128)(2,1)S(1)}, bf16[2,160,648]{2,1,0:T(8,128)(2,1)S(1)}, u32[]{:S(2)}, u32[]{:S(2)}) collective-permute-start(bf16[2,160,648]{2,1,0:T(8,128)(2,1)S(1)} %fusion.27), channel_id=1, source_target_pairs={{0,2},{2,4},{4,6},{6,8},{8,10},{10,12},{12,14},{14,16},{16,18},{18... | collective-permute-start | bytes 1244168 | tf_op jit(solution)/shard_map/ppermute | solution.py:18
  80.5 1.4 %copy-start.4 = (bf16[2,160,648]{2,1,0:T(8,128)(2,1)}, bf16[2,160,648]{2,1,0:T(8,128)(2,1)S(1)}, u32[]{:S(2)}) copy-start(bf16[2,160,648]{2,1,0:T(8,128)(2,1)S(1)} %collective-permute-done.1) | copy-start | bytes 1244164
  81.9 15.0 %copy-start.2 = (bf16[361,1296]{0,1:T(8,128)(2,1)S(1)}, bf16[361,1296]{0,1:T(8,128)(2,1)}, u32[]{:S(2)}) copy-start(bf16[361,1296]{0,1:T(8,128)(2,1)} %param.11) | copy-start | bytes 2807140
  96.9 2.3 %copy-start.1 = (bf16[8,16,8,648]{3,2,1,0:T(8,128)(2,1)S(1)}, bf16[8,16,8,648]{3,2,1,0:T(8,128)(2,1)}, u32[]{:S(2)}) copy-start(bf16[8,16,8,648]{3,2,1,0:T(8,128)(2,1)} %get-tuple-element.11) | copy-start | bytes 3981316

commit v11 on v10

--- a/solution.py
+++ b/solution.py
@@ -160,7 +160,7 @@
     outgoing = box_terms[:, layers - 1]
     for j in range(layers - 1):
         outgoing = outgoing + jnp.exp(-rate[0] * float(layers - 1 - j)) * box_terms[:, j]
-    outgoing, box_terms = lax.optimization_barrier((outgoing, box_terms))
+    outgoing = lax.optimization_barrier(outgoing)
     before_term = from_behind(box_terms[:, layers - 1].astype(jnp.bfloat16), "gz", 1)
 
     rate_full = jnp.broadcast_to(decay_rate, outgoing.shape)

time: 102 us -> 102 us (level)
  waiting for transfers between devices: 39.5 us -> 32.4 us
  other arithmetic: 4.62 us -> 11.7 us
    mul x1 -> x2, other arithmetic: 0.78 us -> 7.92 us  [body(): box_terms = weight * jnp.stack(halves)]
    all_to_all x1, waiting for transfers between devices: 15 us -> 9.1 us  [entering_sums(): back = lax.all_to_all(sums, 'gz', 0, 0, tiled=True)]
    all_to_all x1, waiting for transfers between devices: 16.4 us -> 15.1 us  [entering_sums(): held = lax.all_to_all(spread(outgoing, 0.0), 'gz', 0, 0, tiled=True)]
    unnamed x28 -> x32, local copies, waits for them, and re-layouts: 7.76 us -> 8.94 us
  transfers between devices with their start and end apart: 4 -> 4, of which waited for: 4 -> 4; matrix products, arithmetic and copies ran while one was open for 6% -> 13% of each run, Pallas kernels for 0% -> 0%
where the time goes in v11:
time: 102 us
  waiting for transfers between devices  32.4 us (32%)
  local copies, waits for them, and re-layouts  18.9 us (19%)
  starting transfers between devices  18.1 us (18%)
  Pallas kernels  14.8 us (15%)
  other arithmetic  11.7 us (11%)
  matrix products  5.54 us (5%)
    all_to_all x1, waiting for transfers between devices, entering_sums(): held = lax.all_to_all(spread(outgoing, 0.0), 'gz', 0, 0, tiled=True)  15.1 us
    pallas_call x1, Pallas kernels, shift_layers(): pl.pallas_call(shift_kernel, out_shape=(half, half), in_specs=[smem] + [v...  14.8 us
    all_to_all x1, starting transfers between devices, entering_sums(): held = lax.all_to_all(spread(outgoing, 0.0), 'gz', 0, 0, tiled=True)  9.84 us
    all_to_all x1, waiting for transfers between devices, entering_sums(): back = lax.all_to_all(sums, 'gz', 0, 0, tiled=True)  9.1 us
    unnamed x32, local copies, waits for them, and re-layouts  8.94 us
    ppermute x2, waiting for transfers between devices, from_behind(): return lax.ppermute(value, axis, pairs)  8.15 us
    mul x2, other arithmetic, body(): box_terms = weight * jnp.stack(halves)  7.92 us
    all_to_all x1, starting transfers between devices, entering_sums(): back = lax.all_to_all(sums, 'gz', 0, 0, tiled=True)  4.83 us
  transfers between devices with their start and end apart: 4, of which 4 were waited for; matrix products, arithmetic and copies ran while one was open for 13% of the time, Pallas kernels for 0%

profile of v11, /device:TPU:0, one launch (start us, length us, event | category | flops | bytes accessed | tf_op | source)
XLA Modules:
  0.0 101.9 jit_solution(17027006712974954746)
XLA Ops:
  0.0 1.7 %copy.27 = bf16[361,8,128]{0,2,1:T(8,128)(2,1)S(1)} copy(bf16[361,8,128]{2,1,0:T(8,128)(2,1)} %param.8) | data formatting | bytes 1478656 | tf_op args[0]
  1.7 0.7 convert_element_type.22
  2.4 0.2 multiply_convert_fusion
  2.7 3.4 %collective-permute-start = (bf16[361,8,32]{0,2,1:T(8,128)(2,1)S(1)}, bf16[361,8,32]{0,2,1:T(8,128)(2,1)S(1)}, u32[]{:S(2)}, u32[]{:S(2)}) collective-permute-start(bf16[361,8,32]{0,2,1:T(8,128)(2,1)S(1)} %pad_maximum_fusion), channel_id=1, source_target_pairs={{0,1},{1,0},{2,3},{3,2},{4,5},{5,4},{6,7},{7,6},{8,9},{9,8},{10,11... | collective-permute-start | bytes 554504 | tf_op jit(solution)/shard_map/ppermute | solution.py:18
  6.0 4.9 %collective-permute-done = bf16[361,8,32]{0,2,1:T(8,128)(2,1)S(1)} collective-permute-done((bf16[361,8,32]{0,2,1:T(8,128)(2,1)S(1)}, bf16[361,8,32]{0,2,1:T(8,128)(2,1)S(1)}, u32[]{:S(2)}, u32[]{:S(2)}) %collective-permute-start) | collective-permute-done | bytes 184864 | tf_op jit(solution)/shard_map/ppermute | solution.py:18
  10.9 1.2 %fusion.23 = f32[8,160,648]{2,1,0:T(8,128)S(1)} fusion(bf16[1296,361]{1,0:T(8,128)(2,1)S(1)} %copy-done.5, bf16[361,8,16]{0,2,1:T(8,128)(2,1)S(1)} %get-tuple-element.21, bf16[361,8,128]{0,2,1:T(8,128)(2,1)S(1)} %multiply_convert_fusion, bf16[361,8,16]{0,2,1:T(8,128)(2,1)S(1)} %get-tuple-element.20), kind=kOutput, calls=%fused_computation.43 | convolution fusion | flops 601628160 | bytes 4798464 | tf_op jit(solution)/shard_map/dot_general | solution.py:154
  12.2 1.2 %fusion.21 = f32[8,160,648]{2,1,0:T(8,128)S(1)} fusion(bf16[1296,361]{1,0:T(8,128)(2,1)S(1)} %copy-done.5, bf16[361,8,16]{0,2,1:T(8,128)(2,1)S(1)} %get-tuple-element.21, bf16[361,8,128]{0,2,1:T(8,128)(2,1)S(1)} %multiply_convert_fusion, bf16[361,8,16]{0,2,1:T(8,128)(2,1)S(1)} %get-tuple-element.20), kind=kOutput, calls=%fused_computation.41 | convolution fusion | flops 601628160 | bytes 4798464 | tf_op jit(solution)/shard_map/dot_general | solution.py:154
  13.4 0.7 copy-done
  14.1 0.8 maximum_multiply_fusion.1
  14.9 0.5 copy-done.1
  15.3 3.1 %copy-done.2 = f32[2,8,160,648]{3,2,1,0:T(8,128)} copy-done((f32[2,8,160,648]{3,2,1,0:T(8,128)}, f32[2,8,160,648]{3,2,1,0:T(8,128)S(1)}, u32[]{:S(2)}) %copy-start.2) | copy-done | bytes 6635544
  18.4 0.5 fusion.7
  18.9 0.9 reshape.178
  19.8 0.1 pad.7
  19.9 1.1 %reshape.179 = f32[64,8,512]{2,1,0:T(8,128)} reshape(f32[262144]{0:T(1024)S(1)} %pad.7) | data formatting | bytes 2097152 | tf_op jit(solution)/shard_map/reshape | solution.py:61
  21.0 9.8 %all-to-all-start = ((f32[64,8,512]{2,1,0:T(8,128)}), f32[64,8,512]{2,1,0:T(8,128)S(1)}, u32[]{:S(2)}, u32[]{:S(2)}) async-start(f32[64,8,512]{2,1,0:T(8,128)} %reshape.179), calls=%async_computation | async-start | bytes 2097152 | tf_op jit(solution)/shard_map/all_to_all | solution.py:63
  30.9 0.6 broadcast_in_dim.9.factor_ref
  31.5 0.7 copy.35.steps_ref
  32.2 0.9 reshape.181
  33.2 0.2 reshape_reshape.6
  33.4 0.2 subtract_reduce_fusion
  33.6 15.1 %all-to-all-done = f32[64,8,512]{2,1,0:T(8,128)S(1)} async-done(((f32[64,8,512]{2,1,0:T(8,128)}), f32[64,8,512]{2,1,0:T(8,128)S(1)}, u32[]{:S(2)}, u32[]{:S(2)}) %all-to-all-start) | async-done | bytes 1048608 | tf_op jit(solution)/shard_map/all_to_all | solution.py:63
  48.8 0.6 copy.45
  49.4 0.6 copy.43
  50.1 0.2 fusion
  50.3 0.2 fusion.1
  50.5 0.2 fusion.2
  50.7 0.1 fusion.3
  50.9 0.1 fusion.4
  51.1 0.1 fusion.5
  51.3 0.6 copy.46
  52.1 1.1 %maximum_divide_fusion = f32[64,8,512]{2,1,0:T(8,128)} fusion(f32[63,8,512]{2,1,0:T(8,128)S(1)} %slice.180, f32[1,8,512]{2,1,0:T(8,128)S(1)} %concatenate.47, f32[8,512]{1,0:T(8,128)S(1)} %div.11), kind=kLoop, calls=%fused_computation.16 | loop fusion | flops 524288 | bytes 2113536 | tf_op jit(solution)/shard_map/div | solution.py:67
  53.2 4.8 %all-to-all-start.1 = ((f32[64,8,512]{2,1,0:T(8,128)}), f32[64,8,512]{2,1,0:T(8,128)S(1)}, u32[]{:S(2)}, u32[]{:S(2)}) async-start(f32[64,8,512]{2,1,0:T(8,128)} %maximum_divide_fusion), calls=%async_computation.1 | async-start | bytes 2097152 | tf_op jit(solution)/shard_map/all_to_all | solution.py:69
  58.0 0.2 fusion.30
  58.2 1.3 %fusion.20 = bf16[2,160,648]{2,1,0:T(8,128)(2,1)S(1)} fusion(f32[2,8,160,648]{3,2,1,0:T(8,128)} %copy-done.2), kind=kLoop, calls=%fused_computation.40 | loop fusion | bytes 829440 | tf_op jit(solution)/shard_map/convert_element_type | solution.py:164
  59.5 0.1 collective-permute-start.1
  59.6 7.1 %maximum_multiply_fusion.terms_ref = f32[2,8,20,8,648]{4,3,2,1,0:T(8,128)} fusion(f32[1,8,20,8,648]{4,3,2,1,0:T(8,128)} %bitcast.130, f32[1,8,20,8,648]{4,3,2,1,0:T(8,128)} %bitcast.128, f32[648]{0:T(1024)S(1)} %get-tuple-element.25), kind=kLoop, calls=%fused_computation | loop fusion | flops 3317760 | bytes 13273632 | tf_op jit(solution)/shard_map/mul | solution.py:158
  66.7 9.1 %all-to-all-done.1 = f32[64,8,512]{2,1,0:T(8,128)S(1)} async-done(((f32[64,8,512]{2,1,0:T(8,128)}), f32[64,8,512]{2,1,0:T(8,128)S(1)}, u32[]{:S(2)}, u32[]{:S(2)}) %all-to-all-start.1) | async-done | bytes 1048608 | tf_op jit(solution)/shard_map/all_to_all | solution.py:69
  75.8 0.3 copy.47
  76.2 2.0 %reshape_reshape.7.entering_ref = f32[2,20,8,648]{3,2,1,0:T(8,128)} reshape(f32[207360]{0:T(1024)S(1)} %slice.179) | data formatting | bytes 1658880 | tf_op jit(solution)/shard_map/reshape;reshape | solution.py:132
  78.2 3.3 %collective-permute-done.1 = bf16[2,160,648]{2,1,0:T(8,128)(2,1)S(1)} collective-permute-done((bf16[2,160,648]{2,1,0:T(8,128)(2,1)S(1)}, bf16[2,160,648]{2,1,0:T(8,128)(2,1)S(1)}, u32[]{:S(2)}, u32[]{:S(2)}) %collective-permute-start.1) | collective-permute-done | bytes 414752 | tf_op jit(solution)/shard_map/ppermute | solution.py:18
  81.5 0.7 broadcast_in_dim.10.cos_ref
  82.2 0.7 broadcast_in_dim.11.sin_ref
  82.8 14.8 %shard_map.82 = (bf16[8,16,8,648]{3,2,1,0:T(8,128)(2,1)}, bf16[8,16,8,648]{3,2,1,0:T(8,128)(2,1)}) custom-call(s32[6,2]{1,0:T(8,128)} %copy.35.steps_ref, f32[2,8,20,8,648]{4,3,2,1,0:T(8,128)} %maximum_multiply_fusion.terms_ref, f32[2,20,8,648]{3,2,1,0:T(8,128)} %reshape_reshape.7.entering_ref, bf16[2,20,8,648]{3,2,1,0:T(8,128)(2,1)} %bitcast.145, ...), custom_call_target="tpu_custom_call" | custom-call | flops 49766400 | bytes 9123840 | tf_op jit(solution)/shard_map/pallas_call | solution.py:120
  97.6 2.3 %fusion.25 = f32[1024,361]{0,1:T(8,128)S(1)} fusion(bf16[1024,648]{1,0:T(8,128)(2,1)} %bitcast.144, bf16[361,1296]{0,1:T(8,128)(2,1)S(1)} %copy-done.4), kind=kOutput, calls=%fused_computation.45 | convolution fusion | flops 479084544 | bytes 3303424 | tf_op jit(solution)/shard_map/dot_general | solution.py:174
  100.0 0.8 add_convert_fusion
  100.8 0.2 copy.48
  101.0 0.9 slice.181
  (43 shorter events, 0.9 us)
Async XLA Ops:
  0.0 6.0 %copy-start.7 = (f32[648]{0:T(1024)S(1)}, f32[648]{0:T(1024)}, u32[]{:S(2)}) copy-start(f32[648]{0:T(1024)} %param.12) | copy-start | bytes 7780
  0.0 10.9 %copy-start.5 = (bf16[1296,361]{1,0:T(8,128)(2,1)S(1)}, bf16[1296,361]{1,0:T(8,128)(2,1)}, u32[]{:S(2)}) copy-start(bf16[1296,361]{1,0:T(8,128)(2,1)} %param.10) | copy-start | bytes 2807140
  2.7 8.3 %collective-permute-start = (bf16[361,8,32]{0,2,1:T(8,128)(2,1)S(1)}, bf16[361,8,32]{0,2,1:T(8,128)(2,1)S(1)}, u32[]{:S(2)}, u32[]{:S(2)}) collective-permute-start(bf16[361,8,32]{0,2,1:T(8,128)(2,1)S(1)} %pad_maximum_fusion), channel_id=1, source_target_pairs={{0,1},{1,0},{2,3},{3,2},{4,5},{5,4},{6,7},{7,6},{8,9},{9,8},{10,11... | collective-permute-start | bytes 554504 | tf_op jit(solution)/shard_map/ppermute | solution.py:18
  12.2 1.9 %copy-start = (f32[8,160,648]{2,1,0:T(8,128)}, f32[8,160,648]{2,1,0:T(8,128)S(1)}, u32[]{:S(2)}) copy-start(f32[8,160,648]{2,1,0:T(8,128)S(1)} %fusion.23) | copy-start | bytes 9953284
  13.4 1.9 %copy-start.1 = (f32[8,160,648]{2,1,0:T(8,128)}, f32[8,160,648]{2,1,0:T(8,128)S(1)}, u32[]{:S(2)}) copy-start(f32[8,160,648]{2,1,0:T(8,128)S(1)} %fusion.21) | copy-start | bytes 9953284
  15.3 3.1 %copy-start.2 = (f32[2,8,160,648]{3,2,1,0:T(8,128)}, f32[2,8,160,648]{3,2,1,0:T(8,128)S(1)}, u32[]{:S(2)}) copy-start(f32[2,8,160,648]{3,2,1,0:T(8,128)S(1)} %maximum_multiply_fusion.1) | copy-start | bytes 19906564
  19.9 11.6 %copy-start.10 = (s32[6,2]{0,1:T(2,128)S(1)}, s32[6,2]{0,1:T(2,128)}, u32[]{:S(2)}) copy-start(s32[6,2]{0,1:T(2,128)} %param.15) | copy-start | bytes 148
  21.0 27.7 %all-to-all-start = ((f32[64,8,512]{2,1,0:T(8,128)}), f32[64,8,512]{2,1,0:T(8,128)S(1)}, u32[]{:S(2)}, u32[]{:S(2)}) async-start(f32[64,8,512]{2,1,0:T(8,128)} %reshape.179), calls=%async_computation | async-start | bytes 2097152 | tf_op jit(solution)/shard_map/all_to_all | solution.py:63
  52.0 6.0 %copy-start.8 = (f32[648]{0:T(1024)S(1)}, f32[648]{0:T(1024)}, u32[]{:S(2)}) copy-start(f32[648]{0:T(1024)} %param.14) | copy-start | bytes 7780
  52.0 6.0 %copy-start.9 = (f32[648]{0:T(1024)S(1)}, f32[648]{0:T(1024)}, u32[]{:S(2)}) copy-start(f32[648]{0:T(1024)} %param.13) | copy-start | bytes 7780
  53.2 22.7 %all-to-all-start.1 = ((f32[64,8,512]{2,1,0:T(8,128)}), f32[64,8,512]{2,1,0:T(8,128)S(1)}, u32[]{:S(2)}, u32[]{:S(2)}) async-start(f32[64,8,512]{2,1,0:T(8,128)} %maximum_divide_fusion), calls=%async_computation.1 | async-start | bytes 2097152 | tf_op jit(solution)/shard_map/all_to_all | solution.py:69
  59.5 22.0 %collective-permute-start.1 = (bf16[2,160,648]{2,1,0:T(8,128)(2,1)S(1)}, bf16[2,160,648]{2,1,0:T(8,128)(2,1)S(1)}, u32[]{:S(2)}, u32[]{:S(2)}) collective-permute-start(bf16[2,160,648]{2,1,0:T(8,128)(2,1)S(1)} %fusion.20), channel_id=1, source_target_pairs={{0,2},{2,4},{4,6},{6,8},{8,10},{10,12},{12,14},{14,16},{16,18},{18... | collective-permute-start | bytes 1244168 | tf_op jit(solution)/shard_map/ppermute | solution.py:18
  81.5 1.4 %copy-start.6 = (bf16[2,160,648]{2,1,0:T(8,128)(2,1)}, bf16[2,160,648]{2,1,0:T(8,128)(2,1)S(1)}, u32[]{:S(2)}) copy-start(bf16[2,160,648]{2,1,0:T(8,128)(2,1)S(1)} %collective-permute-done.1) | copy-start | bytes 1244164
  82.8 14.8 %copy-start.4 = (bf16[361,1296]{0,1:T(8,128)(2,1)S(1)}, bf16[361,1296]{0,1:T(8,128)(2,1)}, u32[]{:S(2)}) copy-start(bf16[361,1296]{0,1:T(8,128)(2,1)} %param.11) | copy-start | bytes 2807140
  97.6 2.3 %copy-start.3 = (bf16[8,16,8,648]{3,2,1,0:T(8,128)(2,1)S(1)}, bf16[8,16,8,648]{3,2,1,0:T(8,128)(2,1)}, u32[]{:S(2)}) copy-start(bf16[8,16,8,648]{3,2,1,0:T(8,128)(2,1)} %get-tuple-element.7) | copy-start | bytes 3981316

commit v12 on v10

--- a/solution.py
+++ b/solution.py
@@ -106,7 +106,7 @@
             imag_ref[i, x] = acc_imag.astype(imag_ref.dtype)
             return carry
 
-        lax.fori_loop(0, columns, column, 0, unroll=2)
+        lax.fori_loop(0, columns, column, 0, unroll=4)
 
 
 def shift_layers(offsets, box_terms, entering, before_term, rate, wave_x, wave_y, columns):

time: 102 us -> 101 us (level)
  no operation moved by 1% of the time
where the time goes in v12:
time: 101 us; the launch traced here: 100 us
  waiting for transfers between devices  39.5 us (39%)
  starting transfers between devices  18.3 us (18%)
  local copies, waits for them, and re-layouts  17.9 us (18%)
  Pallas kernels  14.2 us (14%)
  matrix products  5.54 us (5%)
  other arithmetic  4.62 us (5%)
    all_to_all x1, waiting for transfers between devices, entering_sums(): held = lax.all_to_all(spread(outgoing, 0.0), 'gz', 0, 0, tiled=True)  16.4 us
    all_to_all x1, waiting for transfers between devices, entering_sums(): back = lax.all_to_all(sums, 'gz', 0, 0, tiled=True)  15 us
    pallas_call x1, Pallas kernels, shift_layers(): pl.pallas_call(shift_kernel, out_shape=(half, half), in_specs=[smem] + [v...  14.2 us
    all_to_all x1, starting transfers between devices, entering_sums(): held = lax.all_to_all(spread(outgoing, 0.0), 'gz', 0, 0, tiled=True)  9.84 us
    ppermute x2, waiting for transfers between devices, from_behind(): return lax.ppermute(value, axis, pairs)  8.14 us
    unnamed x28, local copies, waits for them, and re-layouts  7.76 us
    all_to_all x1, starting transfers between devices, entering_sums(): back = lax.all_to_all(sums, 'gz', 0, 0, tiled=True)  4.96 us
    ppermute x2, starting transfers between devices, from_behind(): return lax.ppermute(value, axis, pairs)  3.45 us
  transfers between devices with their start and end apart: 4, of which 4 were waited for; matrix products, arithmetic and copies ran while one was open for 6% of the time, Pallas kernels for 0%

profile of v12, /device:TPU:0, one launch (start us, length us, event | category | flops | bytes accessed | tf_op | source)
XLA Modules:
  0.0 100.4 jit_solution(12938108997091944525)
XLA Ops:
  0.0 1.7 %copy.27 = bf16[361,8,128]{0,2,1:T(8,128)(2,1)S(1)} copy(bf16[361,8,128]{2,1,0:T(8,128)(2,1)} %param.8) | data formatting | bytes 1478656 | tf_op args[0]
  1.7 0.7 convert_element_type.23
  2.4 0.2 multiply_convert_fusion
  2.7 3.4 %collective-permute-start = (bf16[361,8,32]{0,2,1:T(8,128)(2,1)S(1)}, bf16[361,8,32]{0,2,1:T(8,128)(2,1)S(1)}, u32[]{:S(2)}, u32[]{:S(2)}) collective-permute-start(bf16[361,8,32]{0,2,1:T(8,128)(2,1)S(1)} %pad_maximum_fusion), channel_id=1, source_target_pairs={{0,1},{1,0},{2,3},{3,2},{4,5},{5,4},{6,7},{7,6},{8,9},{9,8},{10,11... | collective-permute-start | bytes 554504 | tf_op jit(solution)/shard_map/ppermute | solution.py:18
  6.0 4.9 %collective-permute-done = bf16[361,8,32]{0,2,1:T(8,128)(2,1)S(1)} collective-permute-done((bf16[361,8,32]{0,2,1:T(8,128)(2,1)S(1)}, bf16[361,8,32]{0,2,1:T(8,128)(2,1)S(1)}, u32[]{:S(2)}, u32[]{:S(2)}) %collective-permute-start) | collective-permute-done | bytes 184864 | tf_op jit(solution)/shard_map/ppermute | solution.py:18
  10.9 1.2 %convolution_bitcast_fusion.1 = f32[1,8,160,648]{3,2,1,0:T(8,128)S(1)} fusion(bf16[1296,361]{1,0:T(8,128)(2,1)S(1)} %copy-done.3, bf16[361,8,16]{0,2,1:T(8,128)(2,1)S(1)} %get-tuple-element.25, bf16[361,8,128]{0,2,1:T(8,128)(2,1)S(1)} %multiply_convert_fusion, bf16[361,8,16]{0,2,1:T(8,128)(2,1)S(1)} %get-tuple-element.24), kind=kOutput, calls=%fused_computation.2 | convolution fusion | flops 601628160 | bytes 4798464 | tf_op jit(solution)/shard_map/dot_general | solution.py:154
  12.2 1.2 %convolution_bitcast_fusion = f32[1,8,160,648]{3,2,1,0:T(8,128)S(1)} fusion(bf16[1296,361]{1,0:T(8,128)(2,1)S(1)} %copy-done.3, bf16[361,8,16]{0,2,1:T(8,128)(2,1)S(1)} %get-tuple-element.25, bf16[361,8,128]{0,2,1:T(8,128)(2,1)S(1)} %multiply_convert_fusion, bf16[361,8,16]{0,2,1:T(8,128)(2,1)S(1)} %get-tuple-element.24), kind=kOutput, calls=%fused_computation.1 | convolution fusion | flops 601628160 | bytes 4798464 | tf_op jit(solution)/shard_map/dot_general | solution.py:154
  13.4 0.8 maximum_multiply_fusion
  14.2 3.0 %copy-done = f32[2,8,160,648]{3,2,1,0:T(8,128)} copy-done((f32[2,8,160,648]{3,2,1,0:T(8,128)}, f32[2,8,160,648]{3,2,1,0:T(8,128)S(1)}, u32[]{:S(2)}) %copy-start) | copy-done | bytes 6635544
  17.2 0.5 fusion.7
  17.7 0.9 reshape.178
  18.6 0.1 pad.7
  18.7 1.2 %reshape.179 = f32[64,8,512]{2,1,0:T(8,128)} reshape(f32[262144]{0:T(1024)S(1)} %pad.7) | data formatting | bytes 2097152 | tf_op jit(solution)/shard_map/reshape | solution.py:61
  19.9 9.8 %all-to-all-start = ((f32[64,8,512]{2,1,0:T(8,128)}), f32[64,8,512]{2,1,0:T(8,128)S(1)}, u32[]{:S(2)}, u32[]{:S(2)}) async-start(f32[64,8,512]{2,1,0:T(8,128)} %reshape.179), calls=%async_computation | async-start | bytes 2097152 | tf_op jit(solution)/shard_map/all_to_all | solution.py:63
  29.8 0.9 reshape.181
  30.7 0.1 pad.8
  30.8 0.2 reshape_reshape.6
  31.0 0.2 subtract_reduce_fusion
  31.2 16.4 %all-to-all-done = f32[64,8,512]{2,1,0:T(8,128)S(1)} async-done(((f32[64,8,512]{2,1,0:T(8,128)}), f32[64,8,512]{2,1,0:T(8,128)S(1)}, u32[]{:S(2)}, u32[]{:S(2)}) %all-to-all-start) | async-done | bytes 1048608 | tf_op jit(solution)/shard_map/all_to_all | solution.py:63
  47.6 0.1 pad.30
  47.7 0.6 copy.45
  48.3 0.6 copy.43
  49.0 0.2 fusion
  49.1 0.2 fusion.1
  49.3 0.2 fusion.2
  49.6 0.1 fusion.3
  49.8 0.1 fusion.4
  49.9 0.1 fusion.32
  50.0 0.1 fusion.5
  50.2 0.6 copy.46
  50.9 1.2 %maximum_divide_fusion = f32[64,8,512]{2,1,0:T(8,128)} fusion(f32[63,8,512]{2,1,0:T(8,128)S(1)} %slice.185, f32[1,8,512]{2,1,0:T(8,128)S(1)} %concatenate.46, f32[8,512]{1,0:T(8,128)S(1)} %div.11), kind=kLoop, calls=%fused_computation.17 | loop fusion | flops 524288 | bytes 2113536 | tf_op jit(solution)/shard_map/div | solution.py:67
  52.1 5.0 %all-to-all-start.1 = ((f32[64,8,512]{2,1,0:T(8,128)}), f32[64,8,512]{2,1,0:T(8,128)S(1)}, u32[]{:S(2)}, u32[]{:S(2)}) async-start(f32[64,8,512]{2,1,0:T(8,128)} %maximum_divide_fusion), calls=%async_computation.1 | async-start | bytes 2097152 | tf_op jit(solution)/shard_map/all_to_all | solution.py:69
  57.1 0.6 broadcast_in_dim.9.factor_ref
  57.7 0.7 copy.35.steps_ref
  58.3 1.3 %fusion.27 = bf16[2,160,648]{2,1,0:T(8,128)(2,1)S(1)} fusion(f32[2,8,160,648]{3,2,1,0:T(8,128)} %copy-done), kind=kLoop, calls=%fused_computation.49 | loop fusion | bytes 829440 | tf_op jit(solution)/shard_map/convert_element_type | solution.py:164
  59.6 0.1 collective-permute-start.1
  59.7 0.2 fusion.28
  59.9 15.0 %all-to-all-done.1 = f32[64,8,512]{2,1,0:T(8,128)S(1)} async-done(((f32[64,8,512]{2,1,0:T(8,128)}), f32[64,8,512]{2,1,0:T(8,128)S(1)}, u32[]{:S(2)}, u32[]{:S(2)}) %all-to-all-start.1) | async-done | bytes 1048608 | tf_op jit(solution)/shard_map/all_to_all | solution.py:69
  74.9 0.3 copy.47
  75.2 2.0 %reshape_reshape.7.entering_ref = f32[2,20,8,648]{3,2,1,0:T(8,128)} reshape(f32[207360]{0:T(1024)S(1)} %slice.183) | data formatting | bytes 1658880 | tf_op jit(solution)/shard_map/reshape;reshape | solution.py:132
  77.2 3.3 %collective-permute-done.1 = bf16[2,160,648]{2,1,0:T(8,128)(2,1)S(1)} collective-permute-done((bf16[2,160,648]{2,1,0:T(8,128)(2,1)S(1)}, bf16[2,160,648]{2,1,0:T(8,128)(2,1)S(1)}, u32[]{:S(2)}, u32[]{:S(2)}) %collective-permute-start.1) | collective-permute-done | bytes 414752 | tf_op jit(solution)/shard_map/ppermute | solution.py:18
  80.5 0.7 broadcast_in_dim.10.cos_ref
  81.2 0.7 broadcast_in_dim.11.sin_ref
  81.9 14.2 %shard_map.82 = (bf16[8,16,8,648]{3,2,1,0:T(8,128)(2,1)}, bf16[8,16,8,648]{3,2,1,0:T(8,128)(2,1)}) custom-call(s32[6,2]{1,0:T(8,128)} %copy.35.steps_ref, f32[2,8,20,8,648]{4,3,2,1,0:T(8,128)} %bitcast.128, f32[2,20,8,648]{3,2,1,0:T(8,128)} %reshape_reshape.7.entering_ref, bf16[2,20,8,648]{3,2,1,0:T(8,128)(2,1)} %bitcast.143, ...), custom_call_target="tpu_custom_call" | custom-call | flops 49766400 | bytes 9123840 | tf_op jit(solution)/shard_map/pallas_call | solution.py:120
  96.2 2.3 %fusion.22 = f32[1024,361]{0,1:T(8,128)S(1)} fusion(bf16[1024,648]{1,0:T(8,128)(2,1)} %bitcast.142, bf16[361,1296]{0,1:T(8,128)(2,1)S(1)} %copy-done.2), kind=kOutput, calls=%fused_computation.44 | convolution fusion | flops 479084544 | bytes 3303424 | tf_op jit(solution)/shard_map/dot_general | solution.py:174
  98.5 0.8 add_convert_fusion
  99.3 0.2 copy.48
  99.5 0.9 slice.186
  (38 shorter events, 0.6 us)
Async XLA Ops:
  0.0 6.0 %copy-start.5 = (f32[648]{0:T(1024)S(1)}, f32[648]{0:T(1024)}, u32[]{:S(2)}) copy-start(f32[648]{0:T(1024)} %param.12) | copy-start | bytes 7780
  0.0 10.9 %copy-start.3 = (bf16[1296,361]{1,0:T(8,128)(2,1)S(1)}, bf16[1296,361]{1,0:T(8,128)(2,1)}, u32[]{:S(2)}) copy-start(bf16[1296,361]{1,0:T(8,128)(2,1)} %param.10) | copy-start | bytes 2807140
  2.7 8.3 %collective-permute-start = (bf16[361,8,32]{0,2,1:T(8,128)(2,1)S(1)}, bf16[361,8,32]{0,2,1:T(8,128)(2,1)S(1)}, u32[]{:S(2)}, u32[]{:S(2)}) collective-permute-start(bf16[361,8,32]{0,2,1:T(8,128)(2,1)S(1)} %pad_maximum_fusion), channel_id=1, source_target_pairs={{0,1},{1,0},{2,3},{3,2},{4,5},{5,4},{6,7},{7,6},{8,9},{9,8},{10,11... | collective-permute-start | bytes 554504 | tf_op jit(solution)/shard_map/ppermute | solution.py:18
  14.1 3.0 %copy-start = (f32[2,8,160,648]{3,2,1,0:T(8,128)}, f32[2,8,160,648]{3,2,1,0:T(8,128)S(1)}, u32[]{:S(2)}) copy-start(f32[2,8,160,648]{3,2,1,0:T(8,128)S(1)} %maximum_multiply_fusion) | copy-start | bytes 19906564
  19.9 27.7 %all-to-all-start = ((f32[64,8,512]{2,1,0:T(8,128)}), f32[64,8,512]{2,1,0:T(8,128)S(1)}, u32[]{:S(2)}, u32[]{:S(2)}) async-start(f32[64,8,512]{2,1,0:T(8,128)} %reshape.179), calls=%async_computation | async-start | bytes 2097152 | tf_op jit(solution)/shard_map/all_to_all | solution.py:63
  50.9 6.8 %copy-start.8 = (s32[6,2]{0,1:T(2,128)S(1)}, s32[6,2]{0,1:T(2,128)}, u32[]{:S(2)}) copy-start(s32[6,2]{0,1:T(2,128)} %param.15) | copy-start | bytes 148
  52.1 7.6 %copy-start.6 = (f32[648]{0:T(1024)S(1)}, f32[648]{0:T(1024)}, u32[]{:S(2)}) copy-start(f32[648]{0:T(1024)} %param.14) | copy-start | bytes 7780
  52.1 7.6 %copy-start.7 = (f32[648]{0:T(1024)S(1)}, f32[648]{0:T(1024)}, u32[]{:S(2)}) copy-start(f32[648]{0:T(1024)} %param.13) | copy-start | bytes 7780
  52.1 22.8 %all-to-all-start.1 = ((f32[64,8,512]{2,1,0:T(8,128)}), f32[64,8,512]{2,1,0:T(8,128)S(1)}, u32[]{:S(2)}, u32[]{:S(2)}) async-start(f32[64,8,512]{2,1,0:T(8,128)} %maximum_divide_fusion), calls=%async_computation.1 | async-start | bytes 2097152 | tf_op jit(solution)/shard_map/all_to_all | solution.py:69
  59.6 20.9 %collective-permute-start.1 = (bf16[2,160,648]{2,1,0:T(8,128)(2,1)S(1)}, bf16[2,160,648]{2,1,0:T(8,128)(2,1)S(1)}, u32[]{:S(2)}, u32[]{:S(2)}) collective-permute-start(bf16[2,160,648]{2,1,0:T(8,128)(2,1)S(1)} %fusion.27), channel_id=1, source_target_pairs={{0,2},{2,4},{4,6},{6,8},{8,10},{10,12},{12,14},{14,16},{16,18},{18... | collective-permute-start | bytes 1244168 | tf_op jit(solution)/shard_map/ppermute | solution.py:18
  80.5 1.4 %copy-start.4 = (bf16[2,160,648]{2,1,0:T(8,128)(2,1)}, bf16[2,160,648]{2,1,0:T(8,128)(2,1)S(1)}, u32[]{:S(2)}) copy-start(bf16[2,160,648]{2,1,0:T(8,128)(2,1)S(1)} %collective-permute-done.1) | copy-start | bytes 1244164
  81.9 14.3 %copy-start.2 = (bf16[361,1296]{0,1:T(8,128)(2,1)S(1)}, bf16[361,1296]{0,1:T(8,128)(2,1)}, u32[]{:S(2)}) copy-start(bf16[361,1296]{0,1:T(8,128)(2,1)} %param.11) | copy-start | bytes 2807140
  96.2 2.3 %copy-start.1 = (bf16[8,16,8,648]{3,2,1,0:T(8,128)(2,1)S(1)}, bf16[8,16,8,648]{3,2,1,0:T(8,128)(2,1)}, u32[]{:S(2)}) copy-start(bf16[8,16,8,648]{3,2,1,0:T(8,128)(2,1)} %get-tuple-element.11) | copy-start | bytes 3981316

commit v13 on v12

--- a/solution.py
+++ b/solution.py
@@ -106,7 +106,7 @@
             imag_ref[i, x] = acc_imag.astype(imag_ref.dtype)
             return carry
 
-        lax.fori_loop(0, columns, column, 0, unroll=4)
+        lax.fori_loop(0, columns, column, 0, unroll=8)
 
 
 def shift_layers(offsets, box_terms, entering, before_term, rate, wave_x, wave_y, columns):

time: 101 us -> 101 us (level)
  no operation moved by 1% of the time
where the time goes in v13:
time: 101 us
  waiting for transfers between devices  39.5 us (39%)
  starting transfers between devices  18.3 us (18%)
  local copies, waits for them, and re-layouts  17.9 us (18%)
  Pallas kernels  14.7 us (15%)
  matrix products  5.53 us (5%)
  other arithmetic  4.62 us (5%)
    all_to_all x1, waiting for transfers between devices, entering_sums(): held = lax.all_to_all(spread(outgoing, 0.0), 'gz', 0, 0, tiled=True)  16.4 us
    all_to_all x1, waiting for transfers between devices, entering_sums(): back = lax.all_to_all(sums, 'gz', 0, 0, tiled=True)  15 us
    pallas_call x1, Pallas kernels, shift_layers(): pl.pallas_call(shift_kernel, out_shape=(half, half), in_specs=[smem] + [v...  14.7 us
    all_to_all x1, starting transfers between devices, entering_sums(): held = lax.all_to_all(spread(outgoing, 0.0), 'gz', 0, 0, tiled=True)  9.84 us
    ppermute x2, waiting for transfers between devices, from_behind(): return lax.ppermute(value, axis, pairs)  8.14 us
    unnamed x28, local copies, waits for them, and re-layouts  7.76 us
    all_to_all x1, starting transfers between devices, entering_sums(): back = lax.all_to_all(sums, 'gz', 0, 0, tiled=True)  4.96 us
    ppermute x2, starting transfers between devices, from_behind(): return lax.ppermute(value, axis, pairs)  3.45 us
  transfers between devices with their start and end apart: 4, of which 4 were waited for; matrix products, arithmetic and copies ran while one was open for 6% of the time, Pallas kernels for 0%

profile of v13, /device:TPU:0, one launch (start us, length us, event | category | flops | bytes accessed | tf_op | source)
XLA Modules:
  0.0 100.9 jit_solution(6233239009909620926)
XLA Ops:
  0.0 1.7 %copy.27 = bf16[361,8,128]{0,2,1:T(8,128)(2,1)S(1)} copy(bf16[361,8,128]{2,1,0:T(8,128)(2,1)} %param.8) | data formatting | bytes 1478656 | tf_op args[0]
  1.7 0.7 convert_element_type.23
  2.4 0.2 multiply_convert_fusion
  2.7 3.4 %collective-permute-start = (bf16[361,8,32]{0,2,1:T(8,128)(2,1)S(1)}, bf16[361,8,32]{0,2,1:T(8,128)(2,1)S(1)}, u32[]{:S(2)}, u32[]{:S(2)}) collective-permute-start(bf16[361,8,32]{0,2,1:T(8,128)(2,1)S(1)} %pad_maximum_fusion), channel_id=1, source_target_pairs={{0,1},{1,0},{2,3},{3,2},{4,5},{5,4},{6,7},{7,6},{8,9},{9,8},{10,11... | collective-permute-start | bytes 554504 | tf_op jit(solution)/shard_map/ppermute | solution.py:18
  6.0 4.9 %collective-permute-done = bf16[361,8,32]{0,2,1:T(8,128)(2,1)S(1)} collective-permute-done((bf16[361,8,32]{0,2,1:T(8,128)(2,1)S(1)}, bf16[361,8,32]{0,2,1:T(8,128)(2,1)S(1)}, u32[]{:S(2)}, u32[]{:S(2)}) %collective-permute-start) | collective-permute-done | bytes 184864 | tf_op jit(solution)/shard_map/ppermute | solution.py:18
  10.9 1.2 %convolution_bitcast_fusion.1 = f32[1,8,160,648]{3,2,1,0:T(8,128)S(1)} fusion(bf16[1296,361]{1,0:T(8,128)(2,1)S(1)} %copy-done.3, bf16[361,8,16]{0,2,1:T(8,128)(2,1)S(1)} %get-tuple-element.25, bf16[361,8,128]{0,2,1:T(8,128)(2,1)S(1)} %multiply_convert_fusion, bf16[361,8,16]{0,2,1:T(8,128)(2,1)S(1)} %get-tuple-element.24), kind=kOutput, calls=%fused_computation.2 | convolution fusion | flops 601628160 | bytes 4798464 | tf_op jit(solution)/shard_map/dot_general | solution.py:154
  12.2 1.2 %convolution_bitcast_fusion = f32[1,8,160,648]{3,2,1,0:T(8,128)S(1)} fusion(bf16[1296,361]{1,0:T(8,128)(2,1)S(1)} %copy-done.3, bf16[361,8,16]{0,2,1:T(8,128)(2,1)S(1)} %get-tuple-element.25, bf16[361,8,128]{0,2,1:T(8,128)(2,1)S(1)} %multiply_convert_fusion, bf16[361,8,16]{0,2,1:T(8,128)(2,1)S(1)} %get-tuple-element.24), kind=kOutput, calls=%fused_computation.1 | convolution fusion | flops 601628160 | bytes 4798464 | tf_op jit(solution)/shard_map/dot_general | solution.py:154
  13.4 0.8 maximum_multiply_fusion
  14.2 3.0 %copy-done = f32[2,8,160,648]{3,2,1,0:T(8,128)} copy-done((f32[2,8,160,648]{3,2,1,0:T(8,128)}, f32[2,8,160,648]{3,2,1,0:T(8,128)S(1)}, u32[]{:S(2)}) %copy-start) | copy-done | bytes 6635544
  17.2 0.5 fusion.7
  17.7 0.9 reshape.178
  18.6 0.1 pad.7
  18.7 1.2 %reshape.179 = f32[64,8,512]{2,1,0:T(8,128)} reshape(f32[262144]{0:T(1024)S(1)} %pad.7) | data formatting | bytes 2097152 | tf_op jit(solution)/shard_map/reshape | solution.py:61
  19.9 9.8 %all-to-all-start = ((f32[64,8,512]{2,1,0:T(8,128)}), f32[64,8,512]{2,1,0:T(8,128)S(1)}, u32[]{:S(2)}, u32[]{:S(2)}) async-start(f32[64,8,512]{2,1,0:T(8,128)} %reshape.179), calls=%async_computation | async-start | bytes 2097152 | tf_op jit(solution)/shard_map/all_to_all | solution.py:63
  29.8 0.9 reshape.181
  30.7 0.1 pad.8
  30.8 0.2 reshape_reshape.6
  31.0 0.2 subtract_reduce_fusion
  31.2 16.4 %all-to-all-done = f32[64,8,512]{2,1,0:T(8,128)S(1)} async-done(((f32[64,8,512]{2,1,0:T(8,128)}), f32[64,8,512]{2,1,0:T(8,128)S(1)}, u32[]{:S(2)}, u32[]{:S(2)}) %all-to-all-start) | async-done | bytes 1048608 | tf_op jit(solution)/shard_map/all_to_all | solution.py:63
  47.6 0.1 pad.30
  47.7 0.6 copy.45
  48.3 0.6 copy.43
  49.0 0.2 fusion
  49.1 0.2 fusion.1
  49.3 0.2 fusion.2
  49.6 0.1 fusion.3
  49.8 0.1 fusion.4
  49.9 0.1 fusion.32
  50.0 0.1 fusion.5
  50.2 0.6 copy.46
  50.9 1.2 %maximum_divide_fusion = f32[64,8,512]{2,1,0:T(8,128)} fusion(f32[63,8,512]{2,1,0:T(8,128)S(1)} %slice.185, f32[1,8,512]{2,1,0:T(8,128)S(1)} %concatenate.46, f32[8,512]{1,0:T(8,128)S(1)} %div.11), kind=kLoop, calls=%fused_computation.17 | loop fusion | flops 524288 | bytes 2113536 | tf_op jit(solution)/shard_map/div | solution.py:67
  52.1 5.0 %all-to-all-start.1 = ((f32[64,8,512]{2,1,0:T(8,128)}), f32[64,8,512]{2,1,0:T(8,128)S(1)}, u32[]{:S(2)}, u32[]{:S(2)}) async-start(f32[64,8,512]{2,1,0:T(8,128)} %maximum_divide_fusion), calls=%async_computation.1 | async-start | bytes 2097152 | tf_op jit(solution)/shard_map/all_to_all | solution.py:69
  57.1 0.6 broadcast_in_dim.9.factor_ref
  57.7 0.7 copy.35.steps_ref
  58.3 1.3 %fusion.27 = bf16[2,160,648]{2,1,0:T(8,128)(2,1)S(1)} fusion(f32[2,8,160,648]{3,2,1,0:T(8,128)} %copy-done), kind=kLoop, calls=%fused_computation.49 | loop fusion | bytes 829440 | tf_op jit(solution)/shard_map/convert_element_type | solution.py:164
  59.6 0.1 collective-permute-start.1
  59.7 0.2 fusion.28
  59.9 15.0 %all-to-all-done.1 = f32[64,8,512]{2,1,0:T(8,128)S(1)} async-done(((f32[64,8,512]{2,1,0:T(8,128)}), f32[64,8,512]{2,1,0:T(8,128)S(1)}, u32[]{:S(2)}, u32[]{:S(2)}) %all-to-all-start.1) | async-done | bytes 1048608 | tf_op jit(solution)/shard_map/all_to_all | solution.py:69
  74.9 0.3 copy.47
  75.2 2.0 %reshape_reshape.7.entering_ref = f32[2,20,8,648]{3,2,1,0:T(8,128)} reshape(f32[207360]{0:T(1024)S(1)} %slice.183) | data formatting | bytes 1658880 | tf_op jit(solution)/shard_map/reshape;reshape | solution.py:132
  77.2 3.3 %collective-permute-done.1 = bf16[2,160,648]{2,1,0:T(8,128)(2,1)S(1)} collective-permute-done((bf16[2,160,648]{2,1,0:T(8,128)(2,1)S(1)}, bf16[2,160,648]{2,1,0:T(8,128)(2,1)S(1)}, u32[]{:S(2)}, u32[]{:S(2)}) %collective-permute-start.1) | collective-permute-done | bytes 414752 | tf_op jit(solution)/shard_map/ppermute | solution.py:18
  80.5 0.7 broadcast_in_dim.10.cos_ref
  81.2 0.7 broadcast_in_dim.11.sin_ref
  81.9 14.7 %shard_map.82 = (bf16[8,16,8,648]{3,2,1,0:T(8,128)(2,1)}, bf16[8,16,8,648]{3,2,1,0:T(8,128)(2,1)}) custom-call(s32[6,2]{1,0:T(8,128)} %copy.35.steps_ref, f32[2,8,20,8,648]{4,3,2,1,0:T(8,128)} %bitcast.128, f32[2,20,8,648]{3,2,1,0:T(8,128)} %reshape_reshape.7.entering_ref, bf16[2,20,8,648]{3,2,1,0:T(8,128)(2,1)} %bitcast.143, ...), custom_call_target="tpu_custom_call" | custom-call | flops 49766400 | bytes 9123840 | tf_op jit(solution)/shard_map/pallas_call | solution.py:120
  96.6 2.3 %fusion.22 = f32[1024,361]{0,1:T(8,128)S(1)} fusion(bf16[1024,648]{1,0:T(8,128)(2,1)} %bitcast.142, bf16[361,1296]{0,1:T(8,128)(2,1)S(1)} %copy-done.2), kind=kOutput, calls=%fused_computation.44 | convolution fusion | flops 479084544 | bytes 3303424 | tf_op jit(solution)/shard_map/dot_general | solution.py:174
  99.0 0.8 add_convert_fusion
  99.8 0.2 copy.48
  100.0 0.9 slice.186
  (38 shorter events, 0.6 us)
Async XLA Ops:
  0.0 6.0 %copy-start.5 = (f32[648]{0:T(1024)S(1)}, f32[648]{0:T(1024)}, u32[]{:S(2)}) copy-start(f32[648]{0:T(1024)} %param.12) | copy-start | bytes 7780
  0.0 10.9 %copy-start.3 = (bf16[1296,361]{1,0:T(8,128)(2,1)S(1)}, bf16[1296,361]{1,0:T(8,128)(2,1)}, u32[]{:S(2)}) copy-start(bf16[1296,361]{1,0:T(8,128)(2,1)} %param.10) | copy-start | bytes 2807140
  2.7 8.3 %collective-permute-start = (bf16[361,8,32]{0,2,1:T(8,128)(2,1)S(1)}, bf16[361,8,32]{0,2,1:T(8,128)(2,1)S(1)}, u32[]{:S(2)}, u32[]{:S(2)}) collective-permute-start(bf16[361,8,32]{0,2,1:T(8,128)(2,1)S(1)} %pad_maximum_fusion), channel_id=1, source_target_pairs={{0,1},{1,0},{2,3},{3,2},{4,5},{5,4},{6,7},{7,6},{8,9},{9,8},{10,11... | collective-permute-start | bytes 554504 | tf_op jit(solution)/shard_map/ppermute | solution.py:18
  14.1 3.0 %copy-start = (f32[2,8,160,648]{3,2,1,0:T(8,128)}, f32[2,8,160,648]{3,2,1,0:T(8,128)S(1)}, u32[]{:S(2)}) copy-start(f32[2,8,160,648]{3,2,1,0:T(8,128)S(1)} %maximum_multiply_fusion) | copy-start | bytes 19906564
  19.9 27.7 %all-to-all-start = ((f32[64,8,512]{2,1,0:T(8,128)}), f32[64,8,512]{2,1,0:T(8,128)S(1)}, u32[]{:S(2)}, u32[]{:S(2)}) async-start(f32[64,8,512]{2,1,0:T(8,128)} %reshape.179), calls=%async_computation | async-start | bytes 2097152 | tf_op jit(solution)/shard_map/all_to_all | solution.py:63
  50.9 6.8 %copy-start.8 = (s32[6,2]{0,1:T(2,128)S(1)}, s32[6,2]{0,1:T(2,128)}, u32[]{:S(2)}) copy-start(s32[6,2]{0,1:T(2,128)} %param.15) | copy-start | bytes 148
  52.1 7.6 %copy-start.6 = (f32[648]{0:T(1024)S(1)}, f32[648]{0:T(1024)}, u32[]{:S(2)}) copy-start(f32[648]{0:T(1024)} %param.14) | copy-start | bytes 7780
  52.1 7.6 %copy-start.7 = (f32[648]{0:T(1024)S(1)}, f32[648]{0:T(1024)}, u32[]{:S(2)}) copy-start(f32[648]{0:T(1024)} %param.13) | copy-start | bytes 7780
  52.1 22.8 %all-to-all-start.1 = ((f32[64,8,512]{2,1,0:T(8,128)}), f32[64,8,512]{2,1,0:T(8,128)S(1)}, u32[]{:S(2)}, u32[]{:S(2)}) async-start(f32[64,8,512]{2,1,0:T(8,128)} %maximum_divide_fusion), calls=%async_computation.1 | async-start | bytes 2097152 | tf_op jit(solution)/shard_map/all_to_all | solution.py:69
  59.6 20.9 %collective-permute-start.1 = (bf16[2,160,648]{2,1,0:T(8,128)(2,1)S(1)}, bf16[2,160,648]{2,1,0:T(8,128)(2,1)S(1)}, u32[]{:S(2)}, u32[]{:S(2)}) collective-permute-start(bf16[2,160,648]{2,1,0:T(8,128)(2,1)S(1)} %fusion.27), channel_id=1, source_target_pairs={{0,2},{2,4},{4,6},{6,8},{8,10},{10,12},{12,14},{14,16},{16,18},{18... | collective-permute-start | bytes 1244168 | tf_op jit(solution)/shard_map/ppermute | solution.py:18
  80.5 1.4 %copy-start.4 = (bf16[2,160,648]{2,1,0:T(8,128)(2,1)}, bf16[2,160,648]{2,1,0:T(8,128)(2,1)S(1)}, u32[]{:S(2)}) copy-start(bf16[2,160,648]{2,1,0:T(8,128)(2,1)S(1)} %collective-permute-done.1) | copy-start | bytes 1244164
  81.9 14.7 %copy-start.2 = (bf16[361,1296]{0,1:T(8,128)(2,1)S(1)}, bf16[361,1296]{0,1:T(8,128)(2,1)}, u32[]{:S(2)}) copy-start(bf16[361,1296]{0,1:T(8,128)(2,1)} %param.11) | copy-start | bytes 2807140
  96.6 2.3 %copy-start.1 = (bf16[8,16,8,648]{3,2,1,0:T(8,128)(2,1)S(1)}, bf16[8,16,8,648]{3,2,1,0:T(8,128)(2,1)}, u32[]{:S(2)}) copy-start(bf16[8,16,8,648]{3,2,1,0:T(8,128)(2,1)} %get-tuple-element.11) | copy-start | bytes 3981316

commit v14 on v12

--- a/solution.py
+++ b/solution.py
@@ -160,8 +160,8 @@
     outgoing = box_terms[:, layers - 1]
     for j in range(layers - 1):
         outgoing = outgoing + jnp.exp(-rate[0] * float(layers - 1 - j)) * box_terms[:, j]
-    outgoing, box_terms = lax.optimization_barrier((outgoing, box_terms))
     before_term = from_behind(box_terms[:, layers - 1].astype(jnp.bfloat16), "gz", 1)
+    outgoing, box_terms, before_term = lax.optimization_barrier((outgoing, box_terms, before_term))
 
     rate_full = jnp.broadcast_to(decay_rate, outgoing.shape)
     entering = entering_sums(outgoing, rate_full, float(layers))

time: 101 us -> 104 us (1.030)
  waiting for transfers between devices: 39.5 us -> 47.3 us
  starting transfers between devices: 18.3 us -> 14 us
  local copies, waits for them, and re-layouts: 17.9 us -> 15.9 us
    ppermute x2, waiting for transfers between devices: 8.14 us -> 14.5 us  [from_behind(): return lax.ppermute(value, axis, pairs)]
    all_to_all x1, starting transfers between devices: 9.84 us -> 5.63 us  [entering_sums(): held = lax.all_to_all(spread(outgoing, 0.0), 'gz', 0, 0, tiled=True)]
    all_to_all x1, waiting for transfers between devices: 15 us -> 16.3 us  [entering_sums(): back = lax.all_to_all(sums, 'gz', 0, 0, tiled=True)]
    convert_element_type x1, local copies, waits for them, and re-layouts: 1.25 us -> 0.05 us  [body(): box_terms[:, layers - 1].astype(jnp.bfloat16)]
    unnamed x28 -> x26, local copies, waits for them, and re-layouts: 7.76 us -> 7.08 us
  transfers between devices with their start and end apart: 4 -> 4, of which waited for: 4 -> 4; matrix products, arithmetic and copies ran while one was open for 6% -> 3% of each run, Pallas kernels for 0% -> 0%
where the time goes in v14:
time: 104 us; the launch traced here: 102 us
  waiting for transfers between devices  47.3 us (45%)
  local copies, waits for them, and re-layouts  15.9 us (15%)
  Pallas kernels  14.6 us (14%)
  starting transfers between devices  14 us (13%)
  matrix products  5.53 us (5%)
  other arithmetic  4.64 us (4%)
    all_to_all x1, waiting for transfers between devices, entering_sums(): held = lax.all_to_all(spread(outgoing, 0.0), 'gz', 0, 0, tiled=True)  16.4 us
    all_to_all x1, waiting for transfers between devices, entering_sums(): back = lax.all_to_all(sums, 'gz', 0, 0, tiled=True)  16.3 us
    pallas_call x1, Pallas kernels, shift_layers(): pl.pallas_call(shift_kernel, out_shape=(half, half), in_specs=[smem] + [v...  14.6 us
    ppermute x2, waiting for transfers between devices, from_behind(): return lax.ppermute(value, axis, pairs)  14.5 us
    unnamed x26, local copies, waits for them, and re-layouts  7.08 us
    all_to_all x1, starting transfers between devices, entering_sums(): held = lax.all_to_all(spread(outgoing, 0.0), 'gz', 0, 0, tiled=True)  5.63 us
    all_to_all x1, starting transfers between devices, entering_sums(): back = lax.all_to_all(sums, 'gz', 0, 0, tiled=True)  4.99 us
    ppermute x2, starting transfers between devices, from_behind(): return lax.ppermute(value, axis, pairs)  3.43 us
  transfers between devices with their start and end apart: 4, of which 4 were waited for; matrix products, arithmetic and copies ran while one was open for 3% of the time, Pallas kernels for 0%

profile of v14, /device:TPU:0, one launch (start us, length us, event | category | flops | bytes accessed | tf_op | source)
XLA Modules:
  0.0 102.4 jit_solution(1398516390395109232)
XLA Ops:
  0.0 1.7 %copy.27 = bf16[361,8,128]{0,2,1:T(8,128)(2,1)S(1)} copy(bf16[361,8,128]{2,1,0:T(8,128)(2,1)} %param.8) | data formatting | bytes 1478656 | tf_op args[0]
  1.7 0.7 convert_element_type.22
  2.4 0.2 multiply_convert_fusion
  2.7 3.4 %collective-permute-start = (bf16[361,8,32]{0,2,1:T(8,128)(2,1)S(1)}, bf16[361,8,32]{0,2,1:T(8,128)(2,1)S(1)}, u32[]{:S(2)}, u32[]{:S(2)}) collective-permute-start(bf16[361,8,32]{0,2,1:T(8,128)(2,1)S(1)} %pad_maximum_fusion), channel_id=1, source_target_pairs={{0,1},{1,0},{2,3},{3,2},{4,5},{5,4},{6,7},{7,6},{8,9},{9,8},{10,11... | collective-permute-start | bytes 554504 | tf_op jit(solution)/shard_map/ppermute | solution.py:18
  6.0 4.9 %collective-permute-done = bf16[361,8,32]{0,2,1:T(8,128)(2,1)S(1)} collective-permute-done((bf16[361,8,32]{0,2,1:T(8,128)(2,1)S(1)}, bf16[361,8,32]{0,2,1:T(8,128)(2,1)S(1)}, u32[]{:S(2)}, u32[]{:S(2)}) %collective-permute-start) | collective-permute-done | bytes 184864 | tf_op jit(solution)/shard_map/ppermute | solution.py:18
  10.9 1.2 %convolution_bitcast_fusion.1 = f32[1,8,160,648]{3,2,1,0:T(8,128)S(1)} fusion(bf16[1296,361]{1,0:T(8,128)(2,1)S(1)} %copy-done.3, bf16[361,8,16]{0,2,1:T(8,128)(2,1)S(1)} %get-tuple-element.27, bf16[361,8,128]{0,2,1:T(8,128)(2,1)S(1)} %multiply_convert_fusion, bf16[361,8,16]{0,2,1:T(8,128)(2,1)S(1)} %get-tuple-element.26), kind=kOutput, calls=%fused_computation.2 | convolution fusion | flops 601628160 | bytes 4798464 | tf_op jit(solution)/shard_map/dot_general | solution.py:154
  12.2 1.2 %convolution_bitcast_fusion = f32[1,8,160,648]{3,2,1,0:T(8,128)S(1)} fusion(bf16[1296,361]{1,0:T(8,128)(2,1)S(1)} %copy-done.3, bf16[361,8,16]{0,2,1:T(8,128)(2,1)S(1)} %get-tuple-element.27, bf16[361,8,128]{0,2,1:T(8,128)(2,1)S(1)} %multiply_convert_fusion, bf16[361,8,16]{0,2,1:T(8,128)(2,1)S(1)} %get-tuple-element.26), kind=kOutput, calls=%fused_computation.1 | convolution fusion | flops 601628160 | bytes 4798464 | tf_op jit(solution)/shard_map/dot_general | solution.py:154
  13.4 0.8 maximum_multiply_fusion
  14.2 0.1 collective-permute-start.1
  14.3 0.5 fusion.7
  14.8 2.4 %copy-done = f32[2,8,160,648]{3,2,1,0:T(8,128)} copy-done((f32[2,8,160,648]{3,2,1,0:T(8,128)}, f32[2,8,160,648]{3,2,1,0:T(8,128)S(1)}, u32[]{:S(2)}) %copy-start) | copy-done | bytes 6635544
  17.2 9.7 %collective-permute-done.1 = bf16[2,160,648]{2,1,0:T(8,128)(2,1)} collective-permute-done((bf16[2,160,648]{2,1,0:T(8,128)(2,1)S(1)}, bf16[2,160,648]{2,1,0:T(8,128)(2,1)}, u32[]{:S(2)}, u32[]{:S(2)}) %collective-permute-start.1) | collective-permute-done | bytes 414752 | tf_op jit(solution)/shard_map/ppermute | solution.py:18
  26.9 0.9 reshape.177
  27.7 0.1 pad.7
  27.8 1.2 %reshape.178 = f32[64,8,512]{2,1,0:T(8,128)} reshape(f32[262144]{0:T(1024)S(1)} %pad.7) | data formatting | bytes 2097152 | tf_op jit(solution)/shard_map/reshape | solution.py:61
  29.0 5.6 %all-to-all-start = ((f32[64,8,512]{2,1,0:T(8,128)}), f32[64,8,512]{2,1,0:T(8,128)S(1)}, u32[]{:S(2)}, u32[]{:S(2)}) async-start(f32[64,8,512]{2,1,0:T(8,128)} %reshape.178), calls=%async_computation | async-start | bytes 2097152 | tf_op jit(solution)/shard_map/all_to_all | solution.py:63
  34.7 0.9 reshape.180
  35.6 0.1 pad.8
  35.7 0.2 reshape_reshape.6
  35.9 0.2 subtract_reduce_fusion
  36.1 16.4 %all-to-all-done = f32[64,8,512]{2,1,0:T(8,128)S(1)} async-done(((f32[64,8,512]{2,1,0:T(8,128)}), f32[64,8,512]{2,1,0:T(8,128)S(1)}, u32[]{:S(2)}, u32[]{:S(2)}) %all-to-all-start) | async-done | bytes 1048608 | tf_op jit(solution)/shard_map/all_to_all | solution.py:63
  52.5 0.1 pad.30
  52.6 0.6 copy.45
  53.2 0.6 copy.43
  53.9 0.2 fusion
  54.1 0.2 fusion.1
  54.3 0.2 fusion.2
  54.5 0.1 fusion.3
  54.7 0.1 fusion.4
  54.9 0.1 fusion.32
  54.9 0.1 fusion.5
  55.1 0.6 copy.46
  55.7 0.1 slice.180
  55.9 1.2 %maximum_divide_fusion = f32[64,8,512]{2,1,0:T(8,128)} fusion(f32[63,8,512]{2,1,0:T(8,128)S(1)} %slice.180, f32[1,8,512]{2,1,0:T(8,128)S(1)} %concatenate.46, f32[8,512]{1,0:T(8,128)S(1)} %div.11), kind=kLoop, calls=%fused_computation.17 | loop fusion | flops 524288 | bytes 2113536 | tf_op jit(solution)/shard_map/div | solution.py:67
  57.0 5.0 %all-to-all-start.1 = ((f32[64,8,512]{2,1,0:T(8,128)}), f32[64,8,512]{2,1,0:T(8,128)S(1)}, u32[]{:S(2)}, u32[]{:S(2)}) async-start(f32[64,8,512]{2,1,0:T(8,128)} %maximum_divide_fusion), calls=%async_computation.1 | async-start | bytes 2097152 | tf_op jit(solution)/shard_map/all_to_all | solution.py:69
  62.0 0.6 broadcast_in_dim.9.factor_ref
  62.6 0.7 copy.35.steps_ref
  63.3 0.2 fusion.28
  63.5 16.3 %all-to-all-done.1 = f32[64,8,512]{2,1,0:T(8,128)S(1)} async-done(((f32[64,8,512]{2,1,0:T(8,128)}), f32[64,8,512]{2,1,0:T(8,128)S(1)}, u32[]{:S(2)}, u32[]{:S(2)}) %all-to-all-start.1) | async-done | bytes 1048608 | tf_op jit(solution)/shard_map/all_to_all | solution.py:69
  79.8 0.3 copy.47
  80.2 2.0 %reshape_reshape.7.entering_ref = f32[2,20,8,648]{3,2,1,0:T(8,128)} reshape(f32[207360]{0:T(1024)S(1)} %slice.179) | data formatting | bytes 1658880 | tf_op jit(solution)/shard_map/reshape;reshape | solution.py:132
  82.2 0.7 broadcast_in_dim.10.cos_ref
  82.9 0.7 broadcast_in_dim.11.sin_ref
  83.6 14.6 %shard_map.82 = (bf16[8,16,8,648]{3,2,1,0:T(8,128)(2,1)}, bf16[8,16,8,648]{3,2,1,0:T(8,128)(2,1)}) custom-call(s32[6,2]{1,0:T(8,128)} %copy.35.steps_ref, f32[2,8,20,8,648]{4,3,2,1,0:T(8,128)} %bitcast.128, f32[2,20,8,648]{3,2,1,0:T(8,128)} %reshape_reshape.7.entering_ref, bf16[2,20,8,648]{3,2,1,0:T(8,128)(2,1)} %bitcast.24.before_ref, ...), custom_call_target="tpu_custom_call" | custom-call | flops 49766400 | bytes 9123840 | tf_op jit(solution)/shard_map/pallas_call | solution.py:120
  98.1 2.3 %fusion.24 = f32[1024,361]{0,1:T(8,128)S(1)} fusion(bf16[1024,648]{1,0:T(8,128)(2,1)} %bitcast.142, bf16[361,1296]{0,1:T(8,128)(2,1)S(1)} %copy-done.2), kind=kOutput, calls=%fused_computation.45 | convolution fusion | flops 479084544 | bytes 3303424 | tf_op jit(solution)/shard_map/dot_general | solution.py:174
  100.5 0.8 add_convert_fusion
  101.3 0.2 copy.48
  101.5 0.9 slice.181
  (36 shorter events, 0.6 us)
Async XLA Ops:
  0.0 6.0 %copy-start.4 = (f32[648]{0:T(1024)S(1)}, f32[648]{0:T(1024)}, u32[]{:S(2)}) copy-start(f32[648]{0:T(1024)} %param.12) | copy-start | bytes 7780
  0.0 10.9 %copy-start.3 = (bf16[1296,361]{1,0:T(8,128)(2,1)S(1)}, bf16[1296,361]{1,0:T(8,128)(2,1)}, u32[]{:S(2)}) copy-start(bf16[1296,361]{1,0:T(8,128)(2,1)} %param.10) | copy-start | bytes 2807140
  2.7 8.3 %collective-permute-start = (bf16[361,8,32]{0,2,1:T(8,128)(2,1)S(1)}, bf16[361,8,32]{0,2,1:T(8,128)(2,1)S(1)}, u32[]{:S(2)}, u32[]{:S(2)}) collective-permute-start(bf16[361,8,32]{0,2,1:T(8,128)(2,1)S(1)} %pad_maximum_fusion), channel_id=1, source_target_pairs={{0,1},{1,0},{2,3},{3,2},{4,5},{5,4},{6,7},{7,6},{8,9},{9,8},{10,11... | collective-permute-start | bytes 554504 | tf_op jit(solution)/shard_map/ppermute | solution.py:18
  14.1 3.1 %copy-start = (f32[2,8,160,648]{3,2,1,0:T(8,128)}, f32[2,8,160,648]{3,2,1,0:T(8,128)S(1)}, u32[]{:S(2)}) copy-start(f32[2,8,160,648]{3,2,1,0:T(8,128)S(1)} %maximum_multiply_fusion) | copy-start | bytes 19906564
  14.2 12.6 %collective-permute-start.1 = (bf16[2,160,648]{2,1,0:T(8,128)(2,1)S(1)}, bf16[2,160,648]{2,1,0:T(8,128)(2,1)}, u32[]{:S(2)}, u32[]{:S(2)}) collective-permute-start(bf16[2,160,648]{2,1,0:T(8,128)(2,1)S(1)} %fusion.20), channel_id=1, source_target_pairs={{0,2},{2,4},{4,6},{6,8},{8,10},{10,12},{12,14},{14,16},{16,18},{18... | collective-permute-start | bytes 1244168 | tf_op jit(solution)/shard_map/ppermute | solution.py:18
  29.0 23.4 %all-to-all-start = ((f32[64,8,512]{2,1,0:T(8,128)}), f32[64,8,512]{2,1,0:T(8,128)S(1)}, u32[]{:S(2)}, u32[]{:S(2)}) async-start(f32[64,8,512]{2,1,0:T(8,128)} %reshape.178), calls=%async_computation | async-start | bytes 2097152 | tf_op jit(solution)/shard_map/all_to_all | solution.py:63
  55.8 6.8 %copy-start.7 = (s32[6,2]{0,1:T(2,128)S(1)}, s32[6,2]{0,1:T(2,128)}, u32[]{:S(2)}) copy-start(s32[6,2]{0,1:T(2,128)} %param.15) | copy-start | bytes 148
  55.8 7.5 %copy-start.5 = (f32[648]{0:T(1024)S(1)}, f32[648]{0:T(1024)}, u32[]{:S(2)}) copy-start(f32[648]{0:T(1024)} %param.14) | copy-start | bytes 7780
  55.9 7.5 %copy-start.6 = (f32[648]{0:T(1024)S(1)}, f32[648]{0:T(1024)}, u32[]{:S(2)}) copy-start(f32[648]{0:T(1024)} %param.13) | copy-start | bytes 7780
  57.0 22.8 %all-to-all-start.1 = ((f32[64,8,512]{2,1,0:T(8,128)}), f32[64,8,512]{2,1,0:T(8,128)S(1)}, u32[]{:S(2)}, u32[]{:S(2)}) async-start(f32[64,8,512]{2,1,0:T(8,128)} %maximum_divide_fusion), calls=%async_computation.1 | async-start | bytes 2097152 | tf_op jit(solution)/shard_map/all_to_all | solution.py:69
  83.6 14.6 %copy-start.2 = (bf16[361,1296]{0,1:T(8,128)(2,1)S(1)}, bf16[361,1296]{0,1:T(8,128)(2,1)}, u32[]{:S(2)}) copy-start(bf16[361,1296]{0,1:T(8,128)(2,1)} %param.11) | copy-start | bytes 2807140
  98.1 2.3 %copy-start.1 = (bf16[8,16,8,648]{3,2,1,0:T(8,128)(2,1)S(1)}, bf16[8,16,8,648]{3,2,1,0:T(8,128)(2,1)}, u32[]{:S(2)}) copy-start(bf16[8,16,8,648]{3,2,1,0:T(8,128)(2,1)} %get-tuple-element.14) | copy-start | bytes 3981316

commit v15 on v12

--- a/solution.py
+++ b/solution.py
@@ -89,7 +89,7 @@
             field_ref[i, :, c] = up.astype(jnp.bfloat16).astype(jnp.float32)
         return carry
 
-    lax.fori_loop(0, ext_columns, build, 0)
+    lax.fori_loop(0, ext_columns, build, 0, unroll=4)
     for i in range(layers):
 
         def column(x, carry, i=i):

time: 101 us -> 101 us (level)
  no operation moved by 1% of the time
where the time goes in v15:
time: 101 us
  waiting for transfers between devices  39.5 us (39%)
  starting transfers between devices  18.3 us (18%)
  local copies, waits for them, and re-layouts  17.9 us (18%)
  Pallas kernels  14.7 us (15%)
  matrix products  5.54 us (5%)
  other arithmetic  4.62 us (5%)
    all_to_all x1, waiting for transfers between devices, entering_sums(): held = lax.all_to_all(spread(outgoing, 0.0), 'gz', 0, 0, tiled=True)  16.4 us
    all_to_all x1, waiting for transfers between devices, entering_sums(): back = lax.all_to_all(sums, 'gz', 0, 0, tiled=True)  15 us
    pallas_call x1, Pallas kernels, shift_layers(): pl.pallas_call(shift_kernel, out_shape=(half, half), in_specs=[smem] + [v...  14.7 us
    all_to_all x1, starting transfers between devices, entering_sums(): held = lax.all_to_all(spread(outgoing, 0.0), 'gz', 0, 0, tiled=True)  9.84 us
    ppermute x2, waiting for transfers between devices, from_behind(): return lax.ppermute(value, axis, pairs)  8.14 us
    unnamed x28, local copies, waits for them, and re-layouts  7.76 us
    all_to_all x1, starting transfers between devices, entering_sums(): back = lax.all_to_all(sums, 'gz', 0, 0, tiled=True)  4.96 us
    ppermute x2, starting transfers between devices, from_behind(): return lax.ppermute(value, axis, pairs)  3.45 us
  transfers between devices with their start and end apart: 4, of which 4 were waited for; matrix products, arithmetic and copies ran while one was open for 6% of the time, Pallas kernels for 0%

profile of v15, /device:TPU:0, one launch (start us, length us, event | category | flops | bytes accessed | tf_op | source)
XLA Modules:
  0.0 100.8 jit_solution(13406812500795443334)
XLA Ops:
  0.0 1.7 %copy.27 = bf16[361,8,128]{0,2,1:T(8,128)(2,1)S(1)} copy(bf16[361,8,128]{2,1,0:T(8,128)(2,1)} %param.8) | data formatting | bytes 1478656 | tf_op args[0]
  1.7 0.7 convert_element_type.23
  2.4 0.2 multiply_convert_fusion
  2.7 3.4 %collective-permute-start = (bf16[361,8,32]{0,2,1:T(8,128)(2,1)S(1)}, bf16[361,8,32]{0,2,1:T(8,128)(2,1)S(1)}, u32[]{:S(2)}, u32[]{:S(2)}) collective-permute-start(bf16[361,8,32]{0,2,1:T(8,128)(2,1)S(1)} %pad_maximum_fusion), channel_id=1, source_target_pairs={{0,1},{1,0},{2,3},{3,2},{4,5},{5,4},{6,7},{7,6},{8,9},{9,8},{10,11... | collective-permute-start | bytes 554504 | tf_op jit(solution)/shard_map/ppermute | solution.py:18
  6.0 4.9 %collective-permute-done = bf16[361,8,32]{0,2,1:T(8,128)(2,1)S(1)} collective-permute-done((bf16[361,8,32]{0,2,1:T(8,128)(2,1)S(1)}, bf16[361,8,32]{0,2,1:T(8,128)(2,1)S(1)}, u32[]{:S(2)}, u32[]{:S(2)}) %collective-permute-start) | collective-permute-done | bytes 184864 | tf_op jit(solution)/shard_map/ppermute | solution.py:18
  10.9 1.2 %convolution_bitcast_fusion.1 = f32[1,8,160,648]{3,2,1,0:T(8,128)S(1)} fusion(bf16[1296,361]{1,0:T(8,128)(2,1)S(1)} %copy-done.3, bf16[361,8,16]{0,2,1:T(8,128)(2,1)S(1)} %get-tuple-element.25, bf16[361,8,128]{0,2,1:T(8,128)(2,1)S(1)} %multiply_convert_fusion, bf16[361,8,16]{0,2,1:T(8,128)(2,1)S(1)} %get-tuple-element.24), kind=kOutput, calls=%fused_computation.2 | convolution fusion | flops 601628160 | bytes 4798464 | tf_op jit(solution)/shard_map/dot_general | solution.py:154
  12.2 1.2 %convolution_bitcast_fusion = f32[1,8,160,648]{3,2,1,0:T(8,128)S(1)} fusion(bf16[1296,361]{1,0:T(8,128)(2,1)S(1)} %copy-done.3, bf16[361,8,16]{0,2,1:T(8,128)(2,1)S(1)} %get-tuple-element.25, bf16[361,8,128]{0,2,1:T(8,128)(2,1)S(1)} %multiply_convert_fusion, bf16[361,8,16]{0,2,1:T(8,128)(2,1)S(1)} %get-tuple-element.24), kind=kOutput, calls=%fused_computation.1 | convolution fusion | flops 601628160 | bytes 4798464 | tf_op jit(solution)/shard_map/dot_general | solution.py:154
  13.4 0.8 maximum_multiply_fusion
  14.2 3.0 %copy-done = f32[2,8,160,648]{3,2,1,0:T(8,128)} copy-done((f32[2,8,160,648]{3,2,1,0:T(8,128)}, f32[2,8,160,648]{3,2,1,0:T(8,128)S(1)}, u32[]{:S(2)}) %copy-start) | copy-done | bytes 6635544
  17.2 0.5 fusion.7
  17.7 0.9 reshape.178
  18.6 0.1 pad.7
  18.7 1.2 %reshape.179 = f32[64,8,512]{2,1,0:T(8,128)} reshape(f32[262144]{0:T(1024)S(1)} %pad.7) | data formatting | bytes 2097152 | tf_op jit(solution)/shard_map/reshape | solution.py:61
  19.9 9.8 %all-to-all-start = ((f32[64,8,512]{2,1,0:T(8,128)}), f32[64,8,512]{2,1,0:T(8,128)S(1)}, u32[]{:S(2)}, u32[]{:S(2)}) async-start(f32[64,8,512]{2,1,0:T(8,128)} %reshape.179), calls=%async_computation | async-start | bytes 2097152 | tf_op jit(solution)/shard_map/all_to_all | solution.py:63
  29.8 0.9 reshape.181
  30.7 0.1 pad.8
  30.8 0.2 reshape_reshape.6
  31.0 0.2 subtract_reduce_fusion
  31.2 16.4 %all-to-all-done = f32[64,8,512]{2,1,0:T(8,128)S(1)} async-done(((f32[64,8,512]{2,1,0:T(8,128)}), f32[64,8,512]{2,1,0:T(8,128)S(1)}, u32[]{:S(2)}, u32[]{:S(2)}) %all-to-all-start) | async-done | bytes 1048608 | tf_op jit(solution)/shard_map/all_to_all | solution.py:63
  47.6 0.1 pad.30
  47.7 0.6 copy.45
  48.3 0.6 copy.43
  49.0 0.2 fusion
  49.1 0.2 fusion.1
  49.3 0.2 fusion.2
  49.6 0.1 fusion.3
  49.8 0.1 fusion.4
  49.9 0.1 fusion.32
  50.0 0.1 fusion.5
  50.2 0.6 copy.46
  50.9 1.2 %maximum_divide_fusion = f32[64,8,512]{2,1,0:T(8,128)} fusion(f32[63,8,512]{2,1,0:T(8,128)S(1)} %slice.185, f32[1,8,512]{2,1,0:T(8,128)S(1)} %concatenate.46, f32[8,512]{1,0:T(8,128)S(1)} %div.11), kind=kLoop, calls=%fused_computation.17 | loop fusion | flops 524288 | bytes 2113536 | tf_op jit(solution)/shard_map/div | solution.py:67
  52.1 5.0 %all-to-all-start.1 = ((f32[64,8,512]{2,1,0:T(8,128)}), f32[64,8,512]{2,1,0:T(8,128)S(1)}, u32[]{:S(2)}, u32[]{:S(2)}) async-start(f32[64,8,512]{2,1,0:T(8,128)} %maximum_divide_fusion), calls=%async_computation.1 | async-start | bytes 2097152 | tf_op jit(solution)/shard_map/all_to_all | solution.py:69
  57.1 0.6 broadcast_in_dim.9.factor_ref
  57.7 0.7 copy.35.steps_ref
  58.3 1.3 %fusion.27 = bf16[2,160,648]{2,1,0:T(8,128)(2,1)S(1)} fusion(f32[2,8,160,648]{3,2,1,0:T(8,128)} %copy-done), kind=kLoop, calls=%fused_computation.49 | loop fusion | bytes 829440 | tf_op jit(solution)/shard_map/convert_element_type | solution.py:164
  59.6 0.1 collective-permute-start.1
  59.7 0.2 fusion.28
  59.9 15.0 %all-to-all-done.1 = f32[64,8,512]{2,1,0:T(8,128)S(1)} async-done(((f32[64,8,512]{2,1,0:T(8,128)}), f32[64,8,512]{2,1,0:T(8,128)S(1)}, u32[]{:S(2)}, u32[]{:S(2)}) %all-to-all-start.1) | async-done | bytes 1048608 | tf_op jit(solution)/shard_map/all_to_all | solution.py:69
  74.9 0.3 copy.47
  75.2 2.0 %reshape_reshape.7.entering_ref = f32[2,20,8,648]{3,2,1,0:T(8,128)} reshape(f32[207360]{0:T(1024)S(1)} %slice.183) | data formatting | bytes 1658880 | tf_op jit(solution)/shard_map/reshape;reshape | solution.py:132
  77.2 3.3 %collective-permute-done.1 = bf16[2,160,648]{2,1,0:T(8,128)(2,1)S(1)} collective-permute-done((bf16[2,160,648]{2,1,0:T(8,128)(2,1)S(1)}, bf16[2,160,648]{2,1,0:T(8,128)(2,1)S(1)}, u32[]{:S(2)}, u32[]{:S(2)}) %collective-permute-start.1) | collective-permute-done | bytes 414752 | tf_op jit(solution)/shard_map/ppermute | solution.py:18
  80.5 0.7 broadcast_in_dim.10.cos_ref
  81.2 0.7 broadcast_in_dim.11.sin_ref
  81.9 14.7 %shard_map.82 = (bf16[8,16,8,648]{3,2,1,0:T(8,128)(2,1)}, bf16[8,16,8,648]{3,2,1,0:T(8,128)(2,1)}) custom-call(s32[6,2]{1,0:T(8,128)} %copy.35.steps_ref, f32[2,8,20,8,648]{4,3,2,1,0:T(8,128)} %bitcast.128, f32[2,20,8,648]{3,2,1,0:T(8,128)} %reshape_reshape.7.entering_ref, bf16[2,20,8,648]{3,2,1,0:T(8,128)(2,1)} %bitcast.143, ...), custom_call_target="tpu_custom_call" | custom-call | flops 49766400 | bytes 9123840 | tf_op jit(solution)/shard_map/pallas_call | solution.py:120
  96.6 2.3 %fusion.22 = f32[1024,361]{0,1:T(8,128)S(1)} fusion(bf16[1024,648]{1,0:T(8,128)(2,1)} %bitcast.142, bf16[361,1296]{0,1:T(8,128)(2,1)S(1)} %copy-done.2), kind=kOutput, calls=%fused_computation.44 | convolution fusion | flops 479084544 | bytes 3303424 | tf_op jit(solution)/shard_map/dot_general | solution.py:174
  98.9 0.8 add_convert_fusion
  99.8 0.2 copy.48
  99.9 0.9 slice.186
  (38 shorter events, 0.6 us)
Async XLA Ops:
  0.0 6.0 %copy-start.5 = (f32[648]{0:T(1024)S(1)}, f32[648]{0:T(1024)}, u32[]{:S(2)}) copy-start(f32[648]{0:T(1024)} %param.12) | copy-start | bytes 7780
  0.0 10.9 %copy-start.3 = (bf16[1296,361]{1,0:T(8,128)(2,1)S(1)}, bf16[1296,361]{1,0:T(8,128)(2,1)}, u32[]{:S(2)}) copy-start(bf16[1296,361]{1,0:T(8,128)(2,1)} %param.10) | copy-start | bytes 2807140
  2.7 8.3 %collective-permute-start = (bf16[361,8,32]{0,2,1:T(8,128)(2,1)S(1)}, bf16[361,8,32]{0,2,1:T(8,128)(2,1)S(1)}, u32[]{:S(2)}, u32[]{:S(2)}) collective-permute-start(bf16[361,8,32]{0,2,1:T(8,128)(2,1)S(1)} %pad_maximum_fusion), channel_id=1, source_target_pairs={{0,1},{1,0},{2,3},{3,2},{4,5},{5,4},{6,7},{7,6},{8,9},{9,8},{10,11... | collective-permute-start | bytes 554504 | tf_op jit(solution)/shard_map/ppermute | solution.py:18
  14.1 3.0 %copy-start = (f32[2,8,160,648]{3,2,1,0:T(8,128)}, f32[2,8,160,648]{3,2,1,0:T(8,128)S(1)}, u32[]{:S(2)}) copy-start(f32[2,8,160,648]{3,2,1,0:T(8,128)S(1)} %maximum_multiply_fusion) | copy-start | bytes 19906564
  19.9 27.7 %all-to-all-start = ((f32[64,8,512]{2,1,0:T(8,128)}), f32[64,8,512]{2,1,0:T(8,128)S(1)}, u32[]{:S(2)}, u32[]{:S(2)}) async-start(f32[64,8,512]{2,1,0:T(8,128)} %reshape.179), calls=%async_computation | async-start | bytes 2097152 | tf_op jit(solution)/shard_map/all_to_all | solution.py:63
  50.9 6.8 %copy-start.8 = (s32[6,2]{0,1:T(2,128)S(1)}, s32[6,2]{0,1:T(2,128)}, u32[]{:S(2)}) copy-start(s32[6,2]{0,1:T(2,128)} %param.15) | copy-start | bytes 148
  52.1 7.6 %copy-start.6 = (f32[648]{0:T(1024)S(1)}, f32[648]{0:T(1024)}, u32[]{:S(2)}) copy-start(f32[648]{0:T(1024)} %param.14) | copy-start | bytes 7780
  52.1 7.6 %copy-start.7 = (f32[648]{0:T(1024)S(1)}, f32[648]{0:T(1024)}, u32[]{:S(2)}) copy-start(f32[648]{0:T(1024)} %param.13) | copy-start | bytes 7780
  52.1 22.8 %all-to-all-start.1 = ((f32[64,8,512]{2,1,0:T(8,128)}), f32[64,8,512]{2,1,0:T(8,128)S(1)}, u32[]{:S(2)}, u32[]{:S(2)}) async-start(f32[64,8,512]{2,1,0:T(8,128)} %maximum_divide_fusion), calls=%async_computation.1 | async-start | bytes 2097152 | tf_op jit(solution)/shard_map/all_to_all | solution.py:69
  59.6 20.9 %collective-permute-start.1 = (bf16[2,160,648]{2,1,0:T(8,128)(2,1)S(1)}, bf16[2,160,648]{2,1,0:T(8,128)(2,1)S(1)}, u32[]{:S(2)}, u32[]{:S(2)}) collective-permute-start(bf16[2,160,648]{2,1,0:T(8,128)(2,1)S(1)} %fusion.27), channel_id=1, source_target_pairs={{0,2},{2,4},{4,6},{6,8},{8,10},{10,12},{12,14},{14,16},{16,18},{18... | collective-permute-start | bytes 1244168 | tf_op jit(solution)/shard_map/ppermute | solution.py:18
  80.5 1.4 %copy-start.4 = (bf16[2,160,648]{2,1,0:T(8,128)(2,1)}, bf16[2,160,648]{2,1,0:T(8,128)(2,1)S(1)}, u32[]{:S(2)}) copy-start(bf16[2,160,648]{2,1,0:T(8,128)(2,1)S(1)} %collective-permute-done.1) | copy-start | bytes 1244164
  81.9 14.7 %copy-start.2 = (bf16[361,1296]{0,1:T(8,128)(2,1)S(1)}, bf16[361,1296]{0,1:T(8,128)(2,1)}, u32[]{:S(2)}) copy-start(bf16[361,1296]{0,1:T(8,128)(2,1)} %param.11) | copy-start | bytes 2807140
  96.6 2.3 %copy-start.1 = (bf16[8,16,8,648]{3,2,1,0:T(8,128)(2,1)S(1)}, bf16[8,16,8,648]{3,2,1,0:T(8,128)(2,1)}, u32[]{:S(2)}) copy-start(bf16[8,16,8,648]{3,2,1,0:T(8,128)(2,1)} %get-tuple-element.11) | copy-start | bytes 3981316

commit v16 on v13

--- a/solution.py
+++ b/solution.py
@@ -106,7 +106,7 @@
             imag_ref[i, x] = acc_imag.astype(imag_ref.dtype)
             return carry
 
-        lax.fori_loop(0, columns, column, 0, unroll=8)
+        lax.fori_loop(0, columns, column, 0, unroll=16)
 
 
 def shift_layers(offsets, box_terms, entering, before_term, rate, wave_x, wave_y, columns):

time: 101 us -> 101 us (level)
  no operation moved by 1% of the time
where the time goes in v16:
time: 101 us; the launch traced here: 100 us
  waiting for transfers between devices  39.5 us (39%)
  starting transfers between devices  18.3 us (18%)
  local copies, waits for them, and re-layouts  17.9 us (18%)
  Pallas kernels  13.9 us (14%)
  matrix products  5.54 us (5%)
  other arithmetic  4.62 us (5%)
    all_to_all x1, waiting for transfers between devices, entering_sums(): held = lax.all_to_all(spread(outgoing, 0.0), 'gz', 0, 0, tiled=True)  16.4 us
    all_to_all x1, waiting for transfers between devices, entering_sums(): back = lax.all_to_all(sums, 'gz', 0, 0, tiled=True)  15 us
    pallas_call x1, Pallas kernels, shift_layers(): pl.pallas_call(shift_kernel, out_shape=(half, half), in_specs=[smem] + [v...  13.9 us
    all_to_all x1, starting transfers between devices, entering_sums(): held = lax.all_to_all(spread(outgoing, 0.0), 'gz', 0, 0, tiled=True)  9.84 us
    ppermute x2, waiting for transfers between devices, from_behind(): return lax.ppermute(value, axis, pairs)  8.14 us
    unnamed x28, local copies, waits for them, and re-layouts  7.76 us
    all_to_all x1, starting transfers between devices, entering_sums(): back = lax.all_to_all(sums, 'gz', 0, 0, tiled=True)  4.96 us
    ppermute x2, starting transfers between devices, from_behind(): return lax.ppermute(value, axis, pairs)  3.45 us
  transfers between devices with their start and end apart: 4, of which 4 were waited for; matrix products, arithmetic and copies ran while one was open for 6% of the time, Pallas kernels for 0%

profile of v16, /device:TPU:0, one launch (start us, length us, event | category | flops | bytes accessed | tf_op | source)
XLA Modules:
  0.0 100.1 jit_solution(7734893740395585531)
XLA Ops:
  0.0 1.7 %copy.27 = bf16[361,8,128]{0,2,1:T(8,128)(2,1)S(1)} copy(bf16[361,8,128]{2,1,0:T(8,128)(2,1)} %param.8) | data formatting | bytes 1478656 | tf_op args[0]
  1.7 0.7 convert_element_type.23
  2.4 0.2 multiply_convert_fusion
  2.7 3.4 %collective-permute-start = (bf16[361,8,32]{0,2,1:T(8,128)(2,1)S(1)}, bf16[361,8,32]{0,2,1:T(8,128)(2,1)S(1)}, u32[]{:S(2)}, u32[]{:S(2)}) collective-permute-start(bf16[361,8,32]{0,2,1:T(8,128)(2,1)S(1)} %pad_maximum_fusion), channel_id=1, source_target_pairs={{0,1},{1,0},{2,3},{3,2},{4,5},{5,4},{6,7},{7,6},{8,9},{9,8},{10,11... | collective-permute-start | bytes 554504 | tf_op jit(solution)/shard_map/ppermute | solution.py:18
  6.0 4.9 %collective-permute-done = bf16[361,8,32]{0,2,1:T(8,128)(2,1)S(1)} collective-permute-done((bf16[361,8,32]{0,2,1:T(8,128)(2,1)S(1)}, bf16[361,8,32]{0,2,1:T(8,128)(2,1)S(1)}, u32[]{:S(2)}, u32[]{:S(2)}) %collective-permute-start) | collective-permute-done | bytes 184864 | tf_op jit(solution)/shard_map/ppermute | solution.py:18
  10.9 1.2 %convolution_bitcast_fusion.1 = f32[1,8,160,648]{3,2,1,0:T(8,128)S(1)} fusion(bf16[1296,361]{1,0:T(8,128)(2,1)S(1)} %copy-done.3, bf16[361,8,16]{0,2,1:T(8,128)(2,1)S(1)} %get-tuple-element.25, bf16[361,8,128]{0,2,1:T(8,128)(2,1)S(1)} %multiply_convert_fusion, bf16[361,8,16]{0,2,1:T(8,128)(2,1)S(1)} %get-tuple-element.24), kind=kOutput, calls=%fused_computation.2 | convolution fusion | flops 601628160 | bytes 4798464 | tf_op jit(solution)/shard_map/dot_general | solution.py:154
  12.2 1.2 %convolution_bitcast_fusion = f32[1,8,160,648]{3,2,1,0:T(8,128)S(1)} fusion(bf16[1296,361]{1,0:T(8,128)(2,1)S(1)} %copy-done.3, bf16[361,8,16]{0,2,1:T(8,128)(2,1)S(1)} %get-tuple-element.25, bf16[361,8,128]{0,2,1:T(8,128)(2,1)S(1)} %multiply_convert_fusion, bf16[361,8,16]{0,2,1:T(8,128)(2,1)S(1)} %get-tuple-element.24), kind=kOutput, calls=%fused_computation.1 | convolution fusion | flops 601628160 | bytes 4798464 | tf_op jit(solution)/shard_map/dot_general | solution.py:154
  13.4 0.8 maximum_multiply_fusion
  14.2 3.0 %copy-done = f32[2,8,160,648]{3,2,1,0:T(8,128)} copy-done((f32[2,8,160,648]{3,2,1,0:T(8,128)}, f32[2,8,160,648]{3,2,1,0:T(8,128)S(1)}, u32[]{:S(2)}) %copy-start) | copy-done | bytes 6635544
  17.2 0.5 fusion.7
  17.7 0.9 reshape.178
  18.6 0.1 pad.7
  18.7 1.2 %reshape.179 = f32[64,8,512]{2,1,0:T(8,128)} reshape(f32[262144]{0:T(1024)S(1)} %pad.7) | data formatting | bytes 2097152 | tf_op jit(solution)/shard_map/reshape | solution.py:61
  19.9 9.8 %all-to-all-start = ((f32[64,8,512]{2,1,0:T(8,128)}), f32[64,8,512]{2,1,0:T(8,128)S(1)}, u32[]{:S(2)}, u32[]{:S(2)}) async-start(f32[64,8,512]{2,1,0:T(8,128)} %reshape.179), calls=%async_computation | async-start | bytes 2097152 | tf_op jit(solution)/shard_map/all_to_all | solution.py:63
  29.8 0.9 reshape.181
  30.7 0.1 pad.8
  30.8 0.2 reshape_reshape.6
  31.0 0.2 subtract_reduce_fusion
  31.2 16.4 %all-to-all-done = f32[64,8,512]{2,1,0:T(8,128)S(1)} async-done(((f32[64,8,512]{2,1,0:T(8,128)}), f32[64,8,512]{2,1,0:T(8,128)S(1)}, u32[]{:S(2)}, u32[]{:S(2)}) %all-to-all-start) | async-done | bytes 1048608 | tf_op jit(solution)/shard_map/all_to_all | solution.py:63
  47.6 0.1 pad.30
  47.7 0.6 copy.45
  48.3 0.6 copy.43
  49.0 0.2 fusion
  49.1 0.2 fusion.1
  49.3 0.2 fusion.2
  49.6 0.1 fusion.3
  49.8 0.1 fusion.4
  49.9 0.1 fusion.32
  50.0 0.1 fusion.5
  50.2 0.6 copy.46
  50.9 1.2 %maximum_divide_fusion = f32[64,8,512]{2,1,0:T(8,128)} fusion(f32[63,8,512]{2,1,0:T(8,128)S(1)} %slice.185, f32[1,8,512]{2,1,0:T(8,128)S(1)} %concatenate.46, f32[8,512]{1,0:T(8,128)S(1)} %div.11), kind=kLoop, calls=%fused_computation.17 | loop fusion | flops 524288 | bytes 2113536 | tf_op jit(solution)/shard_map/div | solution.py:67
  52.1 5.0 %all-to-all-start.1 = ((f32[64,8,512]{2,1,0:T(8,128)}), f32[64,8,512]{2,1,0:T(8,128)S(1)}, u32[]{:S(2)}, u32[]{:S(2)}) async-start(f32[64,8,512]{2,1,0:T(8,128)} %maximum_divide_fusion), calls=%async_computation.1 | async-start | bytes 2097152 | tf_op jit(solution)/shard_map/all_to_all | solution.py:69
  57.1 0.6 broadcast_in_dim.9.factor_ref
  57.7 0.7 copy.35.steps_ref
  58.3 1.3 %fusion.27 = bf16[2,160,648]{2,1,0:T(8,128)(2,1)S(1)} fusion(f32[2,8,160,648]{3,2,1,0:T(8,128)} %copy-done), kind=kLoop, calls=%fused_computation.49 | loop fusion | bytes 829440 | tf_op jit(solution)/shard_map/convert_element_type | solution.py:164
  59.6 0.1 collective-permute-start.1
  59.7 0.2 fusion.28
  59.9 15.0 %all-to-all-done.1 = f32[64,8,512]{2,1,0:T(8,128)S(1)} async-done(((f32[64,8,512]{2,1,0:T(8,128)}), f32[64,8,512]{2,1,0:T(8,128)S(1)}, u32[]{:S(2)}, u32[]{:S(2)}) %all-to-all-start.1) | async-done | bytes 1048608 | tf_op jit(solution)/shard_map/all_to_all | solution.py:69
  74.9 0.3 copy.47
  75.2 2.0 %reshape_reshape.7.entering_ref = f32[2,20,8,648]{3,2,1,0:T(8,128)} reshape(f32[207360]{0:T(1024)S(1)} %slice.183) | data formatting | bytes 1658880 | tf_op jit(solution)/shard_map/reshape;reshape | solution.py:132
  77.2 3.3 %collective-permute-done.1 = bf16[2,160,648]{2,1,0:T(8,128)(2,1)S(1)} collective-permute-done((bf16[2,160,648]{2,1,0:T(8,128)(2,1)S(1)}, bf16[2,160,648]{2,1,0:T(8,128)(2,1)S(1)}, u32[]{:S(2)}, u32[]{:S(2)}) %collective-permute-start.1) | collective-permute-done | bytes 414752 | tf_op jit(solution)/shard_map/ppermute | solution.py:18
  80.5 0.7 broadcast_in_dim.10.cos_ref
  81.2 0.7 broadcast_in_dim.11.sin_ref
  81.9 13.9 %shard_map.82 = (bf16[8,16,8,648]{3,2,1,0:T(8,128)(2,1)}, bf16[8,16,8,648]{3,2,1,0:T(8,128)(2,1)}) custom-call(s32[6,2]{1,0:T(8,128)} %copy.35.steps_ref, f32[2,8,20,8,648]{4,3,2,1,0:T(8,128)} %bitcast.128, f32[2,20,8,648]{3,2,1,0:T(8,128)} %reshape_reshape.7.entering_ref, bf16[2,20,8,648]{3,2,1,0:T(8,128)(2,1)} %bitcast.143, ...), custom_call_target="tpu_custom_call" | custom-call | flops 49766400 | bytes 9123840 | tf_op jit(solution)/shard_map/pallas_call | solution.py:120
  95.9 2.3 %fusion.22 = f32[1024,361]{0,1:T(8,128)S(1)} fusion(bf16[1024,648]{1,0:T(8,128)(2,1)} %bitcast.142, bf16[361,1296]{0,1:T(8,128)(2,1)S(1)} %copy-done.2), kind=kOutput, calls=%fused_computation.44 | convolution fusion | flops 479084544 | bytes 3303424 | tf_op jit(solution)/shard_map/dot_general | solution.py:174
  98.2 0.8 add_convert_fusion
  99.0 0.2 copy.48
  99.2 0.9 slice.186
  (38 shorter events, 0.6 us)
Async XLA Ops:
  0.0 6.0 %copy-start.5 = (f32[648]{0:T(1024)S(1)}, f32[648]{0:T(1024)}, u32[]{:S(2)}) copy-start(f32[648]{0:T(1024)} %param.12) | copy-start | bytes 7780
  0.0 10.9 %copy-start.3 = (bf16[1296,361]{1,0:T(8,128)(2,1)S(1)}, bf16[1296,361]{1,0:T(8,128)(2,1)}, u32[]{:S(2)}) copy-start(bf16[1296,361]{1,0:T(8,128)(2,1)} %param.10) | copy-start | bytes 2807140
  2.7 8.3 %collective-permute-start = (bf16[361,8,32]{0,2,1:T(8,128)(2,1)S(1)}, bf16[361,8,32]{0,2,1:T(8,128)(2,1)S(1)}, u32[]{:S(2)}, u32[]{:S(2)}) collective-permute-start(bf16[361,8,32]{0,2,1:T(8,128)(2,1)S(1)} %pad_maximum_fusion), channel_id=1, source_target_pairs={{0,1},{1,0},{2,3},{3,2},{4,5},{5,4},{6,7},{7,6},{8,9},{9,8},{10,11... | collective-permute-start | bytes 554504 | tf_op jit(solution)/shard_map/ppermute | solution.py:18
  14.1 3.0 %copy-start = (f32[2,8,160,648]{3,2,1,0:T(8,128)}, f32[2,8,160,648]{3,2,1,0:T(8,128)S(1)}, u32[]{:S(2)}) copy-start(f32[2,8,160,648]{3,2,1,0:T(8,128)S(1)} %maximum_multiply_fusion) | copy-start | bytes 19906564
  19.9 27.7 %all-to-all-start = ((f32[64,8,512]{2,1,0:T(8,128)}), f32[64,8,512]{2,1,0:T(8,128)S(1)}, u32[]{:S(2)}, u32[]{:S(2)}) async-start(f32[64,8,512]{2,1,0:T(8,128)} %reshape.179), calls=%async_computation | async-start | bytes 2097152 | tf_op jit(solution)/shard_map/all_to_all | solution.py:63
  50.9 6.8 %copy-start.8 = (s32[6,2]{0,1:T(2,128)S(1)}, s32[6,2]{0,1:T(2,128)}, u32[]{:S(2)}) copy-start(s32[6,2]{0,1:T(2,128)} %param.15) | copy-start | bytes 148
  52.1 7.6 %copy-start.6 = (f32[648]{0:T(1024)S(1)}, f32[648]{0:T(1024)}, u32[]{:S(2)}) copy-start(f32[648]{0:T(1024)} %param.14) | copy-start | bytes 7780
  52.1 7.6 %copy-start.7 = (f32[648]{0:T(1024)S(1)}, f32[648]{0:T(1024)}, u32[]{:S(2)}) copy-start(f32[648]{0:T(1024)} %param.13) | copy-start | bytes 7780
  52.1 22.8 %all-to-all-start.1 = ((f32[64,8,512]{2,1,0:T(8,128)}), f32[64,8,512]{2,1,0:T(8,128)S(1)}, u32[]{:S(2)}, u32[]{:S(2)}) async-start(f32[64,8,512]{2,1,0:T(8,128)} %maximum_divide_fusion), calls=%async_computation.1 | async-start | bytes 2097152 | tf_op jit(solution)/shard_map/all_to_all | solution.py:69
  59.6 20.9 %collective-permute-start.1 = (bf16[2,160,648]{2,1,0:T(8,128)(2,1)S(1)}, bf16[2,160,648]{2,1,0:T(8,128)(2,1)S(1)}, u32[]{:S(2)}, u32[]{:S(2)}) collective-permute-start(bf16[2,160,648]{2,1,0:T(8,128)(2,1)S(1)} %fusion.27), channel_id=1, source_target_pairs={{0,2},{2,4},{4,6},{6,8},{8,10},{10,12},{12,14},{14,16},{16,18},{18... | collective-permute-start | bytes 1244168 | tf_op jit(solution)/shard_map/ppermute | solution.py:18
  80.5 1.4 %copy-start.4 = (bf16[2,160,648]{2,1,0:T(8,128)(2,1)}, bf16[2,160,648]{2,1,0:T(8,128)(2,1)S(1)}, u32[]{:S(2)}) copy-start(bf16[2,160,648]{2,1,0:T(8,128)(2,1)S(1)} %collective-permute-done.1) | copy-start | bytes 1244164
  81.9 13.9 %copy-start.2 = (bf16[361,1296]{0,1:T(8,128)(2,1)S(1)}, bf16[361,1296]{0,1:T(8,128)(2,1)}, u32[]{:S(2)}) copy-start(bf16[361,1296]{0,1:T(8,128)(2,1)} %param.11) | copy-start | bytes 2807140
  95.8 2.3 %copy-start.1 = (bf16[8,16,8,648]{3,2,1,0:T(8,128)(2,1)S(1)}, bf16[8,16,8,648]{3,2,1,0:T(8,128)(2,1)}, u32[]{:S(2)}) copy-start(bf16[8,16,8,648]{3,2,1,0:T(8,128)(2,1)} %get-tuple-element.11) | copy-start | bytes 3981316

commit v17 on v12

--- a/solution.py
+++ b/solution.py
@@ -154,8 +154,8 @@
         expansion = lax.dot_general(
             multipole, rows, (((0,), (1,)), ((), ())), preferred_element_type=jnp.float32
         )
-        halves.append(expansion.reshape(layers, ext_boxes, half_rows))
-    box_terms = weight * jnp.stack(halves)
+        halves.append(weight[0] * expansion.reshape(layers, ext_boxes, half_rows))
+    box_terms = jnp.stack(halves)
 
     outgoing = box_terms[:, layers - 1]
     for j in range(layers - 1):

time: 101 us -> 101 us (level)
  other arithmetic: 4.62 us -> 7.77 us
  local copies, waits for them, and re-layouts: 17.9 us -> 14.8 us
    another operation x0 -> x1, other arithmetic: none -> 3.89 us  [body(): box_terms = jnp.stack(halves)]
    unnamed x28 -> x26, local copies, waits for them, and re-layouts: 7.76 us -> 4.72 us
where the time goes in v17:
time: 101 us
  waiting for transfers between devices  39.5 us (39%)
  starting transfers between devices  18.4 us (18%)
  local copies, waits for them, and re-layouts  14.8 us (15%)
  Pallas kernels  14.4 us (14%)
  other arithmetic  7.77 us (8%)
  matrix products  5.56 us (6%)
    all_to_all x1, waiting for transfers between devices, entering_sums(): held = lax.all_to_all(spread(outgoing, 0.0), 'gz', 0, 0, tiled=True)  16.4 us
    all_to_all x1, waiting for transfers between devices, entering_sums(): back = lax.all_to_all(sums, 'gz', 0, 0, tiled=True)  15 us
    pallas_call x1, Pallas kernels, shift_layers(): pl.pallas_call(shift_kernel, out_shape=(half, half), in_specs=[smem] + [v...  14.4 us
    all_to_all x1, starting transfers between devices, entering_sums(): held = lax.all_to_all(spread(outgoing, 0.0), 'gz', 0, 0, tiled=True)  9.84 us
    ppermute x2, waiting for transfers between devices, from_behind(): return lax.ppermute(value, axis, pairs)  8.14 us
    all_to_all x1, starting transfers between devices, entering_sums(): back = lax.all_to_all(sums, 'gz', 0, 0, tiled=True)  5.12 us
    unnamed x26, local copies, waits for them, and re-layouts  4.72 us
    another operation x1, other arithmetic, body(): box_terms = jnp.stack(halves)  3.89 us
  transfers between devices with their start and end apart: 4, of which 4 were waited for; matrix products, arithmetic and copies ran while one was open for 6% of the time, Pallas kernels for 0%

profile of v17, /device:TPU:0, one launch (start us, length us, event | category | flops | bytes accessed | tf_op | source)
XLA Modules:
  0.0 100.9 jit_solution(6680954932721929141)
XLA Ops:
  0.0 1.7 %copy.27 = bf16[361,8,128]{0,2,1:T(8,128)(2,1)S(1)} copy(bf16[361,8,128]{2,1,0:T(8,128)(2,1)} %param.8) | data formatting | bytes 1478656 | tf_op args[0]
  1.7 0.7 convert_element_type.23
  2.4 0.2 multiply_convert_fusion
  2.7 3.4 %collective-permute-start = (bf16[361,8,32]{0,2,1:T(8,128)(2,1)S(1)}, bf16[361,8,32]{0,2,1:T(8,128)(2,1)S(1)}, u32[]{:S(2)}, u32[]{:S(2)}) collective-permute-start(bf16[361,8,32]{0,2,1:T(8,128)(2,1)S(1)} %pad_maximum_fusion.1), channel_id=1, source_target_pairs={{0,1},{1,0},{2,3},{3,2},{4,5},{5,4},{6,7},{7,6},{8,9},{9,8},{10,11... | collective-permute-start | bytes 554504 | tf_op jit(solution)/shard_map/ppermute | solution.py:18
  6.0 4.9 %collective-permute-done = bf16[361,8,32]{0,2,1:T(8,128)(2,1)S(1)} collective-permute-done((bf16[361,8,32]{0,2,1:T(8,128)(2,1)S(1)}, bf16[361,8,32]{0,2,1:T(8,128)(2,1)S(1)}, u32[]{:S(2)}, u32[]{:S(2)}) %collective-permute-start) | collective-permute-done | bytes 184864 | tf_op jit(solution)/shard_map/ppermute | solution.py:18
  10.9 1.2 %multiply_bitcast_fusion = f32[1,8,160,648]{3,2,1,0:T(8,128)S(1)} fusion(f32[648]{0:T(1024)S(1)} %get-tuple-element.29, bf16[1296,361]{1,0:T(8,128)(2,1)S(1)} %copy-done.7, bf16[361,8,16]{0,2,1:T(8,128)(2,1)S(1)} %get-tuple-element.25, bf16[361,8,128]{0,2,1:T(8,128)(2,1)S(1)} %multiply_convert_fusion, bf16[361,8,16]{0,2,1:T(8,128)(2,1)S(1)} %get-tuple-element.24), kind=kOutput, calls=%fused_computation.17 | convolution fusion | flops 602457600 | bytes 4802560 | tf_op jit(solution)/shard_map/dot_general | solution.py:154
  12.2 1.2 %multiply_bitcast_fusion.1 = f32[1,8,160,648]{3,2,1,0:T(8,128)S(1)} fusion(f32[648]{0:T(1024)S(1)} %get-tuple-element.29, bf16[1296,361]{1,0:T(8,128)(2,1)S(1)} %copy-done.7, bf16[361,8,16]{0,2,1:T(8,128)(2,1)S(1)} %get-tuple-element.25, bf16[361,8,128]{0,2,1:T(8,128)(2,1)S(1)} %multiply_convert_fusion, bf16[361,8,16]{0,2,1:T(8,128)(2,1)S(1)} %get-tuple-element.24), kind=kOutput, calls=%fused_computation.18 | convolution fusion | flops 602457600 | bytes 4802560 | tf_op jit(solution)/shard_map/dot_general | solution.py:154
  13.4 3.9 %pad_maximum_fusion = f32[2,8,160,648]{3,2,1,0:T(8,128)} fusion(f32[1,8,160,648]{3,2,1,0:T(8,128)S(1)} %multiply_bitcast_fusion, f32[1,8,160,648]{3,2,1,0:T(8,128)S(1)} %multiply_bitcast_fusion.1), kind=kLoop, calls=%fused_computation.8 | loop fusion | flops 1658880 | bytes 13271040 | tf_op jit(solution)/shard_map/stack | solution.py:158
  17.3 0.6 fusion.14
  17.8 0.9 reshape.172
  18.7 0.1 pad.7
  18.8 1.2 %reshape.173 = f32[64,8,512]{2,1,0:T(8,128)} reshape(f32[262144]{0:T(1024)S(1)} %pad.7) | data formatting | bytes 2097152 | tf_op jit(solution)/shard_map/reshape | solution.py:61
  20.0 9.8 %all-to-all-start = ((f32[64,8,512]{2,1,0:T(8,128)}), f32[64,8,512]{2,1,0:T(8,128)S(1)}, u32[]{:S(2)}, u32[]{:S(2)}) async-start(f32[64,8,512]{2,1,0:T(8,128)} %reshape.173), calls=%async_computation | async-start | bytes 2097152 | tf_op jit(solution)/shard_map/all_to_all | solution.py:63
  29.9 0.9 reshape.175
  30.8 0.1 pad.8
  30.9 0.2 reshape_reshape.6
  31.1 0.2 subtract_reduce_fusion
  31.3 16.4 %all-to-all-done = f32[64,8,512]{2,1,0:T(8,128)S(1)} async-done(((f32[64,8,512]{2,1,0:T(8,128)}), f32[64,8,512]{2,1,0:T(8,128)S(1)}, u32[]{:S(2)}, u32[]{:S(2)}) %all-to-all-start) | async-done | bytes 1048608 | tf_op jit(solution)/shard_map/all_to_all | solution.py:63
  47.7 0.1 pad.30
  47.8 0.6 copy.45
  48.4 0.6 copy.43
  49.1 0.2 fusion
  49.3 0.2 fusion.1
  49.5 0.2 fusion.2
  49.7 0.1 fusion.3
  49.9 0.1 fusion.4
  50.1 0.1 fusion.48
  50.1 0.1 fusion.5
  50.3 0.6 copy.46
  50.9 0.1 slice.193
  51.0 1.2 %maximum_divide_fusion = f32[64,8,512]{2,1,0:T(8,128)} fusion(f32[63,8,512]{2,1,0:T(8,128)S(1)} %slice.193, f32[1,8,512]{2,1,0:T(8,128)S(1)} %concatenate.46, f32[8,512]{1,0:T(8,128)S(1)} %div.11), kind=kLoop, calls=%fused_computation.33 | loop fusion | flops 524288 | bytes 2113536 | tf_op jit(solution)/shard_map/div | solution.py:67
  52.2 5.1 %all-to-all-start.1 = ((f32[64,8,512]{2,1,0:T(8,128)}), f32[64,8,512]{2,1,0:T(8,128)S(1)}, u32[]{:S(2)}, u32[]{:S(2)}) async-start(f32[64,8,512]{2,1,0:T(8,128)} %maximum_divide_fusion), calls=%async_computation.1 | async-start | bytes 2097152 | tf_op jit(solution)/shard_map/all_to_all | solution.py:69
  57.4 0.6 broadcast_in_dim.9.factor_ref
  57.9 0.7 copy.35.steps_ref
  58.6 1.3 %fusion.43 = bf16[2,160,648]{2,1,0:T(8,128)(2,1)S(1)} fusion(f32[2,8,160,648]{3,2,1,0:T(8,128)} %pad_maximum_fusion), kind=kLoop, calls=%fused_computation.73 | loop fusion | bytes 829440 | tf_op jit(solution)/shard_map/convert_element_type | solution.py:164
  59.9 0.1 collective-permute-start.1
  60.0 0.2 fusion.44
  60.2 15.0 %all-to-all-done.1 = f32[64,8,512]{2,1,0:T(8,128)S(1)} async-done(((f32[64,8,512]{2,1,0:T(8,128)}), f32[64,8,512]{2,1,0:T(8,128)S(1)}, u32[]{:S(2)}, u32[]{:S(2)}) %all-to-all-start.1) | async-done | bytes 1048608 | tf_op jit(solution)/shard_map/all_to_all | solution.py:69
  75.2 0.3 copy.47
  75.5 2.0 %reshape_reshape.7.entering_ref = f32[2,20,8,648]{3,2,1,0:T(8,128)} reshape(f32[207360]{0:T(1024)S(1)} %slice.191) | data formatting | bytes 1658880 | tf_op jit(solution)/shard_map/reshape;reshape | solution.py:132
  77.5 3.3 %collective-permute-done.1 = bf16[2,160,648]{2,1,0:T(8,128)(2,1)S(1)} collective-permute-done((bf16[2,160,648]{2,1,0:T(8,128)(2,1)S(1)}, bf16[2,160,648]{2,1,0:T(8,128)(2,1)S(1)}, u32[]{:S(2)}, u32[]{:S(2)}) %collective-permute-start.1) | collective-permute-done | bytes 414752 | tf_op jit(solution)/shard_map/ppermute | solution.py:18
  80.8 0.7 broadcast_in_dim.10.cos_ref
  81.5 0.7 broadcast_in_dim.11.sin_ref
  82.2 14.4 %shard_map.82 = (bf16[8,16,8,648]{3,2,1,0:T(8,128)(2,1)}, bf16[8,16,8,648]{3,2,1,0:T(8,128)(2,1)}) custom-call(s32[6,2]{1,0:T(8,128)} %copy.35.steps_ref, f32[2,8,20,8,648]{4,3,2,1,0:T(8,128)} %bitcast.128, f32[2,20,8,648]{3,2,1,0:T(8,128)} %reshape_reshape.7.entering_ref, bf16[2,20,8,648]{3,2,1,0:T(8,128)(2,1)} %bitcast.143, ...), custom_call_target="tpu_custom_call" | custom-call | flops 49766400 | bytes 9123840 | tf_op jit(solution)/shard_map/pallas_call | solution.py:120
  96.6 2.3 %fusion.38 = f32[1024,361]{0,1:T(8,128)S(1)} fusion(bf16[1024,648]{1,0:T(8,128)(2,1)} %bitcast.142, bf16[361,1296]{0,1:T(8,128)(2,1)S(1)} %copy-done.1), kind=kOutput, calls=%fused_computation.68 | convolution fusion | flops 479084544 | bytes 3303424 | tf_op jit(solution)/shard_map/dot_general | solution.py:174
  98.9 0.8 add_convert_fusion
  99.8 0.2 copy.48
  99.9 0.9 slice.194
  (36 shorter events, 0.6 us)
Async XLA Ops:
  0.0 6.0 %copy-start.3 = (f32[648]{0:T(1024)S(1)}, f32[648]{0:T(1024)}, u32[]{:S(2)}) copy-start(f32[648]{0:T(1024)} %param.12) | copy-start | bytes 7780
  0.0 10.9 %copy-start.7 = (bf16[1296,361]{1,0:T(8,128)(2,1)S(1)}, bf16[1296,361]{1,0:T(8,128)(2,1)}, u32[]{:S(2)}) copy-start(bf16[1296,361]{1,0:T(8,128)(2,1)} %param.10) | copy-start | bytes 2807140
  2.7 8.3 %collective-permute-start = (bf16[361,8,32]{0,2,1:T(8,128)(2,1)S(1)}, bf16[361,8,32]{0,2,1:T(8,128)(2,1)S(1)}, u32[]{:S(2)}, u32[]{:S(2)}) collective-permute-start(bf16[361,8,32]{0,2,1:T(8,128)(2,1)S(1)} %pad_maximum_fusion.1), channel_id=1, source_target_pairs={{0,1},{1,0},{2,3},{3,2},{4,5},{5,4},{6,7},{7,6},{8,9},{9,8},{10,11... | collective-permute-start | bytes 554504 | tf_op jit(solution)/shard_map/ppermute | solution.py:18
  20.0 27.7 %all-to-all-start = ((f32[64,8,512]{2,1,0:T(8,128)}), f32[64,8,512]{2,1,0:T(8,128)S(1)}, u32[]{:S(2)}, u32[]{:S(2)}) async-start(f32[64,8,512]{2,1,0:T(8,128)} %reshape.173), calls=%async_computation | async-start | bytes 2097152 | tf_op jit(solution)/shard_map/all_to_all | solution.py:63
  51.0 6.9 %copy-start.6 = (s32[6,2]{0,1:T(2,128)S(1)}, s32[6,2]{0,1:T(2,128)}, u32[]{:S(2)}) copy-start(s32[6,2]{0,1:T(2,128)} %param.15) | copy-start | bytes 148
  52.2 7.8 %copy-start.4 = (f32[648]{0:T(1024)S(1)}, f32[648]{0:T(1024)}, u32[]{:S(2)}) copy-start(f32[648]{0:T(1024)} %param.14) | copy-start | bytes 7780
  52.2 7.8 %copy-start.5 = (f32[648]{0:T(1024)S(1)}, f32[648]{0:T(1024)}, u32[]{:S(2)}) copy-start(f32[648]{0:T(1024)} %param.13) | copy-start | bytes 7780
  52.2 22.9 %all-to-all-start.1 = ((f32[64,8,512]{2,1,0:T(8,128)}), f32[64,8,512]{2,1,0:T(8,128)S(1)}, u32[]{:S(2)}, u32[]{:S(2)}) async-start(f32[64,8,512]{2,1,0:T(8,128)} %maximum_divide_fusion), calls=%async_computation.1 | async-start | bytes 2097152 | tf_op jit(solution)/shard_map/all_to_all | solution.py:69
  59.9 20.9 %collective-permute-start.1 = (bf16[2,160,648]{2,1,0:T(8,128)(2,1)S(1)}, bf16[2,160,648]{2,1,0:T(8,128)(2,1)S(1)}, u32[]{:S(2)}, u32[]{:S(2)}) collective-permute-start(bf16[2,160,648]{2,1,0:T(8,128)(2,1)S(1)} %fusion.43), channel_id=1, source_target_pairs={{0,2},{2,4},{4,6},{6,8},{8,10},{10,12},{12,14},{14,16},{16,18},{18... | collective-permute-start | bytes 1244168 | tf_op jit(solution)/shard_map/ppermute | solution.py:18
  80.8 1.4 %copy-start.2 = (bf16[2,160,648]{2,1,0:T(8,128)(2,1)}, bf16[2,160,648]{2,1,0:T(8,128)(2,1)S(1)}, u32[]{:S(2)}) copy-start(bf16[2,160,648]{2,1,0:T(8,128)(2,1)S(1)} %collective-permute-done.1) | copy-start | bytes 1244164
  82.2 14.4 %copy-start.1 = (bf16[361,1296]{0,1:T(8,128)(2,1)S(1)}, bf16[361,1296]{0,1:T(8,128)(2,1)}, u32[]{:S(2)}) copy-start(bf16[361,1296]{0,1:T(8,128)(2,1)} %param.11) | copy-start | bytes 2807140
  96.6 2.3 %copy-start = (bf16[8,16,8,648]{3,2,1,0:T(8,128)(2,1)S(1)}, bf16[8,16,8,648]{3,2,1,0:T(8,128)(2,1)}, u32[]{:S(2)}) copy-start(bf16[8,16,8,648]{3,2,1,0:T(8,128)(2,1)} %get-tuple-element.11) | copy-start | bytes 3981316
